TPU v7x, 32 devices: a whole 2x2x4 slice. The times are simulated.
32 devices in a mesh: groups: 2 (over x), row: 8 (over z, y), col: 2 (over core).
Axes of the slice: x: 2, y: 2, z: 4, core: 2. Of those that a mesh axis runs over, the one named last changes fastest.
Arguments:
- sky_map: bfloat16 [512, 1024, 128], P(('groups', 'row'), 'col'), parts along dimension 0, may hold values from -6 to 6
- expand_weight: bfloat16 [128, 256], replicated, may hold values from -0.5 to 0.5
- expand_bias: float32 [256], replicated, may hold values from -3 to 3
- depth_weight: float32 [3, 3, 256], replicated, may hold values from -2 to 2
- depth_bias: float32 [256], replicated, may hold values from -3 to 3
- project_weight: bfloat16 [256, 128], replicated, may hold values from -0.375 to 0.375
- project_bias: float32 [128], replicated, may hold values from -3 to 3
- norm_gain: float32 [128], replicated, may hold values from 0.1 to 1.9
- norm_bias: float32 [128], replicated, may hold values from -3 to 3
- mixing_weight: bfloat16 [128, 384], replicated
- position_bias: float32 [4, 225], replicated, may hold values from -4 to 4
- output_weight: bfloat16 [128, 128], replicated, may hold values from -0.5 to 0.5
Outputs:
- block_out: bfloat16 [512, 1024, 128], P(('groups', 'row'), 'col'), parts along dimension 0
There are 2 independent parts, one for each index of `groups`. A program takes and returns all parts, laid end to end along the dimension named above; an argument that names none is the same for every part. Nothing has to cross between parts.
All inputs are finite; a program needn't handle non-finite values.
Results may differ from a plain program's by a relative error of at most 0.023.
Values may be sent and summed in bfloat16 or wider, within the bound.
No kernel may reach another device: no remote copies, remote signals or barrier semaphores. Data moves between devices by JAX's collectives and lax.ppermute only.
A program may use at most 128 MiB of HBM per device.

v0:
```python
import jax
import jax.numpy as jnp
from jax import lax
from jax.sharding import PartitionSpec as P

HEADS = 4
G = 8


def with_halo(array, sides, width):
    for axis, dim in sides:
        size, length = (lax.axis_size(axis), array.shape[dim])
        up = [(i, (i + 1) % size) for i in range(size - 1)]
        down = [(j, i) for i, j in up]
        last = lax.slice_in_dim(array, length - width, length, axis=dim)
        initial = lax.slice_in_dim(array, 0, width, axis=dim)
        before = lax.ppermute(last, axis, up)
        after = lax.ppermute(initial, axis, down)
        array = jnp.concatenate([before, array, after], axis=dim)
    return array


def gelu_tanh(values):
    return jax.nn.gelu(values, approximate=True)


def expand_layer(features, expand_weight, expand_bias):
    return gelu_tanh(
        jnp.dot(features, expand_weight, preferred_element_type=jnp.float32) + expand_bias
    ).astype(jnp.bfloat16)


def depthwise(padded, depth_weight, depth_bias, row_count, col_count):
    accumulated = jnp.zeros((row_count, col_count, padded.shape[2]), jnp.float32) + depth_bias
    for row_shift in range(3):
        for col_shift in range(3):
            accumulated = (
                accumulated
                + padded[row_shift : row_shift + row_count, col_shift : col_shift + col_count]
                * depth_weight[row_shift, col_shift]
            )
    return gelu_tanh(accumulated).astype(jnp.bfloat16)


def layer_norm(features, norm_gain, norm_bias):
    values = features.astype(jnp.float32)
    mean_value = jnp.mean(values, axis=-1, keepdims=True)
    variance = jnp.mean((values - mean_value) ** 2, axis=-1, keepdims=True)
    return ((values - mean_value) * lax.rsqrt(variance + 1e-05) * norm_gain + norm_bias).astype(
        jnp.bfloat16
    )


def grid_bias(position_bias, grid_side):
    position = jnp.arange(grid_side * grid_side, dtype=jnp.int32)
    row_of = position // grid_side
    col_of = position % grid_side
    offset_index = (row_of[:, None] - row_of[None, :] + grid_side - 1) * (2 * grid_side - 1) + (
        col_of[:, None] - col_of[None, :] + grid_side - 1
    )
    entries = jnp.arange((2 * grid_side - 1) ** 2, dtype=jnp.int32)
    one_hot = (offset_index[:, :, None] == entries[None, None, :]).astype(jnp.float32)
    return jnp.einsum("qkt,ht->hqk", one_hot, position_bias, precision=lax.Precision.HIGHEST)


def attend(projected, table, head_count):
    group_count, tokens, triple = projected.shape
    channels = triple // 3
    head_size = channels // head_count
    split_parts = projected.reshape(group_count, tokens, 3, head_count, head_size)
    query_part = split_parts[:, :, 0]
    key_part = split_parts[:, :, 1]
    value_part = split_parts[:, :, 2]
    scores = (
        jnp.einsum("nqhd,nkhd->nhqk", query_part, key_part, preferred_element_type=jnp.float32)
        * head_size ** (-0.5)
        + table[None]
    )
    probs = jax.nn.softmax(scores, axis=-1).astype(jnp.bfloat16)
    attended = jnp.einsum("nhqk,nkhd->nqhd", probs, value_part, preferred_element_type=jnp.float32)
    return attended.astype(jnp.bfloat16).reshape(group_count, tokens, channels)


def body(
    sky_map,
    expand_weight,
    expand_bias,
    depth_weight,
    depth_bias,
    project_weight,
    project_bias,
    norm_gain,
    norm_bias,
    mixing_weight,
    position_bias,
    output_weight,
):
    row_count, col_count, channels = sky_map.shape
    expanded = expand_layer(sky_map, expand_weight, expand_bias)
    padded = with_halo(expanded, (("row", 0), ("col", 1)), 1)
    hidden = depthwise(padded, depth_weight, depth_bias, row_count, col_count)
    after_conv = (
        sky_map.astype(jnp.float32)
        + jnp.dot(hidden, project_weight, preferred_element_type=jnp.float32)
        + project_bias
    ).astype(jnp.bfloat16)
    normed = layer_norm(after_conv, norm_gain, norm_bias)
    across = G // lax.axis_size("col")
    stride = col_count // across
    local_proj = jnp.dot(normed, mixing_weight, preferred_element_type=jnp.float32).astype(
        jnp.bfloat16
    )
    projected = lax.all_to_all(
        lax.all_to_all(
            local_proj.reshape(row_count, across, stride, 3 * channels),
            "row",
            split_axis=0,
            concat_axis=0,
            tiled=True,
        ),
        "col",
        split_axis=2,
        concat_axis=1,
        tiled=True,
    )
    inner_rows = row_count // G
    inner_cols = projected.shape[2]
    grouped = (
        projected.reshape(G, inner_rows, G, inner_cols, 3 * channels)
        .transpose(1, 3, 0, 2, 4)
        .reshape(inner_rows, inner_cols, G * G, 3 * channels)
    )
    table = grid_bias(position_bias, G)

    def one_block(block):
        return attend(block, table, HEADS)

    heads_out = lax.map(one_block, grouped)
    returned = (
        heads_out.reshape(inner_rows, inner_cols, G, G, channels)
        .transpose(2, 0, 3, 1, 4)
        .reshape(row_count, G, inner_cols, channels)
    )
    returned = lax.all_to_all(
        lax.all_to_all(returned, "row", split_axis=0, concat_axis=0, tiled=True),
        "col",
        split_axis=1,
        concat_axis=2,
        tiled=True,
    )
    returned = returned.reshape(row_count, col_count, channels)
    return (
        after_conv.astype(jnp.float32)
        + jnp.dot(returned, output_weight, preferred_element_type=jnp.float32)
    ).astype(jnp.bfloat16)


def solution(mesh):
    placed = (
        P(("groups", "row"), "col", None),
        P(),
        P(),
        P(),
        P(),
        P(),
        P(),
        P(),
        P(),
        P(),
        P(),
        P(),
    )
    return jax.shard_map(
        body,
        mesh=mesh,
        in_specs=placed,
        out_specs=P(("groups", "row"), "col", None),
        check_vma=False,
    )
```

profile of v0, /device:TPU:13, one launch (start us, length us, event | category | flops | bytes accessed | tf_op | source)
XLA Modules:
  0.0 630.7 jit_solution(5646105298377893019)
XLA Ops:
  0.0 7.7 %fusion.15 = bf16[32,512,256]{2,1,0:T(8,128)(2,1)S(1)} fusion(bf16[32,512,128]{2,1,0:T(8,128)(2,1)} %param.14, f32[256]{0:T(256)} %param.16, bf16[128,256]{1,0:T(8,128)(2,1)} %param.15), kind=kOutput, calls=%fused_computation.25 | convolution fusion | flops 1115684864 | bytes 12649472 | tf_op jit(solution)/shard_map/dot_general | solution.py:29
  7.7 3.1 collective-permute-start
  13.0 9.4 %collective-permute-done = bf16[1,512,256]{2,1,0:T(8,128)(2,1)S(1)} collective-permute-done((bf16[1,512,256]{2,1,0:T(8,128)(2,1)S(1)}, bf16[1,512,256]{2,1,0:T(8,128)(2,1)S(1)}, u32[]{:S(2)}, u32[]{:S(2)}) %collective-permute-start) | collective-permute-done | bytes 262176 | tf_op jit(solution)/shard_map/ppermute | solution.py:17
  23.8 3.6 collective-permute-start.3
  27.5 6.4 %copy.73 = bf16[32,512,128]{1,2,0:T(8,128)(2,1)} copy(bf16[32,512,128]{2,1,0:T(8,128)(2,1)} %param.14) | data formatting | bytes 8388608 | tf_op args[0]
  33.9 18.2 %maximum_maximum_fusion = (bf16[34,513,256]{2,1,0:T(8,128)(2,1)}, bf16[34,513,256]{2,1,0:T(8,128)(2,1)}) fusion(bf16[1,512,256]{2,1,0:T(8,128)(2,1)S(1)} %collective-permute-done.1, bf16[32,512,256]{2,1,0:T(8,128)(2,1)} %copy-done.4, bf16[1,512,256]{2,1,0:T(8,128)(2,1)S(1)} %collective-permute-done, bf16[34,1,256]{2,1,0:T(2,128)(2,1)S(1)} %collective-permute-done.2, ...), kind=kLoop, calls=%fused_computation.40 | loop fusion | flops 71442432 | bytes 26808320 | tf_op jit(solution)/shard_map/concatenate | solution.py:19
  52.1 36.1 %convert_reduce_fusion = (f32[32,512]{1,0:T(8,128)S(1)}, bf16[32,512,128]{1,2,0:T(8,128)(2,1)S(1)}) fusion(f32[128]{0:T(128)S(1)} %copy-done.12, bf16[256,128]{1,0:T(8,128)(2,1)S(1)} %copy-done.9, bf16[32,512,256]{2,1,0:T(8,128)(2,1)} %copy-done.4, bf16[34,513,256]{2,1,0:T(8,128)(2,1)} %get-tuple-element.59, ...), kind=kOutput, calls=%fused_computation.37 | convolution fusion | flops 1245691904 | bytes 67774976 | tf_op jit(solution)/shard_map/dot_general | solution.py:104
  89.7 7.1 %convolution_convert_fusion = bf16[32,512,384]{2,1,0:T(8,128)(2,1)} fusion(bf16[32,512,128]{1,2,0:T(8,128)(2,1)S(1)} %get-tuple-element.74, f32[128]{0:T(128)S(1)} %copy-done.7, f32[128]{0:T(128)S(1)} %copy-done.8, f32[32,512]{1,0:T(8,128)S(1)} %add_rsqrt_fusion, f32[32,512]{1,0:T(8,128)S(1)} %broadcast_multiply_fusion, bf16[128,384]{1,0:T(8,128)(2,1)S(1)} %copy-done), kind=kOutput, calls=%fused_computation.51 | convolution fusion | flops 1629487104 | bytes 17007616 | tf_op jit(solution)/shard_map/dot_general | solution.py:110
  96.9 15.6 %copy.76 = bf16[32,4,128,384]{3,1,2,0:T(4,128)(2,1)} copy(bf16[32,4,128,384]{3,2,1,0:T(8,128)(2,1)} %bitcast.83) | data formatting | bytes 25165824 | tf_op jit(solution)/shard_map/reshape | solution.py:115
  112.4 6.4 %all-to-all-start = ((bf16[32,4,128,384]{3,1,2,0:T(4,128)(2,1)}), bf16[32,4,128,384]{3,1,2,0:T(4,128)(2,1)}, u32[]{:S(2)}, u32[]{:S(2)}) async-start(bf16[32,4,128,384]{3,1,2,0:T(4,128)(2,1)} %copy.76), calls=%async_computation | async-start | bytes 25165824 | tf_op jit(solution)/shard_map/all_to_all | solution.py:114
  121.8 267.5 %all-to-all-done = bf16[32,4,128,384]{3,1,2,0:T(4,128)(2,1)} async-done(((bf16[32,4,128,384]{3,1,2,0:T(4,128)(2,1)}), bf16[32,4,128,384]{3,1,2,0:T(4,128)(2,1)}, u32[]{:S(2)}, u32[]{:S(2)}) %all-to-all-start) | async-done | bytes 12582944 | tf_op jit(solution)/shard_map/all_to_all | solution.py:114
  389.3 8.7 %copy.77 = bf16[32,4,128,384]{3,1,0,2:T(4,128)(2,1)S(1)} copy(bf16[32,4,128,384]{3,1,2,0:T(4,128)(2,1)} %all-to-all-done) | data formatting | bytes 25165824 | tf_op jit(solution)/shard_map/all_to_all | solution.py:114
  398.0 13.9 %all_to_all.40 = bf16[32,4,128,384]{3,1,0,2:T(4,128)(2,1)S(1)} all-to-all(bf16[32,4,128,384]{3,1,0,2:T(4,128)(2,1)S(1)} %copy.77), channel_id=1, replica_groups=mesh['groups'=2,'row'=8,'col'=2] {'col'}, dimensions={2} | all-to-all | bytes 25165824 | tf_op jit(solution)/shard_map/all_to_all | solution.py:113
  411.8 8.9 %copy.78 = bf16[32,4,128,384]{3,2,1,0:T(8,128)(2,1)S(1)} copy(bf16[32,4,128,384]{3,1,0,2:T(4,128)(2,1)S(1)} %all_to_all.40) | data formatting | bytes 25165824 | tf_op jit(solution)/shard_map/all_to_all | solution.py:113
  420.7 3.2 copy.79
  423.9 9.3 %copy.103 = bf16[4,64,8,8,384]{4,3,2,1,0:T(8,128)(2,1)} copy(bf16[4,64,8,8,384]{4,1,3,0,2:T(8,128)(2,1)S(1)} %bitcast.85) | data formatting | bytes 25165824 | tf_op jit(solution)/shard_map/transpose | solution.py:130
  433.2 72.4 %while.10 = (s32[]{:T(128)}, bf16[4,64,64,128]{3,2,1,0:T(8,128)(2,1)}, bf16[4,64,64,384]{3,2,1,0:T(8,128)(2,1)}, f32[4,64,64]{1,2,0:T(8,128)S(1)}, s32[]{:T(128)}) while((s32[]{:T(128)}, bf16[4,64,64,128]{3,2,1,0:T(8,128)(2,1)}, bf16[4,64,64,384]{3,2,1,0:T(8,128)(2,1)}, f32[4,64,64]{1,2,0:T(8,128)S(1)}, s32[]{:T(128)}) %tuple.42), condition=%wide.region_5.6_spmd, body=%wide.region_2.5_spmd.sunk | while | flops 143130688 | bytes 41091648 | solution.py:138
  435.4 4.8 copy.106
  440.1 3.5 fusion.61
  446.4 2.8 fusion.63
  453.5 4.8 copy.106
  458.3 3.5 fusion.61
  464.5 2.8 fusion.63
  471.6 4.8 copy.106
  476.3 3.5 fusion.61
  489.7 4.8 copy.106
  494.4 3.5 fusion.61
  505.5 7.0 %copy.84 = bf16[8,4,8,64,128]{4,3,2,1,0:T(8,128)(2,1)S(1)} copy(bf16[8,4,8,64,128]{4,2,0,3,1:T(8,128)(2,1)} %bitcast.89) | data formatting | bytes 8388608 | tf_op jit(solution)/shard_map/transpose | solution.py:141
  512.6 96.6 %all_to_all.41 = bf16[32,8,64,128]{3,2,1,0:T(8,128)(2,1)S(1)} all-to-all(bf16[32,8,64,128]{3,2,1,0:T(8,128)(2,1)S(1)} %bitcast.87), channel_id=1, replica_groups=mesh['groups'=2,'row'=8,'col'=2] {'row'}, dimensions={0} | all-to-all | bytes 8388608 | tf_op jit(solution)/shard_map/all_to_all | solution.py:145
  610.6 9.0 %all_to_all.42 = bf16[32,8,64,128]{3,2,0,1:T(8,128)(2,1)S(1)} all-to-all(bf16[32,8,64,128]{3,2,0,1:T(8,128)(2,1)S(1)} %copy.85), channel_id=1, replica_groups=mesh['groups'=2,'row'=8,'col'=2] {'col'}, dimensions={1} | all-to-all | bytes 8388608 | tf_op jit(solution)/shard_map/all_to_all | solution.py:144
  621.0 3.3 fusion.30
  624.2 6.4 %copy.89 = bf16[32,512,128]{2,1,0:T(8,128)(2,1)} copy(bf16[32,512,128]{1,2,0:T(8,128)(2,1)} %fusion.30) | data formatting | bytes 8388608 | tf_op jit(solution)/shard_map/convert_element_type | solution.py:155
  (62 shorter events, 44.2 us)
Async XLA Ops:
  0.0 89.7 %copy-start = (bf16[128,384]{1,0:T(8,128)(2,1)S(1)}, bf16[128,384]{1,0:T(8,128)(2,1)}, u32[]{:S(2)}) copy-start(bf16[128,384]{1,0:T(8,128)(2,1)} %param.23) | copy-start | bytes 294916
  7.7 14.8 %copy-start.4 = (bf16[32,512,256]{2,1,0:T(8,128)(2,1)}, bf16[32,512,256]{2,1,0:T(8,128)(2,1)S(1)}, u32[]{:S(2)}) copy-start(bf16[32,512,256]{2,1,0:T(8,128)(2,1)S(1)} %fusion.15) | copy-start | bytes 25165828
  7.7 19.8 %copy-start.6 = (f32[3,3,256]{2,1,0:T(4,128)S(1)}, f32[3,3,256]{2,1,0:T(4,128)}, u32[]{:S(2)}) copy-start(f32[3,3,256]{2,1,0:T(4,128)} %param.17) | copy-start | bytes 27652
  7.7 14.7 %collective-permute-start = (bf16[1,512,256]{2,1,0:T(8,128)(2,1)S(1)}, bf16[1,512,256]{2,1,0:T(8,128)(2,1)S(1)}, u32[]{:S(2)}, u32[]{:S(2)}) collective-permute-start(bf16[1,512,256]{2,1,0:T(8,128)(2,1)S(1)} %get-tuple-element.62), channel_id=1, source_target_pairs={{0,2},{2,4},{4,6},{6,8},{8,10},{10,12},{12,14},{1,3},{3,5},{5,7},{... | collective-permute-start | bytes 786440 | tf_op jit(solution)/shard_map/ppermute | solution.py:17
  10.9 11.5 %collective-permute-start.1 = (bf16[1,512,256]{2,1,0:T(8,128)(2,1)S(1)}, bf16[1,512,256]{2,1,0:T(8,128)(2,1)S(1)}, u32[]{:S(2)}, u32[]{:S(2)}) collective-permute-start(bf16[1,512,256]{2,1,0:T(8,128)(2,1)S(1)} %get-tuple-element.63), channel_id=1, source_target_pairs={{2,0},{4,2},{6,4},{8,6},{10,8},{12,10},{14,12},{3,1},{5,3},{7,5},{... | collective-permute-start | bytes 786440 | tf_op jit(solution)/shard_map/ppermute | solution.py:18
  22.5 11.4 %collective-permute-start.2 = (bf16[34,1,256]{2,1,0:T(2,128)(2,1)S(1)}, bf16[34,1,256]{2,1,0:T(2,128)(2,1)S(1)}, u32[]{:S(2)}, u32[]{:S(2)}) collective-permute-start(bf16[34,1,256]{2,1,0:T(2,128)(2,1)S(1)} %get-tuple-element.60), channel_id=1, source_target_pairs={{0,1},{2,3},{4,5},{6,7},{8,9},{10,11},{12,13},{14,15},{16,17},{18,... | collective-permute-start | bytes 52232 | tf_op jit(solution)/shard_map/ppermute | solution.py:17
  23.8 10.1 %collective-permute-start.3 = (bf16[34,1,256]{2,1,0:T(2,128)(2,1)S(1)}, bf16[34,1,256]{2,1,0:T(2,128)(2,1)S(1)}, u32[]{:S(2)}, u32[]{:S(2)}) collective-permute-start(bf16[34,1,256]{2,1,0:T(2,128)(2,1)S(1)} %get-tuple-element.61), channel_id=1, source_target_pairs={{1,0},{3,2},{5,4},{7,6},{9,8},{11,10},{13,12},{15,14},{17,16},{19,... | collective-permute-start | bytes 52232 | tf_op jit(solution)/shard_map/ppermute | solution.py:18
  33.9 18.2 %copy-start.9 = (bf16[256,128]{1,0:T(8,128)(2,1)S(1)}, bf16[256,128]{1,0:T(8,128)(2,1)}, u32[]{:S(2)}) copy-start(bf16[256,128]{1,0:T(8,128)(2,1)} %param.19) | copy-start | bytes 196612
  33.9 18.2 %copy-start.11 = (f32[256]{0:T(256)S(1)}, f32[256]{0:T(256)}, u32[]{:S(2)}) copy-start(f32[256]{0:T(256)} %param.18) | copy-start | bytes 3076
  33.9 18.2 %copy-start.12 = (f32[128]{0:T(128)S(1)}, f32[128]{0:T(128)}, u32[]{:S(2)}) copy-start(f32[128]{0:T(128)} %param.20) | copy-start | bytes 1540
  52.1 37.6 %copy-start.7 = (f32[128]{0:T(128)S(1)}, f32[128]{0:T(128)}, u32[]{:S(2)}) copy-start(f32[128]{0:T(128)} %param.22) | copy-start | bytes 1540
  52.1 37.6 %copy-start.8 = (f32[128]{0:T(128)S(1)}, f32[128]{0:T(128)}, u32[]{:S(2)}) copy-start(f32[128]{0:T(128)} %param.21) | copy-start | bytes 1540
  88.3 8.6 %copy-start.2 = (bf16[32,512,128]{1,2,0:T(8,128)(2,1)}, bf16[32,512,128]{1,2,0:T(8,128)(2,1)S(1)}, u32[]{:S(2)}) copy-start(bf16[32,512,128]{1,2,0:T(8,128)(2,1)S(1)} %get-tuple-element.74) | copy-start | bytes 12582916
  112.4 6.5 %copy-start.10 = (f32[4,225]{1,0:T(4,128)S(1)}, f32[4,225]{1,0:T(4,128)}, u32[]{:S(2)}) copy-start(f32[4,225]{1,0:T(4,128)} %param.24) | copy-start | bytes 10804
  112.4 276.9 %all-to-all-start = ((bf16[32,4,128,384]{3,1,2,0:T(4,128)(2,1)}), bf16[32,4,128,384]{3,1,2,0:T(4,128)(2,1)}, u32[]{:S(2)}, u32[]{:S(2)}) async-start(bf16[32,4,128,384]{3,1,2,0:T(4,128)(2,1)} %copy.76), calls=%async_computation | async-start | bytes 25165824 | tf_op jit(solution)/shard_map/all_to_all | solution.py:114
  610.6 10.4 %copy-start.3 = (bf16[32,512,128]{1,2,0:T(8,128)(2,1)S(1)}, bf16[32,512,128]{1,2,0:T(8,128)(2,1)}, u32[]{:S(2)}) copy-start(bf16[32,512,128]{1,2,0:T(8,128)(2,1)} %copy-done.2) | copy-start | bytes 12582916
  610.6 10.4 %copy-start.5 = (bf16[128,128]{1,0:T(8,128)(2,1)S(1)}, bf16[128,128]{1,0:T(8,128)(2,1)}, u32[]{:S(2)}) copy-start(bf16[128,128]{1,0:T(8,128)(2,1)} %param.25) | copy-start | bytes 98308
  621.0 9.7 %copy-start.1 = (bf16[128,384]{1,0:T(8,128)(2,1)S(1)}, bf16[128,384]{1,0:T(8,128)(2,1)}, u32[]{:S(2)}) copy-start(bf16[128,384]{1,0:T(8,128)(2,1)} %param.23) | copy-start | bytes 294916
where the time goes:
time: 635 us; the launch traced here: 631 us
  waiting for transfers between devices  277 us (44%)
  blocking collectives  119 us (19%)
  local copies, waits for them, and re-layouts  104 us (16%)
  matrix products  82.4 us (13%)
  other arithmetic  30.6 us (5%)
  starting transfers between devices  16.6 us (3%)
    all_to_all x1, waiting for transfers between devices, body(): lax.all_to_all(local_proj.reshape(row_count, across, stride, 3 * channels...  267 us
    all_to_all x1, blocking collectives, body(): lax.all_to_all(returned, 'row', split_axis=0, concat_axis=0, tiled=True)  96.6 us
    dot_general x1, matrix products, body(): jnp.dot(hidden, project_weight, preferred_element_type=jnp.float32)  36.1 us
    dynamic_slice x8, local copies, waits for them, and re-layouts, body(): heads_out = lax.map(one_block, grouped)  27.9 us
    concatenate x1, other arithmetic, with_halo(): array = jnp.concatenate([before, array, after], axis=dim)  18.2 us
    reshape x1, local copies, waits for them, and re-layouts, body(): local_proj.reshape(row_count, across, stride, 3 * channels)  15.6 us
    dot_general x4, matrix products, attend(): jnp.einsum('nqhd,nkhd->nhqk', query_part, key_part, preferred_element_typ...  14.2 us
    all_to_all x1, blocking collectives, body(): lax.all_to_all(lax.all_to_all(local_proj.reshape(row_count, across, strid...  13.9 us
  transfers between devices with their start and end apart: 5, of which 2 were waited for; matrix products, arithmetic and copies ran while one was open for 1% of the time, Pallas kernels for 0%

commit v1 on v0

--- a/solution.py
+++ b/solution.py
@@ -58,9 +58,7 @@
     offset_index = (row_of[:, None] - row_of[None, :] + grid_side - 1) * (2 * grid_side - 1) + (
         col_of[:, None] - col_of[None, :] + grid_side - 1
     )
-    entries = jnp.arange((2 * grid_side - 1) ** 2, dtype=jnp.int32)
-    one_hot = (offset_index[:, :, None] == entries[None, None, :]).astype(jnp.float32)
-    return jnp.einsum("qkt,ht->hqk", one_hot, position_bias, precision=lax.Precision.HIGHEST)
+    return jnp.take(position_bias, offset_index, axis=1)
 
 
 def attend(projected, table, head_count):
@@ -107,12 +105,9 @@
     normed = layer_norm(after_conv, norm_gain, norm_bias)
     across = G // lax.axis_size("col")
     stride = col_count // across
-    local_proj = jnp.dot(normed, mixing_weight, preferred_element_type=jnp.float32).astype(
-        jnp.bfloat16
-    )
-    projected = lax.all_to_all(
+    moved = lax.all_to_all(
         lax.all_to_all(
-            local_proj.reshape(row_count, across, stride, 3 * channels),
+            normed.reshape(row_count, across, stride, channels),
             "row",
             split_axis=0,
             concat_axis=0,
@@ -122,6 +117,9 @@
         split_axis=2,
         concat_axis=1,
         tiled=True,
+    )
+    projected = jnp.dot(moved, mixing_weight, preferred_element_type=jnp.float32).astype(
+        jnp.bfloat16
     )
     inner_rows = row_count // G
     inner_cols = projected.shape[2]

time: 635 us -> 421 us (0.66)
  waiting for transfers between devices: 277 us -> 88.2 us
  local copies, waits for them, and re-layouts: 104 us -> 84.4 us
    all_to_all x1, waiting for transfers between devices: 267 us -> 78.2 us  [body(): lax.all_to_all(normed.reshape(row_count, across, stride, channels), 'row'...]
    gather x0 -> x2, local copies, waits for them, and re-layouts: none -> 12 us  [grid_bias(): return jnp.take(position_bias, offset_index, axis=1)]
    all_to_all x3 -> x2, local copies, waits for them, and re-layouts: 20.7 us -> 11.4 us  [the longest x1 6.81 us: body(): lax.all_to_all(lax.all_to_all(normed.reshape(row_count, across, stride, c...]
    transpose x1 -> x0, local copies, waits for them, and re-layouts: 9.25 us -> none  [body(): grouped = projected.reshape(G, inner_rows, G, inner_cols, 3 * channels).t...]
    convert_element_type x1 -> x0, local copies, waits for them, and re-layouts: 6.4 us -> none  [body(): return (after_conv.astype(jnp.float32) + jnp.dot(returned, output_weight,...]
    reshape x1 -> x2, local copies, waits for them, and re-layouts: 15.6 us -> 15.1 us  [the longest x1 9.25 us: body(): projected.reshape(G, inner_rows, G, inner_cols, 3 * channels)]
  transfers between devices with their start and end apart: 5 -> 5, of which waited for: 2 -> 3; matrix products, arithmetic and copies ran while one was open for 1% -> 3% of each run, Pallas kernels for 0% -> 0%
where the time goes in v1:
time: 421 us; the launch traced here: 414 us
  blocking collectives  113 us (27%)
  waiting for transfers between devices  88.2 us (21%)
  local copies, waits for them, and re-layouts  84.4 us (20%)
  matrix products  78.2 us (19%)
  other arithmetic  33.2 us (8%)
  starting transfers between devices  16.4 us (4%)
    all_to_all x1, blocking collectives, body(): lax.all_to_all(returned, 'row', split_axis=0, concat_axis=0, tiled=True)  96.5 us
    all_to_all x1, waiting for transfers between devices, body(): lax.all_to_all(normed.reshape(row_count, across, stride, channels), 'row'...  78.2 us
    dot_general x1, matrix products, body(): jnp.dot(hidden, project_weight, preferred_element_type=jnp.float32)  36.2 us
    dynamic_slice x8, local copies, waits for them, and re-layouts, body(): heads_out = lax.map(one_block, grouped)  27.9 us
    dot_general x4, matrix products, attend(): jnp.einsum('nqhd,nkhd->nhqk', query_part, key_part, preferred_element_typ...  14.2 us
    concatenate x1, other arithmetic, with_halo(): array = jnp.concatenate([before, array, after], axis=dim)  12.1 us
    gather x2, local copies, waits for them, and re-layouts, grid_bias(): return jnp.take(position_bias, offset_index, axis=1)  12 us
    dot_general x4, matrix products, attend(): jnp.einsum('nhqk,nkhd->nqhd', probs, value_part, preferred_element_type=j...  11.3 us
  transfers between devices with their start and end apart: 5, of which 3 were waited for; matrix products, arithmetic and copies ran while one was open for 3% of the time, Pallas kernels for 0%

profile of v1, /device:TPU:13, one launch (start us, length us, event | category | flops | bytes accessed | tf_op | source)
XLA Modules:
  0.0 414.4 jit_solution(1829143538454560903)
XLA Ops:
  0.0 7.7 %fusion.15 = bf16[32,512,256]{2,1,0:T(8,128)(2,1)S(1)} fusion(bf16[32,512,128]{2,1,0:T(8,128)(2,1)} %param.14, f32[256]{0:T(256)} %param.16, bf16[128,256]{1,0:T(8,128)(2,1)} %param.15), kind=kOutput, calls=%fused_computation.26 | convolution fusion | flops 1115684864 | bytes 12649472 | tf_op jit(solution)/shard_map/dot_general | solution.py:29
  7.7 3.1 collective-permute-start
  13.0 9.4 %collective-permute-done = bf16[1,512,256]{2,1,0:T(8,128)(2,1)S(1)} collective-permute-done((bf16[1,512,256]{2,1,0:T(8,128)(2,1)S(1)}, bf16[1,512,256]{2,1,0:T(8,128)(2,1)S(1)}, u32[]{:S(2)}, u32[]{:S(2)}) %collective-permute-start) | collective-permute-done | bytes 262176 | tf_op jit(solution)/shard_map/ppermute | solution.py:17
  23.8 3.6 collective-permute-start.3
  28.1 12.1 %maximum_maximum_fusion = (bf16[34,513,256]{2,1,0:T(8,128)(2,1)}, bf16[34,513,256]{2,1,0:T(8,128)(2,1)}) fusion(bf16[1,512,256]{2,1,0:T(8,128)(2,1)S(1)} %collective-permute-done.1, bf16[32,512,256]{2,1,0:T(8,128)(2,1)S(1)} %fusion.15, bf16[1,512,256]{2,1,0:T(8,128)(2,1)S(1)} %collective-permute-done, bf16[34,1,256]{2,1,0:T(2,128)(2,1)S(1)} %collective-permute-done.2, ...), kind=kLoop, calls=%fused_computation.41 | loop fusion | flops 71442432 | bytes 26808320 | tf_op jit(solution)/shard_map/concatenate | solution.py:19
  40.3 36.2 %convert_reduce_fusion = (f32[32,512]{1,0:T(8,128)S(1)}, bf16[32,512,128]{2,1,0:T(8,128)(2,1)S(1)}) fusion(f32[128]{0:T(128)S(1)} %copy-done.12, bf16[256,128]{1,0:T(8,128)(2,1)S(1)} %copy-done.10, bf16[32,512,256]{2,1,0:T(8,128)(2,1)} %copy-done.4, bf16[34,513,256]{2,1,0:T(8,128)(2,1)} %get-tuple-element.51, ...), kind=kOutput, calls=%fused_computation.38 | convolution fusion | flops 1245691904 | bytes 67774976 | tf_op jit(solution)/shard_map/dot_general | solution.py:102
  76.5 4.8 %fusion.26 = f32[32,512]{1,0:T(8,128)S(1)} fusion(bf16[32,512,128]{2,1,0:T(8,128)(2,1)S(1)} %get-tuple-element.66, f32[32,512]{1,0:T(8,128)S(1)} %broadcast_multiply_fusion), kind=kLoop, calls=%fused_computation.43 | loop fusion | flops 8372224 | bytes 4325376 | tf_op jit(solution)/shard_map/reduce_sum | solution.py:48
  81.3 5.2 %fusion.29 = bf16[32,512,128]{2,1,0:T(8,128)(2,1)S(1)} fusion(bf16[32,512,128]{2,1,0:T(8,128)(2,1)S(1)} %get-tuple-element.66, f32[128]{0:T(128)S(1)} %copy-done.8, f32[128]{0:T(128)S(1)} %copy-done.9, f32[32,512]{1,0:T(8,128)S(1)} %add_rsqrt_fusion, f32[32,512]{1,0:T(8,128)S(1)} %broadcast_multiply_fusion), kind=kLoop, calls=%fused_computation.46 | loop fusion | flops 12582912 | bytes 8520704 | tf_op jit(solution)/shard_map/convert_element_type | solution.py:49
  86.5 5.9 %copy.60 = bf16[32,4,128,128]{3,1,2,0:T(4,128)(2,1)} copy(bf16[32,4,128,128]{3,2,1,0:T(8,128)(2,1)S(1)} %bitcast.89) | data formatting | bytes 8388608 | tf_op jit(solution)/shard_map/reshape | solution.py:110
  92.4 6.2 %all-to-all-start = ((bf16[32,4,128,128]{3,1,2,0:T(4,128)(2,1)}), bf16[32,4,128,128]{3,1,2,0:T(4,128)(2,1)}, u32[]{:S(2)}, u32[]{:S(2)}) async-start(bf16[32,4,128,128]{3,1,2,0:T(4,128)(2,1)} %copy.60), calls=%async_computation | async-start | bytes 8388608 | tf_op jit(solution)/shard_map/all_to_all | solution.py:109
  99.0 10.8 %gather_fusion = f32[4096,4]{1,0:T(8,128)S(1)} fusion(f32[4,225]{0,1:T(8,128)S(1)} %copy.64, s32[4096]{0:T(1024)S(1)} %broadcast_clamp_fusion), kind=kCustom, calls=%fused_computation | custom fusion | bytes 147456 | tf_op jit(solution)/shard_map/jit(_take)/gather | solution.py:61
  111.1 78.2 %all-to-all-done = bf16[32,4,128,128]{3,1,2,0:T(4,128)(2,1)} async-done(((bf16[32,4,128,128]{3,1,2,0:T(4,128)(2,1)}), bf16[32,4,128,128]{3,1,2,0:T(4,128)(2,1)}, u32[]{:S(2)}, u32[]{:S(2)}) %all-to-all-start) | async-done | bytes 4194336 | tf_op jit(solution)/shard_map/all_to_all | solution.py:109
  189.3 4.5 %copy.61 = bf16[32,4,128,128]{3,1,0,2:T(4,128)(2,1)S(1)} copy(bf16[32,4,128,128]{3,1,2,0:T(4,128)(2,1)} %all-to-all-done) | data formatting | bytes 8388608 | tf_op jit(solution)/shard_map/all_to_all | solution.py:109
  193.8 7.6 %all_to_all.43 = bf16[32,4,128,128]{3,1,0,2:T(4,128)(2,1)S(1)} all-to-all(bf16[32,4,128,128]{3,1,0,2:T(4,128)(2,1)S(1)} %copy.61), channel_id=1, replica_groups=mesh['groups'=2,'row'=8,'col'=2] {'col'}, dimensions={2} | all-to-all | bytes 8388608 | tf_op jit(solution)/shard_map/all_to_all | solution.py:108
  201.5 6.8 %copy.62 = bf16[32,4,2,64,128]{4,3,1,2,0:T(8,128)(2,1)} copy(bf16[32,4,2,64,128]{4,1,0,3,2:T(4,128)(2,1)S(1)} %bitcast.90) | data formatting | bytes 8388608 | tf_op jit(solution)/shard_map/all_to_all | solution.py:108
  208.3 5.6 %convolution_convert_fusion = bf16[32,8,64,384]{3,2,1,0:T(8,128)(2,1)S(1)} fusion(bf16[32,8,64,128]{3,2,1,0:T(8,128)(2,1)} %bitcast.93, bf16[128,384]{1,0:T(8,128)(2,1)S(1)} %copy-done), kind=kOutput, calls=%fused_computation.52 | convolution fusion | flops 1616904192 | bytes 16875520 | tf_op jit(solution)/shard_map/dot_general | solution.py:121
  213.9 9.3 %copy.82 = bf16[8,4,8,64,384]{4,2,0,3,1:T(8,128)(2,1)} copy(bf16[8,4,8,64,384]{4,3,2,1,0:T(8,128)(2,1)S(1)} %bitcast.87) | data formatting | bytes 25165824 | tf_op jit(solution)/shard_map/reshape | solution.py:127
  223.1 72.5 %while.10 = (s32[]{:T(128)}, bf16[4,64,64,128]{3,2,1,0:T(8,128)(2,1)}, bf16[4,64,64,384]{3,2,1,0:T(8,128)(2,1)}, f32[4,64,64]{1,2,0:T(8,128)S(1)}, s32[]{:T(128)}) while((s32[]{:T(128)}, bf16[4,64,64,128]{3,2,1,0:T(8,128)(2,1)}, bf16[4,64,64,384]{3,2,1,0:T(8,128)(2,1)}, f32[4,64,64]{1,2,0:T(8,128)S(1)}, s32[]{:T(128)}) %tuple.40), condition=%wide.region_5.6_spmd, body=%wide.region_2.5_spmd.sunk | while | flops 143130688 | bytes 41091648 | solution.py:136
  225.5 4.8 %copy.85 = bf16[1,64,64,384]{2,3,1,0:T(8,128)(2,1)} copy(bf16[1,64,64,384]{3,2,1,0:T(8,128)(2,1)S(1)} %constant_dynamic-slice_fusion.2) | data formatting | bytes 6291456 | tf_op jit(solution)/shard_map/while/body/jit(dynamic_index_in_dim)/dynamic_slice | solution.py:136
  230.3 3.5 fusion.53
  236.5 2.8 fusion.55
  243.6 4.8 %copy.85 = bf16[1,64,64,384]{2,3,1,0:T(8,128)(2,1)} copy(bf16[1,64,64,384]{3,2,1,0:T(8,128)(2,1)S(1)} %constant_dynamic-slice_fusion.2) | data formatting | bytes 6291456 | tf_op jit(solution)/shard_map/while/body/jit(dynamic_index_in_dim)/dynamic_slice | solution.py:136
  248.3 3.5 fusion.53
  254.6 2.8 fusion.55
  261.7 4.8 %copy.85 = bf16[1,64,64,384]{2,3,1,0:T(8,128)(2,1)} copy(bf16[1,64,64,384]{3,2,1,0:T(8,128)(2,1)S(1)} %constant_dynamic-slice_fusion.2) | data formatting | bytes 6291456 | tf_op jit(solution)/shard_map/while/body/jit(dynamic_index_in_dim)/dynamic_slice | solution.py:136
  266.4 3.5 fusion.53
  279.7 4.8 %copy.85 = bf16[1,64,64,384]{2,3,1,0:T(8,128)(2,1)} copy(bf16[1,64,64,384]{3,2,1,0:T(8,128)(2,1)S(1)} %constant_dynamic-slice_fusion.2) | data formatting | bytes 6291456 | tf_op jit(solution)/shard_map/while/body/jit(dynamic_index_in_dim)/dynamic_slice | solution.py:136
  284.5 3.5 fusion.53
  295.6 7.0 %copy.68 = bf16[8,4,8,64,128]{4,3,2,1,0:T(8,128)(2,1)S(1)} copy(bf16[8,4,8,64,128]{4,2,0,3,1:T(8,128)(2,1)} %bitcast.94) | data formatting | bytes 8388608 | tf_op jit(solution)/shard_map/transpose | solution.py:139
  302.7 96.5 %all_to_all.44 = bf16[32,8,64,128]{3,2,1,0:T(8,128)(2,1)S(1)} all-to-all(bf16[32,8,64,128]{3,2,1,0:T(8,128)(2,1)S(1)} %bitcast.91), channel_id=1, replica_groups=mesh['groups'=2,'row'=8,'col'=2] {'row'}, dimensions={0} | all-to-all | bytes 8388608 | tf_op jit(solution)/shard_map/all_to_all | solution.py:143
  400.5 9.0 %all_to_all.45 = bf16[32,8,64,128]{3,2,0,1:T(8,128)(2,1)S(1)} all-to-all(bf16[32,8,64,128]{3,2,0,1:T(8,128)(2,1)S(1)} %copy.69), channel_id=1, replica_groups=mesh['groups'=2,'row'=8,'col'=2] {'col'}, dimensions={1} | all-to-all | bytes 8388608 | tf_op jit(solution)/shard_map/all_to_all | solution.py:142
  410.9 3.3 fusion.30
  (65 shorter events, 41.9 us)
Async XLA Ops:
  0.0 208.3 %copy-start = (bf16[128,384]{1,0:T(8,128)(2,1)S(1)}, bf16[128,384]{1,0:T(8,128)(2,1)}, u32[]{:S(2)}) copy-start(bf16[128,384]{1,0:T(8,128)(2,1)} %param.23) | copy-start | bytes 294916
  7.7 32.5 %copy-start.4 = (bf16[32,512,256]{2,1,0:T(8,128)(2,1)}, bf16[32,512,256]{2,1,0:T(8,128)(2,1)S(1)}, u32[]{:S(2)}) copy-start(bf16[32,512,256]{2,1,0:T(8,128)(2,1)S(1)} %fusion.15) | copy-start | bytes 25165828
  7.7 19.7 %copy-start.6 = (f32[3,3,256]{2,1,0:T(4,128)S(1)}, f32[3,3,256]{2,1,0:T(4,128)}, u32[]{:S(2)}) copy-start(f32[3,3,256]{2,1,0:T(4,128)} %param.17) | copy-start | bytes 27652
  7.7 14.7 %collective-permute-start = (bf16[1,512,256]{2,1,0:T(8,128)(2,1)S(1)}, bf16[1,512,256]{2,1,0:T(8,128)(2,1)S(1)}, u32[]{:S(2)}, u32[]{:S(2)}) collective-permute-start(bf16[1,512,256]{2,1,0:T(8,128)(2,1)S(1)} %get-tuple-element.54), channel_id=1, source_target_pairs={{0,2},{2,4},{4,6},{6,8},{8,10},{10,12},{12,14},{1,3},{3,5},{5,7},{... | collective-permute-start | bytes 786440 | tf_op jit(solution)/shard_map/ppermute | solution.py:17
  10.9 11.5 %collective-permute-start.1 = (bf16[1,512,256]{2,1,0:T(8,128)(2,1)S(1)}, bf16[1,512,256]{2,1,0:T(8,128)(2,1)S(1)}, u32[]{:S(2)}, u32[]{:S(2)}) collective-permute-start(bf16[1,512,256]{2,1,0:T(8,128)(2,1)S(1)} %get-tuple-element.55), channel_id=1, source_target_pairs={{2,0},{4,2},{6,4},{8,6},{10,8},{12,10},{14,12},{3,1},{5,3},{7,5},{... | collective-permute-start | bytes 786440 | tf_op jit(solution)/shard_map/ppermute | solution.py:18
  22.5 5.0 %collective-permute-start.2 = (bf16[34,1,256]{2,1,0:T(2,128)(2,1)S(1)}, bf16[34,1,256]{2,1,0:T(2,128)(2,1)S(1)}, u32[]{:S(2)}, u32[]{:S(2)}) collective-permute-start(bf16[34,1,256]{2,1,0:T(2,128)(2,1)S(1)} %get-tuple-element.52), channel_id=1, source_target_pairs={{0,1},{2,3},{4,5},{6,7},{8,9},{10,11},{12,13},{14,15},{16,17},{18,... | collective-permute-start | bytes 52232 | tf_op jit(solution)/shard_map/ppermute | solution.py:17
  23.8 4.3 %collective-permute-start.3 = (bf16[34,1,256]{2,1,0:T(2,128)(2,1)S(1)}, bf16[34,1,256]{2,1,0:T(2,128)(2,1)S(1)}, u32[]{:S(2)}, u32[]{:S(2)}) collective-permute-start(bf16[34,1,256]{2,1,0:T(2,128)(2,1)S(1)} %get-tuple-element.53), channel_id=1, source_target_pairs={{1,0},{3,2},{5,4},{7,6},{9,8},{11,10},{13,12},{15,14},{17,16},{19,... | collective-permute-start | bytes 52232 | tf_op jit(solution)/shard_map/ppermute | solution.py:18
  27.5 12.8 %copy-start.10 = (bf16[256,128]{1,0:T(8,128)(2,1)S(1)}, bf16[256,128]{1,0:T(8,128)(2,1)}, u32[]{:S(2)}) copy-start(bf16[256,128]{1,0:T(8,128)(2,1)} %param.19) | copy-start | bytes 196612
  27.5 12.8 %copy-start.11 = (f32[256]{0:T(256)S(1)}, f32[256]{0:T(256)}, u32[]{:S(2)}) copy-start(f32[256]{0:T(256)} %param.18) | copy-start | bytes 3076
  27.5 12.7 %copy-start.12 = (f32[128]{0:T(128)S(1)}, f32[128]{0:T(128)}, u32[]{:S(2)}) copy-start(f32[128]{0:T(128)} %param.20) | copy-start | bytes 1540
  40.2 41.0 %copy-start.8 = (f32[128]{0:T(128)S(1)}, f32[128]{0:T(128)}, u32[]{:S(2)}) copy-start(f32[128]{0:T(128)} %param.22) | copy-start | bytes 1540
  40.2 41.0 %copy-start.9 = (f32[128]{0:T(128)S(1)}, f32[128]{0:T(128)}, u32[]{:S(2)}) copy-start(f32[128]{0:T(128)} %param.21) | copy-start | bytes 1540
  76.4 4.8 %copy-start.2 = (bf16[32,512,128]{2,1,0:T(8,128)(2,1)}, bf16[32,512,128]{2,1,0:T(8,128)(2,1)S(1)}, u32[]{:S(2)}) copy-start(bf16[32,512,128]{2,1,0:T(8,128)(2,1)S(1)} %get-tuple-element.66) | copy-start | bytes 12582916
  86.5 12.3 %copy-start.7 = (f32[4,225]{1,0:T(4,128)S(1)}, f32[4,225]{1,0:T(4,128)}, u32[]{:S(2)}) copy-start(f32[4,225]{1,0:T(4,128)} %param.24) | copy-start | bytes 10804
  92.4 96.9 %all-to-all-start = ((bf16[32,4,128,128]{3,1,2,0:T(4,128)(2,1)}), bf16[32,4,128,128]{3,1,2,0:T(4,128)(2,1)}, u32[]{:S(2)}, u32[]{:S(2)}) async-start(bf16[32,4,128,128]{3,1,2,0:T(4,128)(2,1)} %copy.60), calls=%async_computation | async-start | bytes 8388608 | tf_op jit(solution)/shard_map/all_to_all | solution.py:109
  400.5 10.4 %copy-start.3 = (bf16[32,512,128]{2,1,0:T(8,128)(2,1)S(1)}, bf16[32,512,128]{2,1,0:T(8,128)(2,1)}, u32[]{:S(2)}) copy-start(bf16[32,512,128]{2,1,0:T(8,128)(2,1)} %copy-done.2) | copy-start | bytes 12582916
  400.5 10.4 %copy-start.5 = (bf16[128,128]{1,0:T(8,128)(2,1)S(1)}, bf16[128,128]{1,0:T(8,128)(2,1)}, u32[]{:S(2)}) copy-start(bf16[128,128]{1,0:T(8,128)(2,1)} %param.25) | copy-start | bytes 98308
  409.5 4.7 %copy-start.1 = (bf16[128,384]{1,0:T(8,128)(2,1)S(1)}, bf16[128,384]{1,0:T(8,128)(2,1)}, u32[]{:S(2)}) copy-start(bf16[128,384]{1,0:T(8,128)(2,1)} %param.23) | copy-start | bytes 294916

commit v2 on v1

--- a/solution.py
+++ b/solution.py
@@ -94,63 +94,68 @@
     output_weight,
 ):
     row_count, col_count, channels = sky_map.shape
+    row_size = lax.axis_size("row")
     expanded = expand_layer(sky_map, expand_weight, expand_bias)
     padded = with_halo(expanded, (("row", 0), ("col", 1)), 1)
-    hidden = depthwise(padded, depth_weight, depth_bias, row_count, col_count)
-    after_conv = (
-        sky_map.astype(jnp.float32)
-        + jnp.dot(hidden, project_weight, preferred_element_type=jnp.float32)
-        + project_bias
-    ).astype(jnp.bfloat16)
-    normed = layer_norm(after_conv, norm_gain, norm_bias)
     across = G // lax.axis_size("col")
     stride = col_count // across
-    moved = lax.all_to_all(
-        lax.all_to_all(
-            normed.reshape(row_count, across, stride, channels),
-            "row",
-            split_axis=0,
-            concat_axis=0,
+    table = grid_bias(position_bias, G)
+    pieces = 2 if row_count % (2 * row_size) == 0 and (row_count // 2) % G == 0 else 1
+    span = row_count // pieces
+    outs = []
+    for piece in range(pieces):
+        first = piece * span
+        hidden = depthwise(padded[first : first + span + 2], depth_weight, depth_bias, span, col_count)
+        after_conv = (
+            sky_map[first : first + span].astype(jnp.float32)
+            + jnp.dot(hidden, project_weight, preferred_element_type=jnp.float32)
+            + project_bias
+        ).astype(jnp.bfloat16)
+        normed = layer_norm(after_conv, norm_gain, norm_bias)
+        moved = lax.all_to_all(
+            lax.all_to_all(
+                normed.reshape(span, across, stride, channels),
+                "row",
+                split_axis=0,
+                concat_axis=0,
+                tiled=True,
+            ),
+            "col",
+            split_axis=2,
+            concat_axis=1,
             tiled=True,
-        ),
-        "col",
-        split_axis=2,
-        concat_axis=1,
-        tiled=True,
-    )
-    projected = jnp.dot(moved, mixing_weight, preferred_element_type=jnp.float32).astype(
-        jnp.bfloat16
-    )
-    inner_rows = row_count // G
-    inner_cols = projected.shape[2]
-    grouped = (
-        projected.reshape(G, inner_rows, G, inner_cols, 3 * channels)
-        .transpose(1, 3, 0, 2, 4)
-        .reshape(inner_rows, inner_cols, G * G, 3 * channels)
-    )
-    table = grid_bias(position_bias, G)
-
-    def one_block(block):
-        return attend(block, table, HEADS)
-
-    heads_out = lax.map(one_block, grouped)
-    returned = (
-        heads_out.reshape(inner_rows, inner_cols, G, G, channels)
-        .transpose(2, 0, 3, 1, 4)
-        .reshape(row_count, G, inner_cols, channels)
-    )
-    returned = lax.all_to_all(
-        lax.all_to_all(returned, "row", split_axis=0, concat_axis=0, tiled=True),
-        "col",
-        split_axis=1,
-        concat_axis=2,
-        tiled=True,
-    )
-    returned = returned.reshape(row_count, col_count, channels)
-    return (
-        after_conv.astype(jnp.float32)
-        + jnp.dot(returned, output_weight, preferred_element_type=jnp.float32)
-    ).astype(jnp.bfloat16)
+        )
+        projected = jnp.dot(moved, mixing_weight, preferred_element_type=jnp.float32).astype(
+            jnp.bfloat16
+        )
+        inner_rows = span // G
+        inner_cols = projected.shape[2]
+        grouped = (
+            projected.reshape(G, inner_rows, G, inner_cols, 3 * channels)
+            .transpose(1, 3, 0, 2, 4)
+            .reshape(inner_rows * inner_cols, G * G, 3 * channels)
+        )
+        heads_out = attend(grouped, table, HEADS)
+        returned = (
+            heads_out.reshape(inner_rows, inner_cols, G, G, channels)
+            .transpose(2, 0, 3, 1, 4)
+            .reshape(span, G, inner_cols, channels)
+        )
+        returned = lax.all_to_all(
+            lax.all_to_all(returned, "row", split_axis=0, concat_axis=0, tiled=True),
+            "col",
+            split_axis=1,
+            concat_axis=2,
+            tiled=True,
+        )
+        returned = returned.reshape(span, col_count, channels)
+        outs.append(
+            (
+                after_conv.astype(jnp.float32)
+                + jnp.dot(returned, output_weight, preferred_element_type=jnp.float32)
+            ).astype(jnp.bfloat16)
+        )
+    return jnp.concatenate(outs, axis=0)
 
 
 def solution(mesh):

time: 421 us -> 585 us (1.39)
  local copies, waits for them, and re-layouts: 84.4 us -> 269 us
  blocking collectives: 113 us -> 25.5 us
  other arithmetic: 33.2 us -> 61.2 us
  matrix products: 78.2 us -> 106 us
  starting transfers between devices: 16.4 us -> 35.5 us
  waiting for transfers between devices: 88.2 us -> 75.7 us
    all_to_all x2, blocking collectives: 104 us -> 13 us  [body(): lax.all_to_all(lax.all_to_all(normed.reshape(span, across, stride, channe...]
    another operation x0 -> x4, local copies, waits for them, and re-layouts: none -> 58.1 us  [the longest x2 41.1 us: attend(): projected.reshape(group_count, tokens, 3, head_count, head_size)]
    unnamed x27 -> x33, local copies, waits for them, and re-layouts: 0.2 us -> 53.3 us
    reshape x1 -> x2, local copies, waits for them, and re-layouts: 9.25 us -> 60.1 us  [body(): projected.reshape(G, inner_rows, G, inner_cols, 3 * channels)]
    dynamic_slice x8 -> x0, local copies, waits for them, and re-layouts: 27.9 us -> none  [body(): heads_out = lax.map(one_block, grouped)]
    sub x4 -> x2, other arithmetic: 10.8 us -> 35.9 us  [attend(): probs = jax.nn.softmax(scores, axis=-1).astype(jnp.bfloat16)]
    all_to_all x1 -> x4, starting transfers between devices: 6.23 us -> 24.9 us  [the longest x2 14 us: body(): lax.all_to_all(normed.reshape(span, across, stride, channels), 'row', spl...]
    convert_element_type x0 -> x2, local copies, waits for them, and re-layouts: none -> 16.9 us  [attend(): return attended.astype(jnp.bfloat16).reshape(group_count, tokens, channels)]
  transfers between devices with their start and end apart: 5 -> 8, of which waited for: 3 -> 4; matrix products, arithmetic and copies ran while one was open for 3% -> 61% of each run, Pallas kernels for 0% -> 0%
where the time goes in v2:
time: 585 us; the launch traced here: 574 us
  local copies, waits for them, and re-layouts  269 us (46%)
  matrix products  106 us (18%)
  waiting for transfers between devices  75.7 us (13%)
  other arithmetic  61.2 us (10%)
  starting transfers between devices  35.5 us (6%)
  blocking collectives  25.5 us (4%)
    reshape x2, local copies, waits for them, and re-layouts, body(): projected.reshape(G, inner_rows, G, inner_cols, 3 * channels)  60.1 us
    unnamed x33, local copies, waits for them, and re-layouts  53.3 us
    all_to_all x2, waiting for transfers between devices, body(): lax.all_to_all(returned, 'row', split_axis=0, concat_axis=0, tiled=True)  42.5 us
    dot_general x2, matrix products, body(): jnp.dot(hidden, project_weight, preferred_element_type=jnp.float32)  42.1 us
    another operation x2, local copies, waits for them, and re-layouts, attend(): projected.reshape(group_count, tokens, 3, head_count, head_size)  41.1 us
    sub x2, other arithmetic, attend(): probs = jax.nn.softmax(scores, axis=-1).astype(jnp.bfloat16)  35.9 us
    all_to_all x2, waiting for transfers between devices, body(): lax.all_to_all(normed.reshape(span, across, stride, channels), 'row', spl...  23.6 us
    dot_general x2, matrix products, attend(): jnp.einsum('nqhd,nkhd->nhqk', query_part, key_part, preferred_element_typ...  23.3 us
  transfers between devices with their start and end apart: 8, of which 4 were waited for; matrix products, arithmetic and copies ran while one was open for 61% of the time, Pallas kernels for 0%

profile of v2, /device:TPU:13, one launch (start us, length us, event | category | flops | bytes accessed | tf_op | source)
XLA Modules:
  0.0 573.9 jit_solution(2565471760360706368)
XLA Ops:
  0.0 7.7 %fusion.9 = bf16[32,512,256]{2,1,0:T(8,128)(2,1)S(1)} fusion(bf16[32,512,128]{2,1,0:T(8,128)(2,1)} %param.12, f32[256]{0:T(256)} %param.14, bf16[128,256]{1,0:T(8,128)(2,1)} %param.13), kind=kOutput, calls=%fused_computation.11 | convolution fusion | flops 1115684864 | bytes 12649472 | tf_op jit(solution)/shard_map/dot_general | solution.py:29
  13.0 9.4 %collective-permute-done = bf16[1,512,256]{2,1,0:T(8,128)(2,1)S(1)} collective-permute-done((bf16[1,512,256]{2,1,0:T(8,128)(2,1)S(1)}, bf16[1,512,256]{2,1,0:T(8,128)(2,1)S(1)}, u32[]{:S(2)}, u32[]{:S(2)}) %collective-permute-start) | collective-permute-done | bytes 262176 | tf_op jit(solution)/shard_map/ppermute | solution.py:17
  28.1 12.0 %maximum_maximum_fusion = (bf16[34,513,256]{2,1,0:T(8,128)(2,1)}, bf16[34,513,256]{2,1,0:T(8,128)(2,1)}) fusion(bf16[1,512,256]{2,1,0:T(8,128)(2,1)S(1)} %collective-permute-done.1, bf16[32,512,256]{2,1,0:T(8,128)(2,1)S(1)} %fusion.9, bf16[1,512,256]{2,1,0:T(8,128)(2,1)S(1)} %collective-permute-done, bf16[34,1,256]{2,1,0:T(2,128)(2,1)S(1)} %collective-permute-done.2, ...), kind=kLoop, calls=%fused_computation.22 | loop fusion | flops 71442432 | bytes 26808320 | tf_op jit(solution)/shard_map/concatenate | solution.py:19
  40.2 21.1 %convert_reduce_fusion.1 = (f32[16,512]{1,0:T(8,128)S(1)}, bf16[16,512,128]{2,1,0:T(8,128)(2,1)S(1)}) fusion(f32[128]{0:T(128)S(1)} %copy-done.12, bf16[256,128]{1,0:T(8,128)(2,1)S(1)} %copy-done.10, bf16[34,513,256]{2,1,0:T(8,128)(2,1)} %get-tuple-element.6, bf16[32,512,256]{2,1,0:T(8,128)(2,1)} %copy-done.1, bf16[34,513,256]{2,1,0:T(8,128)(2,1)} %get-tuple-element.5, ...), kind=kOutput, calls=%fused_computation.51 | convolution fusion | flops 620748800 | bytes 46508544 | tf_op jit(solution)/shard_map/dot_general | solution.py:111
  61.3 20.9 %convert_reduce_fusion = (f32[16,512]{1,0:T(8,128)S(1)}, bf16[16,512,128]{2,1,0:T(8,128)(2,1)S(1)}) fusion(f32[128]{0:T(128)S(1)} %copy-done.12, bf16[256,128]{1,0:T(8,128)(2,1)S(1)} %copy-done.10, bf16[34,513,256]{2,1,0:T(8,128)(2,1)} %get-tuple-element.6, bf16[1,512,256]{2,1,0:T(8,128)(2,1)S(1)} %collective-permute-done.1, ...), kind=kOutput, calls=%fused_computation.48 | convolution fusion | flops 620748800 | bytes 46508544 | tf_op jit(solution)/shard_map/dot_general | solution.py:111
  103.1 14.2 %gather_fusion = f32[4096,4]{1,0:T(8,128)} fusion(f32[4,225]{0,1:T(8,128)S(1)} %copy.72, s32[4096]{0:T(1024)S(1)} %broadcast_clamp_fusion), kind=kCustom, calls=%fused_computation | custom fusion | bytes 147456 | tf_op jit(solution)/shard_map/jit(_take)/gather | solution.py:61
  124.9 23.6 %all-to-all-done = bf16[16,4,128,128]{3,1,2,0:T(4,128)(2,1)} async-done(((bf16[16,4,128,128]{3,1,2,0:T(4,128)(2,1)}), bf16[16,4,128,128]{3,1,2,0:T(4,128)(2,1)}, u32[]{:S(2)}, u32[]{:S(2)}) %all-to-all-start) | async-done | bytes 2097184 | tf_op jit(solution)/shard_map/all_to_all | solution.py:116
  157.7 7.3 %all-to-all-start.4 = ((bf16[16,4,128,128]{3,1,2,0:T(4,128)(2,1)}), bf16[16,4,128,128]{3,1,2,0:T(4,128)(2,1)}, u32[]{:S(2)}, u32[]{:S(2)}) async-start(bf16[16,4,128,128]{3,1,2,0:T(4,128)(2,1)} %copy.80), calls=%async_computation.4 | async-start | bytes 4194304 | tf_op jit(solution)/shard_map/all_to_all | solution.py:116
  173.4 30.1 %copy.68 = bf16[8,2,8,64,384]{3,1,4,2,0:T(2,128)(2,1)} copy(bf16[8,2,8,64,384]{4,3,2,1,0:T(8,128)(2,1)} %bitcast.109) | data formatting | bytes 12582912 | tf_op jit(solution)/shard_map/reshape | solution.py:134
  203.5 20.5 %reshape_reshape.12 = bf16[128,64,3,4,32]{0,4,3,2,1:T(8,128)(2,1)} reshape(bf16[2,64,8,8,384]{1,0,4,3,2:T(2,128)(2,1)} %bitcast.107) | data formatting | bytes 12582912 | tf_op jit(solution)/shard_map/reshape;reshape | solution.py:68
  231.1 8.8 %copy.100 = bf16[128,64,1,4,32]{1,4,3,0,2:T(8,128)(2,1)} copy(bf16[128,64,1,4,32]{0,4,3,2,1:T(8,128)(2,1)} %get-tuple-element.13) | data formatting | bytes 4194304
  239.8 9.0 %copy.99 = bf16[128,64,1,4,32]{1,4,3,0,2:T(8,128)(2,1)} copy(bf16[128,64,1,4,32]{0,4,3,2,1:T(8,128)(2,1)} %get-tuple-element.12) | data formatting | bytes 4194304
  248.8 11.6 %fusion.52 = f32[128,4,64,64]{2,3,1,0:T(8,128)} fusion(bf16[128,64,1,4,32]{1,4,3,0,2:T(8,128)(2,1)} %copy.100, bf16[128,64,1,4,32]{1,4,3,0,2:T(8,128)(2,1)} %copy.99), kind=kOutput, calls=%fused_computation.73 | convolution fusion | flops 134217728 | bytes 12582912 | tf_op jit(solution)/shard_map/nqhd,nkhd->nhqk/dot_general | solution.py:73
  260.5 8.8 %copy.98 = bf16[128,64,1,4,32]{1,4,3,0,2:T(8,128)(2,1)} copy(bf16[128,64,1,4,32]{0,4,3,2,1:T(8,128)(2,1)} %get-tuple-element.11) | data formatting | bytes 4194304
  269.3 17.9 %fusion.92 = (f32[128,4,64]{2,1,0:T(4,128)S(1)}, f32[128,4,64,64]{2,3,1,0:T(8,128)}) fusion(f32[128,4,64,64]{2,3,1,0:T(8,128)} %fusion.52, f32[4,64,64]{1,2,0:T(8,128)S(1)} %select_bitcast_fusion), kind=kOutput, calls=%fused_computation.126 | output fusion | flops 12582975 | bytes 16973824 | tf_op jit(solution)/shard_map/sub | solution.py:77
  287.2 11.4 %convert_bitcast_fusion.1 = bf16[128,64,4,32]{1,3,2,0:T(8,128)(2,1)} fusion(f32[128,4,64,64]{2,3,1,0:T(8,128)} %get-tuple-element.35, f32[128,4,64]{2,1,0:T(4,128)S(1)} %get-tuple-element.34, bf16[128,64,1,4,32]{1,4,3,0,2:T(8,128)(2,1)} %copy.98), kind=kOutput, calls=%fused_computation.79 | convolution fusion | flops 139460608 | bytes 12713984 | tf_op jit(solution)/shard_map/nhqk,nkhd->nqhd/dot_general | solution.py:78
  298.6 8.4 %copy.75 = bf16[128,64,4,32]{0,3,2,1:T(8,128)(2,1)} copy(bf16[128,64,4,32]{1,3,2,0:T(8,128)(2,1)} %convert_bitcast_fusion.1) | data formatting | bytes 4194304 | tf_op jit(solution)/shard_map/convert_element_type | solution.py:79
  307.0 8.6 %reshape_reshape.13 = bf16[2,64,8,8,128]{1,0,4,3,2:T(2,128)(2,1)} reshape(bf16[128,64,4,32]{0,3,2,1:T(8,128)(2,1)} %copy.75) | data formatting | bytes 4194304 | tf_op jit(solution)/shard_map/reshape;reshape | solution.py:140
  315.6 10.6 %copy.76 = bf16[8,2,8,64,128]{4,3,2,1,0:T(8,128)(2,1)} copy(bf16[8,2,8,64,128]{3,1,4,2,0:T(2,128)(2,1)} %bitcast.111) | data formatting | bytes 4194304 | tf_op jit(solution)/shard_map/transpose | solution.py:141
  349.5 30.1 %copy.83 = bf16[8,2,8,64,384]{3,1,4,2,0:T(2,128)(2,1)} copy(bf16[8,2,8,64,384]{4,3,2,1,0:T(8,128)(2,1)} %bitcast.110) | data formatting | bytes 12582912 | tf_op jit(solution)/shard_map/reshape | solution.py:134
  379.6 20.5 %reshape_reshape.14 = bf16[128,64,3,4,32]{0,4,3,2,1:T(8,128)(2,1)} reshape(bf16[2,64,8,8,384]{1,0,4,3,2:T(2,128)(2,1)} %bitcast.108) | data formatting | bytes 12582912 | tf_op jit(solution)/shard_map/reshape;reshape | solution.py:68
  400.1 7.1 %fusion.89 = (bf16[128,64,1,4,32]{0,4,3,2,1:T(8,128)(2,1)}, bf16[128,64,1,4,32]{0,4,3,2,1:T(8,128)(2,1)}, bf16[128,64,1,4,32]{0,4,3,2,1:T(8,128)(2,1)}) fusion(bf16[128,64,3,4,32]{0,4,3,2,1:T(8,128)(2,1)} %reshape_reshape.14), kind=kLoop, calls=%fused_computation.123 | loop fusion | bytes 12582912 | tf_op jit(solution)/shard_map/slice | solution.py:71
  407.2 8.8 %copy.102 = bf16[128,64,1,4,32]{1,4,3,0,2:T(8,128)(2,1)} copy(bf16[128,64,1,4,32]{0,4,3,2,1:T(8,128)(2,1)} %get-tuple-element.15) | data formatting | bytes 4194304
  416.0 8.9 %copy.103 = bf16[128,64,1,4,32]{1,4,3,0,2:T(8,128)(2,1)} copy(bf16[128,64,1,4,32]{0,4,3,2,1:T(8,128)(2,1)} %get-tuple-element.16) | data formatting | bytes 4194304
  425.0 11.6 %fusion.48 = f32[128,4,64,64]{2,3,1,0:T(8,128)} fusion(bf16[128,64,1,4,32]{1,4,3,0,2:T(8,128)(2,1)} %copy.103, bf16[128,64,1,4,32]{1,4,3,0,2:T(8,128)(2,1)} %copy.102), kind=kOutput, calls=%fused_computation.69 | convolution fusion | flops 134217728 | bytes 12582912 | tf_op jit(solution)/shard_map/nqhd,nkhd->nhqk/dot_general | solution.py:73
  436.6 8.8 %copy.101 = bf16[128,64,1,4,32]{1,4,3,0,2:T(8,128)(2,1)} copy(bf16[128,64,1,4,32]{0,4,3,2,1:T(8,128)(2,1)} %get-tuple-element.14) | data formatting | bytes 4194304
  445.4 17.9 %fusion.91 = (f32[128,4,64]{2,1,0:T(4,128)S(1)}, f32[128,4,64,64]{2,3,1,0:T(8,128)}) fusion(f32[128,4,64,64]{2,3,1,0:T(8,128)} %fusion.48, f32[4,64,64]{1,2,0:T(8,128)S(1)} %select_bitcast_fusion), kind=kOutput, calls=%fused_computation.125 | output fusion | flops 12582975 | bytes 16973824 | tf_op jit(solution)/shard_map/sub | solution.py:77
  463.3 11.4 %convert_bitcast_fusion = bf16[128,64,4,32]{1,3,2,0:T(8,128)(2,1)} fusion(f32[128,4,64,64]{2,3,1,0:T(8,128)} %get-tuple-element.33, f32[128,4,64]{2,1,0:T(4,128)S(1)} %get-tuple-element.32, bf16[128,64,1,4,32]{1,4,3,0,2:T(8,128)(2,1)} %copy.101), kind=kOutput, calls=%fused_computation.77 | convolution fusion | flops 139460608 | bytes 12713984 | tf_op jit(solution)/shard_map/nhqk,nkhd->nqhd/dot_general | solution.py:78
  474.7 8.5 %copy.88 = bf16[128,64,4,32]{0,3,2,1:T(8,128)(2,1)} copy(bf16[128,64,4,32]{1,3,2,0:T(8,128)(2,1)} %convert_bitcast_fusion) | data formatting | bytes 4194304 | tf_op jit(solution)/shard_map/convert_element_type | solution.py:79
  483.2 8.4 %reshape_reshape.15 = bf16[2,64,8,8,128]{1,0,4,3,2:T(2,128)(2,1)} reshape(bf16[128,64,4,32]{0,3,2,1:T(8,128)(2,1)} %copy.88) | data formatting | bytes 4194304 | tf_op jit(solution)/shard_map/reshape;reshape | solution.py:140
  491.6 10.6 %copy.89 = bf16[8,2,8,64,128]{4,3,2,1,0:T(8,128)(2,1)} copy(bf16[8,2,8,64,128]{3,1,4,2,0:T(2,128)(2,1)} %bitcast.112) | data formatting | bytes 4194304 | tf_op jit(solution)/shard_map/transpose | solution.py:141
  519.5 42.5 %all-to-all-done.6 = bf16[16,8,64,128]{3,2,1,0:T(8,128)(2,1)} async-done(((bf16[16,8,64,128]{3,2,1,0:T(8,128)(2,1)}), bf16[16,8,64,128]{3,2,1,0:T(8,128)(2,1)}, u32[]{:S(2)}, u32[]{:S(2)}) %all-to-all-start.6) | async-done | bytes 2097184 | tf_op jit(solution)/shard_map/all_to_all | solution.py:145
  (75 shorter events, 115.9 us)
Async XLA Ops:
  0.0 169.0 %copy-start = (bf16[128,384]{1,0:T(8,128)(2,1)S(1)}, bf16[128,384]{1,0:T(8,128)(2,1)}, u32[]{:S(2)}) copy-start(bf16[128,384]{1,0:T(8,128)(2,1)} %param.21) | copy-start | bytes 294916
  7.7 32.5 %copy-start.1 = (bf16[32,512,256]{2,1,0:T(8,128)(2,1)}, bf16[32,512,256]{2,1,0:T(8,128)(2,1)S(1)}, u32[]{:S(2)}) copy-start(bf16[32,512,256]{2,1,0:T(8,128)(2,1)S(1)} %fusion.9) | copy-start | bytes 25165828
  7.7 20.1 %copy-start.6 = (f32[3,3,256]{2,1,0:T(4,128)S(1)}, f32[3,3,256]{2,1,0:T(4,128)}, u32[]{:S(2)}) copy-start(f32[3,3,256]{2,1,0:T(4,128)} %param.15) | copy-start | bytes 27652
  7.7 14.7 %collective-permute-start = (bf16[1,512,256]{2,1,0:T(8,128)(2,1)S(1)}, bf16[1,512,256]{2,1,0:T(8,128)(2,1)S(1)}, u32[]{:S(2)}, u32[]{:S(2)}) collective-permute-start(bf16[1,512,256]{2,1,0:T(8,128)(2,1)S(1)} %get-tuple-element.9), channel_id=1, source_target_pairs={{0,2},{2,4},{4,6},{6,8},{8,10},{10,12},{12,14},{1,3},{3,5},{5,7},{... | collective-permute-start | bytes 786440 | tf_op jit(solution)/shard_map/ppermute | solution.py:17
  10.9 11.5 %collective-permute-start.1 = (bf16[1,512,256]{2,1,0:T(8,128)(2,1)S(1)}, bf16[1,512,256]{2,1,0:T(8,128)(2,1)S(1)}, u32[]{:S(2)}, u32[]{:S(2)}) collective-permute-start(bf16[1,512,256]{2,1,0:T(8,128)(2,1)S(1)} %get-tuple-element.10), channel_id=1, source_target_pairs={{2,0},{4,2},{6,4},{8,6},{10,8},{12,10},{14,12},{3,1},{5,3},{7,5},{... | collective-permute-start | bytes 786440 | tf_op jit(solution)/shard_map/ppermute | solution.py:18
  22.5 5.4 collective-permute-start.2
  23.8 4.3 collective-permute-start.3
  27.8 12.3 %copy-start.10 = (bf16[256,128]{1,0:T(8,128)(2,1)S(1)}, bf16[256,128]{1,0:T(8,128)(2,1)}, u32[]{:S(2)}) copy-start(bf16[256,128]{1,0:T(8,128)(2,1)} %param.17) | copy-start | bytes 196612
  27.8 12.3 %copy-start.11 = (f32[256]{0:T(256)S(1)}, f32[256]{0:T(256)}, u32[]{:S(2)}) copy-start(f32[256]{0:T(256)} %param.16) | copy-start | bytes 3076
  27.8 12.3 %copy-start.12 = (f32[128]{0:T(128)S(1)}, f32[128]{0:T(128)}, u32[]{:S(2)}) copy-start(f32[128]{0:T(128)} %param.18) | copy-start | bytes 1540
  61.3 25.8 %copy-start.8 = (f32[128]{0:T(128)S(1)}, f32[128]{0:T(128)}, u32[]{:S(2)}) copy-start(f32[128]{0:T(128)} %param.20) | copy-start | bytes 1540
  61.3 25.8 %copy-start.9 = (f32[128]{0:T(128)S(1)}, f32[128]{0:T(128)}, u32[]{:S(2)}) copy-start(f32[128]{0:T(128)} %param.19) | copy-start | bytes 1540
  82.3 4.8 copy-start.2
  87.1 15.9 %copy-start.7 = (f32[4,225]{1,0:T(4,128)S(1)}, f32[4,225]{1,0:T(4,128)}, u32[]{:S(2)}) copy-start(f32[4,225]{1,0:T(4,128)} %param.22) | copy-start | bytes 10804
  96.1 52.4 %all-to-all-start = ((bf16[16,4,128,128]{3,1,2,0:T(4,128)(2,1)}), bf16[16,4,128,128]{3,1,2,0:T(4,128)(2,1)}, u32[]{:S(2)}, u32[]{:S(2)}) async-start(bf16[16,4,128,128]{3,1,2,0:T(4,128)(2,1)} %copy.65), calls=%async_computation | async-start | bytes 4194304 | tf_op jit(solution)/shard_map/all_to_all | solution.py:116
  157.7 168.6 %all-to-all-start.4 = ((bf16[16,4,128,128]{3,1,2,0:T(4,128)(2,1)}), bf16[16,4,128,128]{3,1,2,0:T(4,128)(2,1)}, u32[]{:S(2)}, u32[]{:S(2)}) async-start(bf16[16,4,128,128]{3,1,2,0:T(4,128)(2,1)} %copy.80), calls=%async_computation.4 | async-start | bytes 4194304 | tf_op jit(solution)/shard_map/all_to_all | solution.py:116
  335.6 166.6 %all-to-all-start.2 = ((bf16[16,8,64,128]{3,2,1,0:T(8,128)(2,1)}), bf16[16,8,64,128]{3,2,1,0:T(8,128)(2,1)}, u32[]{:S(2)}, u32[]{:S(2)}) async-start(bf16[16,8,64,128]{3,2,1,0:T(8,128)(2,1)} %bitcast.113), calls=%async_computation.2 | async-start | bytes 4194304 | tf_op jit(solution)/shard_map/all_to_all | solution.py:145
  510.9 51.1 %all-to-all-start.6 = ((bf16[16,8,64,128]{3,2,1,0:T(8,128)(2,1)}), bf16[16,8,64,128]{3,2,1,0:T(8,128)(2,1)}, u32[]{:S(2)}, u32[]{:S(2)}) async-start(bf16[16,8,64,128]{3,2,1,0:T(8,128)(2,1)} %bitcast.115), calls=%async_computation.6 | async-start | bytes 4194304 | tf_op jit(solution)/shard_map/all_to_all | solution.py:145
  516.3 53.5 %copy-start.5 = (bf16[128,128]{1,0:T(8,128)(2,1)S(1)}, bf16[128,128]{1,0:T(8,128)(2,1)}, u32[]{:S(2)}) copy-start(bf16[128,128]{1,0:T(8,128)(2,1)} %param.23) | copy-start | bytes 98308
  562.0 7.8 %copy-start.4 = (bf16[16,4,2,64,128]{4,3,2,1,0:T(8,128)(2,1)S(1)}, bf16[16,4,2,64,128]{4,3,2,1,0:T(8,128)(2,1)}, u32[]{:S(2)}) copy-start(bf16[16,4,2,64,128]{4,3,2,1,0:T(8,128)(2,1)} %copy.79) | copy-start | bytes 6291460
  563.9 6.7 %copy-start.3 = (bf16[16,512,128]{2,1,0:T(8,128)(2,1)S(1)}, bf16[16,512,128]{2,1,0:T(8,128)(2,1)}, u32[]{:S(2)}) copy-start(bf16[16,512,128]{2,1,0:T(8,128)(2,1)} %copy-done.2) | copy-start | bytes 6291460

commit v3 on v2

--- a/solution.py
+++ b/solution.py
@@ -133,9 +133,9 @@
         grouped = (
             projected.reshape(G, inner_rows, G, inner_cols, 3 * channels)
             .transpose(1, 3, 0, 2, 4)
-            .reshape(inner_rows * inner_cols, G * G, 3 * channels)
+            .reshape(inner_rows, inner_cols, G * G, 3 * channels)
         )
-        heads_out = attend(grouped, table, HEADS)
+        heads_out = lax.map(lambda block: attend(block, table, HEADS), grouped)
         returned = (
             heads_out.reshape(inner_rows, inner_cols, G, G, channels)
             .transpose(2, 0, 3, 1, 4)

time: 585 us -> 365 us (0.62)
  the two profiles are of different devices: /device:TPU:13 before, /device:TPU:0 now
where the time goes in v3:
time: 365 us; the launch traced here: 360 us
  local copies, waits for them, and re-layouts  103 us (28%)
  waiting for transfers between devices  84.9 us (23%)
  matrix products  80.4 us (22%)
  other arithmetic  35.3 us (10%)
  starting transfers between devices  33.3 us (9%)
  blocking collectives  22.7 us (6%)
    all_to_all x2, waiting for transfers between devices, body(): lax.all_to_all(returned, 'row', split_axis=0, concat_axis=0, tiled=True)  45.3 us
    dot_general x2, matrix products, body(): jnp.dot(hidden, project_weight, preferred_element_type=jnp.float32)  42.3 us
    dynamic_slice x8, local copies, waits for them, and re-layouts, body(): heads_out = lax.map(lambda block: attend(block, table, HEADS), grouped)  28.4 us
    all_to_all x2, waiting for transfers between devices, body(): lax.all_to_all(normed.reshape(span, across, stride, channels), 'row', spl...  28.2 us
    gather x2, local copies, waits for them, and re-layouts, grid_bias(): return jnp.take(position_bias, offset_index, axis=1)  16.9 us
    dot_general x4, matrix products, attend(): jnp.einsum('nqhd,nkhd->nhqk', query_part, key_part, preferred_element_typ...  14.2 us
    reshape x2, local copies, waits for them, and re-layouts, body(): projected.reshape(G, inner_rows, G, inner_cols, 3 * channels)  12.9 us
    all_to_all x2, starting transfers between devices, body(): lax.all_to_all(returned, 'row', split_axis=0, concat_axis=0, tiled=True)  12.3 us
  transfers between devices with their start and end apart: 8, of which 4 were waited for; matrix products, arithmetic and copies ran while one was open for 36% of the time, Pallas kernels for 0%

profile of v3, /device:TPU:0, one launch (start us, length us, event | category | flops | bytes accessed | tf_op | source)
XLA Modules:
  0.0 360.4 jit_solution(13300325839293363781)
XLA Ops:
  0.0 7.7 %fusion.23 = bf16[32,512,256]{2,1,0:T(8,128)(2,1)S(1)} fusion(bf16[32,512,128]{2,1,0:T(8,128)(2,1)} %param.16, f32[256]{0:T(256)} %param.18, bf16[128,256]{1,0:T(8,128)(2,1)} %param.17), kind=kOutput, calls=%fused_computation.41 | convolution fusion | flops 1115684864 | bytes 12649472 | tf_op jit(solution)/shard_map/dot_general | solution.py:29
  7.7 4.9 %collective-permute-start = (bf16[1,512,256]{2,1,0:T(8,128)(2,1)S(1)}, bf16[1,512,256]{2,1,0:T(8,128)(2,1)S(1)}, u32[]{:S(2)}, u32[]{:S(2)}) collective-permute-start(bf16[1,512,256]{2,1,0:T(8,128)(2,1)S(1)} %get-tuple-element.99), channel_id=1, source_target_pairs={{0,2},{2,4},{4,6},{6,8},{8,10},{10,12},{12,14},{1,3},{3,5},{5,7},{... | collective-permute-start | bytes 786440 | tf_op jit(solution)/shard_map/ppermute | solution.py:17
  13.9 9.9 %collective-permute-done = bf16[1,512,256]{2,1,0:T(8,128)(2,1)S(1)} collective-permute-done((bf16[1,512,256]{2,1,0:T(8,128)(2,1)S(1)}, bf16[1,512,256]{2,1,0:T(8,128)(2,1)S(1)}, u32[]{:S(2)}, u32[]{:S(2)}) %collective-permute-start) | collective-permute-done | bytes 262176 | tf_op jit(solution)/shard_map/ppermute | solution.py:17
  28.3 12.1 %maximum_maximum_fusion = (bf16[34,513,256]{2,1,0:T(8,128)(2,1)}, bf16[34,513,256]{2,1,0:T(8,128)(2,1)}) fusion(bf16[1,512,256]{2,1,0:T(8,128)(2,1)S(1)} %collective-permute-done.1, bf16[32,512,256]{2,1,0:T(8,128)(2,1)S(1)} %fusion.23, bf16[1,512,256]{2,1,0:T(8,128)(2,1)S(1)} %collective-permute-done, bf16[34,1,256]{2,1,0:T(2,128)(2,1)S(1)} %collective-permute-done.2, ...), kind=kLoop, calls=%fused_computation.44 | loop fusion | flops 71442432 | bytes 26808320 | tf_op jit(solution)/shard_map/concatenate | solution.py:19
  40.3 21.2 %convert_reduce_fusion.1 = (f32[16,512]{1,0:T(8,128)S(1)}, bf16[16,512,128]{2,1,0:T(8,128)(2,1)S(1)}) fusion(f32[128]{0:T(128)S(1)} %copy-done.14, bf16[256,128]{1,0:T(8,128)(2,1)S(1)} %copy-done.12, bf16[34,513,256]{2,1,0:T(8,128)(2,1)} %get-tuple-element.96, bf16[32,512,256]{2,1,0:T(8,128)(2,1)} %copy-done.1, ...), kind=kOutput, calls=%fused_computation.69 | convolution fusion | flops 620748800 | bytes 46508544 | tf_op jit(solution)/shard_map/dot_general | solution.py:111
  61.6 21.1 %convert_reduce_fusion = (f32[16,512]{1,0:T(8,128)S(1)}, bf16[16,512,128]{2,1,0:T(8,128)(2,1)S(1)}) fusion(f32[128]{0:T(128)S(1)} %copy-done.14, bf16[256,128]{1,0:T(8,128)(2,1)S(1)} %copy-done.12, bf16[34,513,256]{2,1,0:T(8,128)(2,1)} %get-tuple-element.96, bf16[1,512,256]{2,1,0:T(8,128)(2,1)S(1)} %collective-permute-done.1, ...), kind=kOutput, calls=%fused_computation.66 | convolution fusion | flops 620748800 | bytes 46508544 | tf_op jit(solution)/shard_map/dot_general | solution.py:111
  87.6 5.0 %fusion.51 = (bf16[16,512,128]{2,1,0:T(8,128)(2,1)S(1)}, bf16[16,512,128]{2,1,0:T(8,128)(2,1)S(1)}) fusion(bf16[16,512,128]{2,1,0:T(8,128)(2,1)S(1)} %get-tuple-element.113, f32[128]{0:T(128)S(1)} %copy-done.10, f32[128]{0:T(128)S(1)} %copy-done.11, f32[16,512]{1,0:T(8,128)S(1)} %get-tuple-element.117, f32[16,512]{1,0:T(8,128)S(1)} %broadcast_multiply_fusion.1, ...), kind=kLoop, calls=%fused_computation.81 | loop fusion | flops 12582912 | bytes 8520704 | tf_op jit(solution)/shard_map/convert_element_type | solution.py:49
  95.7 7.6 %all-to-all-start = ((bf16[16,4,128,128]{3,1,2,0:T(4,128)(2,1)}), bf16[16,4,128,128]{3,1,2,0:T(4,128)(2,1)}, u32[]{:S(2)}, u32[]{:S(2)}) async-start(bf16[16,4,128,128]{3,1,2,0:T(4,128)(2,1)} %copy.99), calls=%async_computation | async-start | bytes 4194304 | tf_op jit(solution)/shard_map/all_to_all | solution.py:116
  103.6 14.2 %gather_fusion = f32[4096,4]{1,0:T(8,128)} fusion(f32[4,225]{0,1:T(8,128)S(1)} %copy.103, s32[4096]{0:T(1024)S(1)} %broadcast_clamp_fusion), kind=kCustom, calls=%fused_computation | custom fusion | bytes 147456 | tf_op jit(solution)/shard_map/jit(_take)/gather | solution.py:61
  123.6 28.2 %all-to-all-done = bf16[16,4,128,128]{3,1,2,0:T(4,128)(2,1)} async-done(((bf16[16,4,128,128]{3,1,2,0:T(4,128)(2,1)}), bf16[16,4,128,128]{3,1,2,0:T(4,128)(2,1)}, u32[]{:S(2)}, u32[]{:S(2)}) %all-to-all-start) | async-done | bytes 2097184 | tf_op jit(solution)/shard_map/all_to_all | solution.py:116
  154.6 5.4 %all_to_all.86 = bf16[16,4,128,128]{3,1,0,2:T(4,128)(2,1)S(1)} all-to-all(bf16[16,4,128,128]{3,1,0,2:T(4,128)(2,1)S(1)} %copy.100), channel_id=1, replica_groups=mesh['groups'=2,'row'=8,'col'=2] {'col'}, dimensions={2} | all-to-all | bytes 4194304 | tf_op jit(solution)/shard_map/all_to_all | solution.py:115
  160.1 4.3 %all-to-all-start.4 = ((bf16[16,4,128,128]{3,1,2,0:T(4,128)(2,1)}), bf16[16,4,128,128]{3,1,2,0:T(4,128)(2,1)}, u32[]{:S(2)}, u32[]{:S(2)}) async-start(bf16[16,4,128,128]{3,1,2,0:T(4,128)(2,1)} %copy.111), calls=%async_computation.4 | async-start | bytes 4194304 | tf_op jit(solution)/shard_map/all_to_all | solution.py:116
  168.6 6.5 %copy.141 = bf16[8,2,8,64,384]{4,2,0,3,1:T(8,128)(2,1)} copy(bf16[8,2,8,64,384]{4,3,2,1,0:T(8,128)(2,1)S(1)} %bitcast.151) | data formatting | bytes 12582912 | tf_op jit(solution)/shard_map/reshape | solution.py:134
  176.9 36.7 %while.20 = (s32[]{:T(128)}, bf16[2,64,64,128]{3,2,1,0:T(8,128)(2,1)}, bf16[2,64,64,384]{3,2,1,0:T(8,128)(2,1)}, f32[4,64,64]{1,2,0:T(8,128)S(1)}, s32[]{:T(128)}) while((s32[]{:T(128)}, bf16[2,64,64,128]{3,2,1,0:T(8,128)(2,1)}, bf16[2,64,64,384]{3,2,1,0:T(8,128)(2,1)}, f32[4,64,64]{1,2,0:T(8,128)S(1)}, s32[]{:T(128)}) %tuple.66), condition=%wide.region_5.6_spmd, body=%wide.region_2.5_spmd.sunk | while | flops 143130688 | bytes 41091648 | solution.py:138
  179.4 4.9 %copy.146 = bf16[1,64,64,384]{2,3,1,0:T(8,128)(2,1)} copy(bf16[1,64,64,384]{3,2,1,0:T(8,128)(2,1)S(1)} %constant_dynamic-slice_fusion.4) | data formatting | bytes 6291456 | tf_op jit(solution)/shard_map/while/body/jit(dynamic_index_in_dim)/dynamic_slice | solution.py:138
  184.3 3.5 fusion.94
  197.6 4.9 %copy.146 = bf16[1,64,64,384]{2,3,1,0:T(8,128)(2,1)} copy(bf16[1,64,64,384]{3,2,1,0:T(8,128)(2,1)S(1)} %constant_dynamic-slice_fusion.4) | data formatting | bytes 6291456 | tf_op jit(solution)/shard_map/while/body/jit(dynamic_index_in_dim)/dynamic_slice | solution.py:138
  202.5 3.5 fusion.94
  213.6 4.3 %copy.107 = bf16[8,2,8,64,128]{4,3,2,1,0:T(8,128)(2,1)} copy(bf16[8,2,8,64,128]{4,2,0,3,1:T(8,128)(2,1)} %bitcast.161) | data formatting | bytes 4194304 | tf_op jit(solution)/shard_map/transpose | solution.py:141
  220.7 5.4 %all_to_all.87 = bf16[16,4,128,128]{3,1,0,2:T(4,128)(2,1)S(1)} all-to-all(bf16[16,4,128,128]{3,1,0,2:T(4,128)(2,1)S(1)} %copy.112), channel_id=1, replica_groups=mesh['groups'=2,'row'=8,'col'=2] {'col'}, dimensions={2} | all-to-all | bytes 4194304 | tf_op jit(solution)/shard_map/all_to_all | solution.py:115
  226.1 6.4 %all-to-all-start.2 = ((bf16[16,8,64,128]{3,2,1,0:T(8,128)(2,1)}), bf16[16,8,64,128]{3,2,1,0:T(8,128)(2,1)}, u32[]{:S(2)}, u32[]{:S(2)}) async-start(bf16[16,8,64,128]{3,2,1,0:T(8,128)(2,1)} %bitcast.36), calls=%async_computation.2 | async-start | bytes 4194304 | tf_op jit(solution)/shard_map/all_to_all | solution.py:145
  236.7 6.5 %copy.140 = bf16[8,2,8,64,384]{4,2,0,3,1:T(8,128)(2,1)} copy(bf16[8,2,8,64,384]{4,3,2,1,0:T(8,128)(2,1)S(1)} %bitcast.152) | data formatting | bytes 12582912 | tf_op jit(solution)/shard_map/reshape | solution.py:134
  245.0 36.6 %while.21 = (s32[]{:T(128)}, bf16[2,64,64,128]{3,2,1,0:T(8,128)(2,1)}, bf16[2,64,64,384]{3,2,1,0:T(8,128)(2,1)}, f32[4,64,64]{1,2,0:T(8,128)S(1)}, s32[]{:T(128)}) while((s32[]{:T(128)}, bf16[2,64,64,128]{3,2,1,0:T(8,128)(2,1)}, bf16[2,64,64,384]{3,2,1,0:T(8,128)(2,1)}, f32[4,64,64]{1,2,0:T(8,128)S(1)}, s32[]{:T(128)}) %tuple.67), condition=%wide.region_11.12_spmd, body=%wide.region_8.11_spmd.sunk | while | flops 143130688 | bytes 41091648 | solution.py:138
  247.4 4.9 %copy.148 = bf16[1,64,64,384]{2,3,1,0:T(8,128)(2,1)} copy(bf16[1,64,64,384]{3,2,1,0:T(8,128)(2,1)S(1)} %constant_dynamic-slice_fusion.5) | data formatting | bytes 6291456 | tf_op jit(solution)/shard_map/while/body/jit(dynamic_index_in_dim)/dynamic_slice | solution.py:138
  252.3 3.5 fusion.97
  265.6 4.9 %copy.148 = bf16[1,64,64,384]{2,3,1,0:T(8,128)(2,1)} copy(bf16[1,64,64,384]{3,2,1,0:T(8,128)(2,1)S(1)} %constant_dynamic-slice_fusion.5) | data formatting | bytes 6291456 | tf_op jit(solution)/shard_map/while/body/jit(dynamic_index_in_dim)/dynamic_slice | solution.py:138
  270.5 3.5 fusion.97
  281.6 4.3 %copy.117 = bf16[8,2,8,64,128]{4,3,2,1,0:T(8,128)(2,1)} copy(bf16[8,2,8,64,128]{4,2,0,3,1:T(8,128)(2,1)} %bitcast.159) | data formatting | bytes 4194304 | tf_op jit(solution)/shard_map/transpose | solution.py:141
  287.6 6.3 %all_to_all.88 = bf16[16,8,64,128]{3,2,0,1:T(8,128)(2,1)} all-to-all(bf16[16,8,64,128]{3,2,0,1:T(8,128)(2,1)S(1)} %copy.108), channel_id=1, replica_groups=mesh['groups'=2,'row'=8,'col'=2] {'col'}, dimensions={1} | all-to-all | bytes 4194304 | tf_op jit(solution)/shard_map/all_to_all | solution.py:144
  294.0 6.0 %all-to-all-start.6 = ((bf16[16,8,64,128]{3,2,1,0:T(8,128)(2,1)}), bf16[16,8,64,128]{3,2,1,0:T(8,128)(2,1)}, u32[]{:S(2)}, u32[]{:S(2)}) async-start(bf16[16,8,64,128]{3,2,1,0:T(8,128)(2,1)} %bitcast.52), calls=%async_computation.6 | async-start | bytes 4194304 | tf_op jit(solution)/shard_map/all_to_all | solution.py:145
  303.3 45.3 %all-to-all-done.6 = bf16[16,8,64,128]{3,2,1,0:T(8,128)(2,1)} async-done(((bf16[16,8,64,128]{3,2,1,0:T(8,128)(2,1)}), bf16[16,8,64,128]{3,2,1,0:T(8,128)(2,1)}, u32[]{:S(2)}, u32[]{:S(2)}) %all-to-all-start.6) | async-done | bytes 2097184 | tf_op jit(solution)/shard_map/all_to_all | solution.py:145
  350.5 5.5 %all_to_all.89 = bf16[16,8,64,128]{3,2,0,1:T(8,128)(2,1)S(1)} all-to-all(bf16[16,8,64,128]{3,2,0,1:T(8,128)(2,1)S(1)} %copy.118), channel_id=1, replica_groups=mesh['groups'=2,'row'=8,'col'=2] {'col'}, dimensions={1} | all-to-all | bytes 4194304 | tf_op jit(solution)/shard_map/all_to_all | solution.py:144
  (91 shorter events, 87.5 us)
Async XLA Ops:
  0.0 166.8 %copy-start = (bf16[128,384]{1,0:T(8,128)(2,1)S(1)}, bf16[128,384]{1,0:T(8,128)(2,1)}, u32[]{:S(2)}) copy-start(bf16[128,384]{1,0:T(8,128)(2,1)} %param.25) | copy-start | bytes 294916
  7.7 32.7 %copy-start.1 = (bf16[32,512,256]{2,1,0:T(8,128)(2,1)}, bf16[32,512,256]{2,1,0:T(8,128)(2,1)S(1)}, u32[]{:S(2)}) copy-start(bf16[32,512,256]{2,1,0:T(8,128)(2,1)S(1)} %fusion.23) | copy-start | bytes 25165828
  7.7 19.1 %copy-start.8 = (f32[3,3,256]{2,1,0:T(4,128)S(1)}, f32[3,3,256]{2,1,0:T(4,128)}, u32[]{:S(2)}) copy-start(f32[3,3,256]{2,1,0:T(4,128)} %param.19) | copy-start | bytes 27652
  7.7 16.0 %collective-permute-start = (bf16[1,512,256]{2,1,0:T(8,128)(2,1)S(1)}, bf16[1,512,256]{2,1,0:T(8,128)(2,1)S(1)}, u32[]{:S(2)}, u32[]{:S(2)}) collective-permute-start(bf16[1,512,256]{2,1,0:T(8,128)(2,1)S(1)} %get-tuple-element.99), channel_id=1, source_target_pairs={{0,2},{2,4},{4,6},{6,8},{8,10},{10,12},{12,14},{1,3},{3,5},{5,7},{... | collective-permute-start | bytes 786440 | tf_op jit(solution)/shard_map/ppermute | solution.py:17
  12.6 11.2 %collective-permute-start.1 = (bf16[1,512,256]{2,1,0:T(8,128)(2,1)S(1)}, bf16[1,512,256]{2,1,0:T(8,128)(2,1)S(1)}, u32[]{:S(2)}, u32[]{:S(2)}) collective-permute-start(bf16[1,512,256]{2,1,0:T(8,128)(2,1)S(1)} %get-tuple-element.100), channel_id=1, source_target_pairs={{2,0},{4,2},{6,4},{8,6},{10,8},{12,10},{14,12},{3,1},{5,3},{7,5},{... | collective-permute-start | bytes 786440 | tf_op jit(solution)/shard_map/ppermute | solution.py:18
  23.9 3.0 collective-permute-start.2
  25.2 3.1 collective-permute-start.3
  26.8 13.6 %copy-start.12 = (bf16[256,128]{1,0:T(8,128)(2,1)S(1)}, bf16[256,128]{1,0:T(8,128)(2,1)}, u32[]{:S(2)}) copy-start(bf16[256,128]{1,0:T(8,128)(2,1)} %param.21) | copy-start | bytes 196612
  26.8 13.5 %copy-start.13 = (f32[256]{0:T(256)S(1)}, f32[256]{0:T(256)}, u32[]{:S(2)}) copy-start(f32[256]{0:T(256)} %param.20) | copy-start | bytes 3076
  26.8 13.5 %copy-start.14 = (f32[128]{0:T(128)S(1)}, f32[128]{0:T(128)}, u32[]{:S(2)}) copy-start(f32[128]{0:T(128)} %param.22) | copy-start | bytes 1540
  61.5 26.0 %copy-start.2 = (bf16[16,512,128]{2,1,0:T(8,128)(2,1)}, bf16[16,512,128]{2,1,0:T(8,128)(2,1)S(1)}, u32[]{:S(2)}) copy-start(bf16[16,512,128]{2,1,0:T(8,128)(2,1)S(1)} %get-tuple-element.113) | copy-start | bytes 6291460
  61.5 26.0 %copy-start.10 = (f32[128]{0:T(128)S(1)}, f32[128]{0:T(128)}, u32[]{:S(2)}) copy-start(f32[128]{0:T(128)} %param.24) | copy-start | bytes 1540
  61.6 26.0 %copy-start.11 = (f32[128]{0:T(128)S(1)}, f32[128]{0:T(128)}, u32[]{:S(2)}) copy-start(f32[128]{0:T(128)} %param.23) | copy-start | bytes 1540
  82.7 9.9 %copy-start.4 = (bf16[16,512,128]{2,1,0:T(8,128)(2,1)}, bf16[16,512,128]{2,1,0:T(8,128)(2,1)S(1)}, u32[]{:S(2)}) copy-start(bf16[16,512,128]{2,1,0:T(8,128)(2,1)S(1)} %get-tuple-element.115) | copy-start | bytes 6291460
  87.6 15.9 %copy-start.9 = (f32[4,225]{1,0:T(4,128)S(1)}, f32[4,225]{1,0:T(4,128)}, u32[]{:S(2)}) copy-start(f32[4,225]{1,0:T(4,128)} %param.26) | copy-start | bytes 10804
  95.7 56.2 %all-to-all-start = ((bf16[16,4,128,128]{3,1,2,0:T(4,128)(2,1)}), bf16[16,4,128,128]{3,1,2,0:T(4,128)(2,1)}, u32[]{:S(2)}, u32[]{:S(2)}) async-start(bf16[16,4,128,128]{3,1,2,0:T(4,128)(2,1)} %copy.99), calls=%async_computation | async-start | bytes 4194304 | tf_op jit(solution)/shard_map/all_to_all | solution.py:116
  160.1 57.8 %all-to-all-start.4 = ((bf16[16,4,128,128]{3,1,2,0:T(4,128)(2,1)}), bf16[16,4,128,128]{3,1,2,0:T(4,128)(2,1)}, u32[]{:S(2)}, u32[]{:S(2)}) async-start(bf16[16,4,128,128]{3,1,2,0:T(4,128)(2,1)} %copy.111), calls=%async_computation.4 | async-start | bytes 4194304 | tf_op jit(solution)/shard_map/all_to_all | solution.py:116
  226.1 59.8 %all-to-all-start.2 = ((bf16[16,8,64,128]{3,2,1,0:T(8,128)(2,1)}), bf16[16,8,64,128]{3,2,1,0:T(8,128)(2,1)}, u32[]{:S(2)}, u32[]{:S(2)}) async-start(bf16[16,8,64,128]{3,2,1,0:T(8,128)(2,1)} %bitcast.36), calls=%async_computation.2 | async-start | bytes 4194304 | tf_op jit(solution)/shard_map/all_to_all | solution.py:145
  294.0 54.6 %all-to-all-start.6 = ((bf16[16,8,64,128]{3,2,1,0:T(8,128)(2,1)}), bf16[16,8,64,128]{3,2,1,0:T(8,128)(2,1)}, u32[]{:S(2)}, u32[]{:S(2)}) async-start(bf16[16,8,64,128]{3,2,1,0:T(8,128)(2,1)} %bitcast.52), calls=%async_computation.6 | async-start | bytes 4194304 | tf_op jit(solution)/shard_map/all_to_all | solution.py:145
  300.0 56.4 %copy-start.3 = (bf16[16,512,128]{2,1,0:T(8,128)(2,1)S(1)}, bf16[16,512,128]{2,1,0:T(8,128)(2,1)}, u32[]{:S(2)}) copy-start(bf16[16,512,128]{2,1,0:T(8,128)(2,1)} %copy-done.2) | copy-start | bytes 6291460
  300.0 56.4 %copy-start.7 = (bf16[128,128]{1,0:T(8,128)(2,1)S(1)}, bf16[128,128]{1,0:T(8,128)(2,1)}, u32[]{:S(2)}) copy-start(bf16[128,128]{1,0:T(8,128)(2,1)} %param.27) | copy-start | bytes 98308
  348.6 7.7 %copy-start.6 = (bf16[16,4,2,64,128]{4,3,2,1,0:T(8,128)(2,1)S(1)}, bf16[16,4,2,64,128]{4,3,2,1,0:T(8,128)(2,1)}, u32[]{:S(2)}) copy-start(bf16[16,4,2,64,128]{4,3,2,1,0:T(8,128)(2,1)} %copy.110) | copy-start | bytes 6291460
  350.5 6.6 %copy-start.5 = (bf16[16,512,128]{2,1,0:T(8,128)(2,1)S(1)}, bf16[16,512,128]{2,1,0:T(8,128)(2,1)}, u32[]{:S(2)}) copy-start(bf16[16,512,128]{2,1,0:T(8,128)(2,1)} %copy-done.4) | copy-start | bytes 6291460

commit v4 on v3

--- a/solution.py
+++ b/solution.py
@@ -100,7 +100,7 @@
     across = G // lax.axis_size("col")
     stride = col_count // across
     table = grid_bias(position_bias, G)
-    pieces = 2 if row_count % (2 * row_size) == 0 and (row_count // 2) % G == 0 else 1
+    pieces = next(n for n in (4, 2, 1) if row_count % (n * row_size) == 0 and (row_count // n) % G == 0)
     span = row_count // pieces
     outs = []
     for piece in range(pieces):

time: 365 us -> 509 us (1.39)
  the two profiles are of different devices: /device:TPU:0 before, /device:TPU:13 now
where the time goes in v4:
time: 509 us; the launch traced here: 500 us
  local copies, waits for them, and re-layouts  190 us (37%)
  matrix products  90.6 us (18%)
  starting transfers between devices  73 us (14%)
  other arithmetic  64.9 us (13%)
  waiting for transfers between devices  53.6 us (11%)
  blocking collectives  26.1 us (5%)
    unnamed x63, local copies, waits for them, and re-layouts  72 us
    sub x4, other arithmetic, attend(): probs = jax.nn.softmax(scores, axis=-1).astype(jnp.bfloat16)  36.7 us
    dot_general x4, matrix products, body(): jnp.dot(hidden, project_weight, preferred_element_type=jnp.float32)  33.5 us
    slice x4, local copies, waits for them, and re-layouts, attend(): value_part = split_parts[:, :, 2]  28.7 us
    all_to_all x4, starting transfers between devices, body(): lax.all_to_all(returned, 'row', split_axis=0, concat_axis=0, tiled=True)  25.2 us
    all_to_all x4, starting transfers between devices, body(): lax.all_to_all(normed.reshape(span, across, stride, channels), 'row', spl...  24.6 us
    all_to_all x4, waiting for transfers between devices, body(): lax.all_to_all(normed.reshape(span, across, stride, channels), 'row', spl...  24.3 us
    dot_general x4, matrix products, attend(): jnp.einsum('nqhd,nkhd->nhqk', query_part, key_part, preferred_element_typ...  23.3 us
  transfers between devices with their start and end apart: 15, of which 7 were waited for; matrix products, arithmetic and copies ran while one was open for 53% of the time, Pallas kernels for 0%

profile of v4, /device:TPU:13, one launch (start us, length us, event | category | flops | bytes accessed | tf_op | source)
XLA Modules:
  0.0 499.5 jit_solution(17134381880897311488)
XLA Ops:
  0.0 7.7 %fusion.11 = bf16[32,512,256]{2,1,0:T(8,128)(2,1)S(1)} fusion(bf16[32,512,128]{2,1,0:T(8,128)(2,1)} %param.12, f32[256]{0:T(256)} %param.14, bf16[128,256]{1,0:T(8,128)(2,1)} %param.13), kind=kOutput, calls=%fused_computation.13 | convolution fusion | flops 1115684864 | bytes 12649472 | tf_op jit(solution)/shard_map/dot_general | solution.py:29
  13.0 9.4 %collective-permute-done = bf16[1,512,256]{2,1,0:T(8,128)(2,1)S(1)} collective-permute-done((bf16[1,512,256]{2,1,0:T(8,128)(2,1)S(1)}, bf16[1,512,256]{2,1,0:T(8,128)(2,1)S(1)}, u32[]{:S(2)}, u32[]{:S(2)}) %collective-permute-start) | collective-permute-done | bytes 262176 | tf_op jit(solution)/shard_map/ppermute | solution.py:17
  28.1 14.0 %maximum_maximum_fusion = (bf16[34,513,256]{2,1,0:T(8,128)(2,1)S(1)}, bf16[34,513,256]{2,1,0:T(8,128)(2,1)S(1)}) fusion(bf16[1,512,256]{2,1,0:T(8,128)(2,1)S(1)} %collective-permute-done.1, bf16[32,512,256]{2,1,0:T(8,128)(2,1)S(1)} %fusion.11, bf16[1,512,256]{2,1,0:T(8,128)(2,1)S(1)} %collective-permute-done, ...), kind=kLoop, calls=%fused_computation.14 | loop fusion | flops 71442432 | bytes 26808320 | tf_op jit(solution)/shard_map/concatenate | solution.py:19
  42.2 8.2 %convert_reduce_fusion.1 = (f32[8,512]{1,0:T(8,128)S(1)}, bf16[8,512,128]{2,1,0:T(8,128)(2,1)S(1)}) fusion(f32[128]{0:T(128)S(1)} %copy-done.24, bf16[256,128]{1,0:T(8,128)(2,1)S(1)} %copy-done.22, bf16[34,513,256]{2,1,0:T(8,128)(2,1)S(1)} %get-tuple-element.40, bf16[32,512,256]{2,1,0:T(8,128)(2,1)S(1)} %fusion.11, ...), kind=kOutput, calls=%fused_computation.88 | convolution fusion | flops 309325824 | bytes 21064192 | tf_op jit(solution)/shard_map/dot_general | solution.py:111
  50.4 8.4 %convert_reduce_fusion.2 = (f32[8,512]{1,0:T(8,128)S(1)}, bf16[8,512,128]{2,1,0:T(8,128)(2,1)S(1)}) fusion(f32[128]{0:T(128)S(1)} %copy-done.24, bf16[256,128]{1,0:T(8,128)(2,1)S(1)} %copy-done.22, bf16[34,513,256]{2,1,0:T(8,128)(2,1)S(1)} %get-tuple-element.40, bf16[32,512,256]{2,1,0:T(8,128)(2,1)S(1)} %fusion.11, ...), kind=kOutput, calls=%fused_computation.92 | convolution fusion | flops 309325824 | bytes 21064192 | tf_op jit(solution)/shard_map/dot_general | solution.py:111
  58.8 8.4 %convert_reduce_fusion = (f32[8,512]{1,0:T(8,128)S(1)}, bf16[8,512,128]{2,1,0:T(8,128)(2,1)S(1)}) fusion(f32[128]{0:T(128)S(1)} %copy-done.24, bf16[256,128]{1,0:T(8,128)(2,1)S(1)} %copy-done.22, bf16[34,513,256]{2,1,0:T(8,128)(2,1)S(1)} %get-tuple-element.40, bf16[1,512,256]{2,1,0:T(8,128)(2,1)S(1)} %collective-permute-done.1, ...), kind=kOutput, calls=%fused_computation.84 | convolution fusion | flops 310374400 | bytes 27617792 | tf_op jit(solution)/shard_map/dot_general | solution.py:111
  67.3 8.4 %convert_reduce_fusion.3 = (f32[8,512]{1,0:T(8,128)S(1)}, bf16[8,512,128]{2,1,0:T(8,128)(2,1)S(1)}) fusion(f32[128]{0:T(128)S(1)} %copy-done.24, bf16[256,128]{1,0:T(8,128)(2,1)S(1)} %copy-done.22, bf16[34,513,256]{2,1,0:T(8,128)(2,1)S(1)} %get-tuple-element.40, bf16[32,512,256]{2,1,0:T(8,128)(2,1)S(1)} %fusion.11, ...), kind=kOutput, calls=%fused_computation.96 | convolution fusion | flops 310374400 | bytes 27617792 | tf_op jit(solution)/shard_map/dot_general | solution.py:111
  88.4 6.2 %all-to-all-start = ((bf16[8,4,128,128]{3,1,2,0:T(4,128)(2,1)}), bf16[8,4,128,128]{3,1,2,0:T(4,128)(2,1)}, u32[]{:S(2)}, u32[]{:S(2)}) async-start(bf16[8,4,128,128]{3,1,2,0:T(4,128)(2,1)} %copy.127), calls=%async_computation | async-start | bytes 2097152 | tf_op jit(solution)/shard_map/all_to_all | solution.py:116
  96.4 21.4 %all-to-all-done = bf16[8,4,128,128]{3,1,2,0:T(4,128)(2,1)} async-done(((bf16[8,4,128,128]{3,1,2,0:T(4,128)(2,1)}), bf16[8,4,128,128]{3,1,2,0:T(4,128)(2,1)}, u32[]{:S(2)}, u32[]{:S(2)}) %all-to-all-start) | async-done | bytes 1048608 | tf_op jit(solution)/shard_map/all_to_all | solution.py:116
  124.1 7.2 %all-to-all-start.4 = ((bf16[8,4,128,128]{3,1,2,0:T(4,128)(2,1)}), bf16[8,4,128,128]{3,1,2,0:T(4,128)(2,1)}, u32[]{:S(2)}, u32[]{:S(2)}) async-start(bf16[8,4,128,128]{3,1,2,0:T(4,128)(2,1)} %copy.142), calls=%async_computation.4 | async-start | bytes 2097152 | tf_op jit(solution)/shard_map/all_to_all | solution.py:116
  131.7 14.2 %gather_fusion = f32[4096,4]{1,0:T(8,128)} fusion(f32[4,225]{0,1:T(8,128)S(1)} %copy.134, s32[4096]{0:T(1024)S(1)} %broadcast_clamp_fusion), kind=kCustom, calls=%fused_computation | custom fusion | bytes 147456 | tf_op jit(solution)/shard_map/jit(_take)/gather | solution.py:61
  159.9 7.2 %fusion.164 = (bf16[64,64,1,4,32]{0,4,3,2,1:T(8,128)(2,1)S(1)}, bf16[64,64,1,4,32]{0,4,3,2,1:T(8,128)(2,1)}, bf16[64,64,1,4,32]{0,4,3,2,1:T(8,128)(2,1)}) fusion(bf16[64,64,3,4,32]{0,4,3,2,1:T(8,128)(2,1)} %bitcast.191), kind=kLoop, calls=%fused_computation.212 | loop fusion | bytes 6291456 | tf_op jit(solution)/shard_map/while/body/eval_jaxpr/slice | solution.py:71
  167.1 6.3 %copy.191 = bf16[64,64,1,4,32]{1,4,3,0,2:T(8,128)(2,1)} copy(bf16[64,64,1,4,32]{0,4,3,2,1:T(8,128)(2,1)} %get-tuple-element.50) | data formatting | bytes 2097152
  173.5 6.3 %copy.192 = bf16[64,64,1,4,32]{1,4,3,0,2:T(8,128)(2,1)} copy(bf16[64,64,1,4,32]{0,4,3,2,1:T(8,128)(2,1)} %get-tuple-element.51) | data formatting | bytes 2097152
  186.5 6.8 %fusion.100 = f32[64,4,64,64]{2,3,1,0:T(8,128)} fusion(bf16[64,64,1,4,32]{1,4,3,0,2:T(8,128)(2,1)} %copy.192, bf16[64,64,1,4,32]{1,4,3,0,2:T(8,128)(2,1)} %copy.191), kind=kOutput, calls=%fused_computation.139 | convolution fusion | flops 67108864 | bytes 6291456 | tf_op jit(solution)/shard_map/while/body/eval_jaxpr/nqhd,nkhd->nhqk/dot_general | solution.py:73
  199.0 12.7 %fusion.172 = (f32[64,4,64]{2,1,0:T(4,128)}, f32[64,4,64,64]{2,3,1,0:T(8,128)}) fusion(f32[64,4,64,64]{2,3,1,0:T(8,128)} %fusion.100, f32[4,64,64]{1,2,0:T(8,128)S(1)} %select_bitcast_fusion), kind=kOutput, calls=%fused_computation.220 | output fusion | flops 6291519 | bytes 8519680 | tf_op jit(solution)/shard_map/while/body/eval_jaxpr/sub | solution.py:77
  216.7 6.5 %convert_bitcast_fusion.7 = bf16[64,64,4,32]{1,3,2,0:T(8,128)(2,1)} fusion(f32[64,4,64,64]{2,3,1,0:T(8,128)} %get-tuple-element.99, f32[64,4,64]{2,1,0:T(4,128)} %get-tuple-element.98, bf16[64,64,1,4,32]{1,4,3,0,2:T(8,128)(2,1)} %copy.190), kind=kOutput, calls=%fused_computation.149 | convolution fusion | flops 69730304 | bytes 6356992 | tf_op jit(solution)/shard_map/while/body/eval_jaxpr/nhqk,nkhd->nqhd/dot_general | solution.py:78
  236.5 7.2 %fusion.165 = (bf16[64,64,1,4,32]{0,4,3,2,1:T(8,128)(2,1)}, bf16[64,64,1,4,32]{0,4,3,2,1:T(8,128)(2,1)}, bf16[64,64,1,4,32]{0,4,3,2,1:T(8,128)(2,1)}) fusion(bf16[64,64,3,4,32]{0,4,3,2,1:T(8,128)(2,1)} %bitcast.192), kind=kLoop, calls=%fused_computation.213 | loop fusion | bytes 6291456 | tf_op jit(solution)/shard_map/while/body/eval_jaxpr/slice | solution.py:71
  249.2 6.3 %copy.195 = bf16[64,64,1,4,32]{1,4,3,0,2:T(8,128)(2,1)} copy(bf16[64,64,1,4,32]{0,4,3,2,1:T(8,128)(2,1)} %get-tuple-element.58) | data formatting | bytes 2097152
  255.5 6.5 %copy.193 = bf16[64,64,1,4,32]{1,4,3,0,2:T(8,128)(2,1)} copy(bf16[64,64,1,4,32]{0,4,3,2,1:T(8,128)(2,1)} %get-tuple-element.56) | data formatting | bytes 2097152
  280.3 9.2 %fusion.171 = (f32[64,4,64]{2,1,0:T(4,128)S(1)}, f32[64,4,64,64]{2,3,1,0:T(8,128)S(1)}) fusion(f32[64,4,64,64]{2,3,1,0:T(8,128)} %fusion.96, f32[4,64,64]{1,2,0:T(8,128)S(1)} %select_bitcast_fusion), kind=kOutput, calls=%fused_computation.219 | output fusion | flops 6291519 | bytes 8519680 | tf_op jit(solution)/shard_map/while/body/eval_jaxpr/sub | solution.py:77
  310.7 7.7 %all-to-all-start.2 = ((bf16[8,8,64,128]{3,2,1,0:T(8,128)(2,1)}), bf16[8,8,64,128]{3,2,1,0:T(8,128)(2,1)}, u32[]{:S(2)}, u32[]{:S(2)}) async-start(bf16[8,8,64,128]{3,2,1,0:T(8,128)(2,1)} %copy.138), calls=%async_computation.2 | async-start | bytes 2097152 | tf_op jit(solution)/shard_map/all_to_all | solution.py:145
  325.3 7.2 %fusion.166 = (bf16[64,64,1,4,32]{0,4,3,2,1:T(8,128)(2,1)S(1)}, bf16[64,64,1,4,32]{0,4,3,2,1:T(8,128)(2,1)}, bf16[64,64,1,4,32]{0,4,3,2,1:T(8,128)(2,1)}) fusion(bf16[64,64,3,4,32]{0,4,3,2,1:T(8,128)(2,1)} %bitcast.193), kind=kLoop, calls=%fused_computation.214 | loop fusion | bytes 6291456 | tf_op jit(solution)/shard_map/while/body/eval_jaxpr/slice | solution.py:71
  332.5 6.3 %copy.197 = bf16[64,64,1,4,32]{1,4,3,0,2:T(8,128)(2,1)} copy(bf16[64,64,1,4,32]{0,4,3,2,1:T(8,128)(2,1)} %get-tuple-element.64) | data formatting | bytes 2097152
  338.8 6.3 %copy.198 = bf16[64,64,1,4,32]{1,4,3,0,2:T(8,128)(2,1)} copy(bf16[64,64,1,4,32]{0,4,3,2,1:T(8,128)(2,1)} %get-tuple-element.66) | data formatting | bytes 2097152
  384.1 7.2 %fusion.167 = (bf16[64,64,1,4,32]{0,4,3,2,1:T(8,128)(2,1)S(1)}, bf16[64,64,1,4,32]{0,4,3,2,1:T(8,128)(2,1)}, bf16[64,64,1,4,32]{0,4,3,2,1:T(8,128)(2,1)}) fusion(bf16[64,64,3,4,32]{0,4,3,2,1:T(8,128)(2,1)} %bitcast.194), kind=kLoop, calls=%fused_computation.215 | loop fusion | bytes 6291456 | tf_op jit(solution)/shard_map/while/body/eval_jaxpr/slice | solution.py:71
  391.3 6.3 %copy.200 = bf16[64,64,1,4,32]{1,4,3,0,2:T(8,128)(2,1)} copy(bf16[64,64,1,4,32]{0,4,3,2,1:T(8,128)(2,1)} %get-tuple-element.69) | data formatting | bytes 2097152
  397.6 6.3 %copy.201 = bf16[64,64,1,4,32]{1,4,3,0,2:T(8,128)(2,1)} copy(bf16[64,64,1,4,32]{0,4,3,2,1:T(8,128)(2,1)} %get-tuple-element.70) | data formatting | bytes 2097152
  408.9 6.8 %fusion.88 = f32[64,4,64,64]{2,3,1,0:T(8,128)} fusion(bf16[64,64,1,4,32]{1,4,3,0,2:T(8,128)(2,1)} %copy.201, bf16[64,64,1,4,32]{1,4,3,0,2:T(8,128)(2,1)} %copy.200), kind=kOutput, calls=%fused_computation.127 | convolution fusion | flops 67108864 | bytes 6291456 | tf_op jit(solution)/shard_map/while/body/eval_jaxpr/nqhd,nkhd->nhqk/dot_general | solution.py:73
  421.3 9.2 %fusion.169 = (f32[64,4,64]{2,1,0:T(4,128)S(1)}, f32[64,4,64,64]{2,3,1,0:T(8,128)S(1)}) fusion(f32[64,4,64,64]{2,3,1,0:T(8,128)} %fusion.88, f32[4,64,64]{1,2,0:T(8,128)S(1)} %select_bitcast_fusion), kind=kOutput, calls=%fused_computation.217 | output fusion | flops 6291519 | bytes 8519680 | tf_op jit(solution)/shard_map/while/body/eval_jaxpr/sub | solution.py:77
  455.6 6.6 %all_to_all.175 = bf16[8,8,64,128]{3,2,0,1:T(8,128)(2,1)} all-to-all(bf16[8,8,64,128]{3,2,0,1:T(8,128)(2,1)} %copy.165), channel_id=1, replica_groups=mesh['groups'=2,'row'=8,'col'=2] {'col'}, dimensions={1} | all-to-all | bytes 2097152 | tf_op jit(solution)/shard_map/all_to_all | solution.py:144
  473.7 17.8 %all-to-all-done.14 = bf16[8,8,64,128]{3,2,1,0:T(8,128)(2,1)S(1)} async-done(((bf16[8,8,64,128]{3,2,1,0:T(8,128)(2,1)}), bf16[8,8,64,128]{3,2,1,0:T(8,128)(2,1)S(1)}, u32[]{:S(2)}, u32[]{:S(2)}) %all-to-all-start.14) | async-done | bytes 1048608 | tf_op jit(solution)/shard_map/all_to_all | solution.py:145
  (151 shorter events, 222.2 us)
Async XLA Ops:
  0.0 154.2 %copy-start = (bf16[128,384]{1,0:T(8,128)(2,1)S(1)}, bf16[128,384]{1,0:T(8,128)(2,1)}, u32[]{:S(2)}) copy-start(bf16[128,384]{1,0:T(8,128)(2,1)} %param.21) | copy-start | bytes 294916
  7.7 14.7 %collective-permute-start = (bf16[1,512,256]{2,1,0:T(8,128)(2,1)S(1)}, bf16[1,512,256]{2,1,0:T(8,128)(2,1)S(1)}, u32[]{:S(2)}, u32[]{:S(2)}) collective-permute-start(bf16[1,512,256]{2,1,0:T(8,128)(2,1)S(1)} %get-tuple-element.43), channel_id=1, source_target_pairs={{0,2},{2,4},{4,6},{6,8},{8,10},{10,12},{12,14},{1,3},{3,5},{5,7},{... | collective-permute-start | bytes 786440 | tf_op jit(solution)/shard_map/ppermute | solution.py:17
  10.9 16.4 %copy-start.18 = (f32[3,3,256]{2,1,0:T(4,128)S(1)}, f32[3,3,256]{2,1,0:T(4,128)}, u32[]{:S(2)}) copy-start(f32[3,3,256]{2,1,0:T(4,128)} %param.15) | copy-start | bytes 27652
  10.9 11.5 %collective-permute-start.1 = (bf16[1,512,256]{2,1,0:T(8,128)(2,1)S(1)}, bf16[1,512,256]{2,1,0:T(8,128)(2,1)S(1)}, u32[]{:S(2)}, u32[]{:S(2)}) collective-permute-start(bf16[1,512,256]{2,1,0:T(8,128)(2,1)S(1)} %get-tuple-element.48), channel_id=1, source_target_pairs={{2,0},{4,2},{6,4},{8,6},{10,8},{12,10},{14,12},{3,1},{5,3},{7,5},{... | collective-permute-start | bytes 786440 | tf_op jit(solution)/shard_map/ppermute | solution.py:18
  22.5 4.8 collective-permute-start.2
  23.8 4.3 collective-permute-start.3
  27.3 14.9 %copy-start.22 = (bf16[256,128]{1,0:T(8,128)(2,1)S(1)}, bf16[256,128]{1,0:T(8,128)(2,1)}, u32[]{:S(2)}) copy-start(bf16[256,128]{1,0:T(8,128)(2,1)} %param.17) | copy-start | bytes 196612
  27.3 14.9 %copy-start.23 = (f32[256]{0:T(256)S(1)}, f32[256]{0:T(256)}, u32[]{:S(2)}) copy-start(f32[256]{0:T(256)} %param.16) | copy-start | bytes 3076
  27.3 14.9 %copy-start.24 = (f32[128]{0:T(128)S(1)}, f32[128]{0:T(128)}, u32[]{:S(2)}) copy-start(f32[128]{0:T(128)} %param.18) | copy-start | bytes 1540
  50.4 30.7 %copy-start.3 = (bf16[8,512,128]{2,1,0:T(8,128)(2,1)}, bf16[8,512,128]{2,1,0:T(8,128)(2,1)S(1)}, u32[]{:S(2)}) copy-start(bf16[8,512,128]{2,1,0:T(8,128)(2,1)S(1)} %get-tuple-element.89) | copy-start | bytes 3145732
  58.8 22.2 %copy-start.5 = (bf16[8,512,128]{2,1,0:T(8,128)(2,1)}, bf16[8,512,128]{2,1,0:T(8,128)(2,1)S(1)}, u32[]{:S(2)}) copy-start(bf16[8,512,128]{2,1,0:T(8,128)(2,1)S(1)} %get-tuple-element.87) | copy-start | bytes 3145732
  67.3 13.8 %copy-start.1 = (bf16[8,512,128]{2,1,0:T(8,128)(2,1)}, bf16[8,512,128]{2,1,0:T(8,128)(2,1)S(1)}, u32[]{:S(2)}) copy-start(bf16[8,512,128]{2,1,0:T(8,128)(2,1)S(1)} %get-tuple-element.91) | copy-start | bytes 3145732
  75.7 10.9 %copy-start.7 = (bf16[8,512,128]{2,1,0:T(8,128)(2,1)}, bf16[8,512,128]{2,1,0:T(8,128)(2,1)S(1)}, u32[]{:S(2)}) copy-start(bf16[8,512,128]{2,1,0:T(8,128)(2,1)S(1)} %get-tuple-element.85) | copy-start | bytes 3145732
  88.4 29.5 %all-to-all-start = ((bf16[8,4,128,128]{3,1,2,0:T(4,128)(2,1)}), bf16[8,4,128,128]{3,1,2,0:T(4,128)(2,1)}, u32[]{:S(2)}, u32[]{:S(2)}) async-start(bf16[8,4,128,128]{3,1,2,0:T(4,128)(2,1)} %copy.127), calls=%async_computation | async-start | bytes 2097152 | tf_op jit(solution)/shard_map/all_to_all | solution.py:116
  94.6 36.9 %copy-start.19 = (f32[4,225]{1,0:T(4,128)S(1)}, f32[4,225]{1,0:T(4,128)}, u32[]{:S(2)}) copy-start(f32[4,225]{1,0:T(4,128)} %param.22) | copy-start | bytes 10804
  124.1 55.6 %all-to-all-start.4 = ((bf16[8,4,128,128]{3,1,2,0:T(4,128)(2,1)}), bf16[8,4,128,128]{3,1,2,0:T(4,128)(2,1)}, u32[]{:S(2)}, u32[]{:S(2)}) async-start(bf16[8,4,128,128]{3,1,2,0:T(4,128)(2,1)} %copy.142), calls=%async_computation.4 | async-start | bytes 2097152 | tf_op jit(solution)/shard_map/all_to_all | solution.py:116
  182.3 11.0 %all-to-all-start.5 = ((bf16[8,4,128,128]{3,1,0,2:T(4,128)(2,1)}), bf16[8,4,128,128]{3,1,0,2:T(4,128)(2,1)S(1)}, u32[]{:S(2)}, u32[]{:S(2)}) async-start(bf16[8,4,128,128]{3,1,0,2:T(4,128)(2,1)} %copy.143), calls=%async_computation.5 | async-start | bytes 2097152 | tf_op jit(solution)/shard_map/all_to_all | solution.py:115
  193.3 68.7 %all-to-all-start.8 = ((bf16[8,4,128,128]{3,1,2,0:T(4,128)(2,1)}), bf16[8,4,128,128]{3,1,2,0:T(4,128)(2,1)}, u32[]{:S(2)}, u32[]{:S(2)}) async-start(bf16[8,4,128,128]{3,1,2,0:T(4,128)(2,1)} %copy.155), calls=%async_computation.8 | async-start | bytes 2097152 | tf_op jit(solution)/shard_map/all_to_all | solution.py:116
  264.6 10.3 %all-to-all-start.9 = ((bf16[8,4,128,128]{3,1,0,2:T(4,128)(2,1)}), bf16[8,4,128,128]{3,1,0,2:T(4,128)(2,1)S(1)}, u32[]{:S(2)}, u32[]{:S(2)}) async-start(bf16[8,4,128,128]{3,1,0,2:T(4,128)(2,1)} %copy.156), calls=%async_computation.9 | async-start | bytes 2097152 | tf_op jit(solution)/shard_map/all_to_all | solution.py:115
  274.9 28.7 %all-to-all-start.12 = ((bf16[8,4,128,128]{3,1,2,0:T(4,128)(2,1)}), bf16[8,4,128,128]{3,1,2,0:T(4,128)(2,1)}, u32[]{:S(2)}, u32[]{:S(2)}) async-start(bf16[8,4,128,128]{3,1,2,0:T(4,128)(2,1)} %copy.168), calls=%async_computation.12 | async-start | bytes 2097152 | tf_op jit(solution)/shard_map/all_to_all | solution.py:116
  280.3 9.2 %copy-start.14 = (bf16[64,64,1,4,32]{1,4,3,0,2:T(8,128)(2,1)S(1)}, bf16[64,64,1,4,32]{1,4,3,0,2:T(8,128)(2,1)}, u32[]{:S(2)}) copy-start(bf16[64,64,1,4,32]{1,4,3,0,2:T(8,128)(2,1)} %copy.193) | copy-start | bytes 3145732
  310.7 48.4 %all-to-all-start.2 = ((bf16[8,8,64,128]{3,2,1,0:T(8,128)(2,1)}), bf16[8,8,64,128]{3,2,1,0:T(8,128)(2,1)}, u32[]{:S(2)}, u32[]{:S(2)}) async-start(bf16[8,8,64,128]{3,2,1,0:T(8,128)(2,1)} %copy.138), calls=%async_computation.2 | async-start | bytes 2097152 | tf_op jit(solution)/shard_map/all_to_all | solution.py:145
  353.6 11.2 %copy-start.16 = (bf16[64,64,1,4,32]{1,4,3,0,2:T(8,128)(2,1)S(1)}, bf16[64,64,1,4,32]{1,4,3,0,2:T(8,128)(2,1)}, u32[]{:S(2)}) copy-start(bf16[64,64,1,4,32]{1,4,3,0,2:T(8,128)(2,1)} %copy.196) | copy-start | bytes 3145732
  359.1 56.5 %all-to-all-start.6 = ((bf16[8,8,64,128]{3,2,1,0:T(8,128)(2,1)}), bf16[8,8,64,128]{3,2,1,0:T(8,128)(2,1)}, u32[]{:S(2)}, u32[]{:S(2)}) async-start(bf16[8,8,64,128]{3,2,1,0:T(8,128)(2,1)} %copy.151), calls=%async_computation.6 | async-start | bytes 2097152 | tf_op jit(solution)/shard_map/all_to_all | solution.py:145
  370.7 7.2 %copy-start.9 = (bf16[8,4,128,128]{3,1,0,2:T(4,128)(2,1)S(1)}, bf16[8,4,128,128]{3,1,0,2:T(4,128)(2,1)}, u32[]{:S(2)}) copy-start(bf16[8,4,128,128]{3,1,0,2:T(4,128)(2,1)} %all_to_all.173) | copy-start | bytes 3145732
  415.6 28.8 %all-to-all-start.10 = ((bf16[8,8,64,128]{3,2,1,0:T(8,128)(2,1)}), bf16[8,8,64,128]{3,2,1,0:T(8,128)(2,1)S(1)}, u32[]{:S(2)}, u32[]{:S(2)}) async-start(bf16[8,8,64,128]{3,2,1,0:T(8,128)(2,1)} %copy.164), calls=%async_computation.10 | async-start | bytes 2097152 | tf_op jit(solution)/shard_map/all_to_all | solution.py:145
  421.3 9.3 %copy-start.15 = (bf16[64,64,1,4,32]{1,4,3,0,2:T(8,128)(2,1)S(1)}, bf16[64,64,1,4,32]{1,4,3,0,2:T(8,128)(2,1)}, u32[]{:S(2)}) copy-start(bf16[64,64,1,4,32]{1,4,3,0,2:T(8,128)(2,1)} %copy.199) | copy-start | bytes 3145732
  444.5 6.6 %all-to-all-start.3 = ((bf16[8,8,64,128]{3,2,0,1:T(8,128)(2,1)}), bf16[8,8,64,128]{3,2,0,1:T(8,128)(2,1)S(1)}, u32[]{:S(2)}, u32[]{:S(2)}) async-start(bf16[8,8,64,128]{3,2,0,1:T(8,128)(2,1)} %copy.139), calls=%async_computation.3 | async-start | bytes 2097152 | tf_op jit(solution)/shard_map/all_to_all | solution.py:144
  462.2 7.7 %copy-start.8 = (bf16[8,512,128]{2,1,0:T(8,128)(2,1)S(1)}, bf16[8,512,128]{2,1,0:T(8,128)(2,1)}, u32[]{:S(2)}) copy-start(bf16[8,512,128]{2,1,0:T(8,128)(2,1)} %copy-done.7) | copy-start | bytes 3145732
  462.2 7.7 %copy-start.17 = (bf16[128,128]{1,0:T(8,128)(2,1)S(1)}, bf16[128,128]{1,0:T(8,128)(2,1)}, u32[]{:S(2)}) copy-start(bf16[128,128]{1,0:T(8,128)(2,1)} %param.23) | copy-start | bytes 98308
  462.2 29.3 %all-to-all-start.14 = ((bf16[8,8,64,128]{3,2,1,0:T(8,128)(2,1)}), bf16[8,8,64,128]{3,2,1,0:T(8,128)(2,1)S(1)}, u32[]{:S(2)}, u32[]{:S(2)}) async-start(bf16[8,8,64,128]{3,2,1,0:T(8,128)(2,1)} %copy.177), calls=%async_computation.14 | async-start | bytes 2097152 | tf_op jit(solution)/shard_map/all_to_all | solution.py:145
  472.4 24.2 %copy-start.2 = (bf16[8,512,128]{2,1,0:T(8,128)(2,1)S(1)}, bf16[8,512,128]{2,1,0:T(8,128)(2,1)}, u32[]{:S(2)}) copy-start(bf16[8,512,128]{2,1,0:T(8,128)(2,1)} %copy-done.1) | copy-start | bytes 3145732
  (8 other events, 31.3 us)

commit v5 on v3

--- a/solution.py
+++ b/solution.py
@@ -2,6 +2,7 @@
 import jax.numpy as jnp
 from jax import lax
 from jax.sharding import PartitionSpec as P
+from jax.experimental import pallas as pl
 
 HEADS = 4
 G = 8
@@ -77,6 +78,48 @@
     probs = jax.nn.softmax(scores, axis=-1).astype(jnp.bfloat16)
     attended = jnp.einsum("nhqk,nkhd->nqhd", probs, value_part, preferred_element_type=jnp.float32)
     return attended.astype(jnp.bfloat16).reshape(group_count, tokens, channels)
+
+
+def attention_kernel(x_ref, w_ref, bias_ref, o_ref):
+    block, tokens, channels = x_ref.shape
+    head_size = channels // HEADS
+    x = x_ref[...].reshape(block * tokens, channels)
+    qkv = jnp.dot(x, w_ref[...], preferred_element_type=jnp.float32).astype(jnp.bfloat16)
+    query = qkv[:, :channels]
+    key = qkv[:, channels : 2 * channels].reshape(block, tokens, channels)
+    value = qkv[:, 2 * channels :]
+    head_of = lax.broadcasted_iota(jnp.int32, (1, channels), 1) // head_size
+    out = jnp.zeros((block, tokens, channels), jnp.float32)
+    for head in range(HEADS):
+        mask = head_of == head
+        masked_query = jnp.where(mask, query, jnp.zeros_like(query)).reshape(block, tokens, channels)
+        scores = (
+            jnp.einsum("gtd,gud->gtu", masked_query, key, preferred_element_type=jnp.float32)
+            * head_size ** (-0.5)
+            + bias_ref[head][None]
+        )
+        shifted = jnp.exp(scores - jnp.max(scores, axis=-1, keepdims=True))
+        probs = (shifted / jnp.sum(shifted, axis=-1, keepdims=True)).astype(jnp.bfloat16)
+        masked_value = jnp.where(mask, value, jnp.zeros_like(value)).reshape(block, tokens, channels)
+        part = jnp.einsum("gtu,gud->gtd", probs, masked_value, preferred_element_type=jnp.float32)
+        out = jnp.where(mask.reshape(1, 1, channels), part, out)
+    o_ref[...] = out.astype(o_ref.dtype)
+
+
+def grid_attention(grouped, mixing_weight, table):
+    count, tokens, channels = grouped.shape
+    block = next(b for b in (32, 16, 8, 4, 2, 1) if count % b == 0)
+    return pl.pallas_call(
+        attention_kernel,
+        grid=(count // block,),
+        in_specs=[
+            pl.BlockSpec((block, tokens, channels), lambda i: (i, 0, 0)),
+            pl.BlockSpec(mixing_weight.shape, lambda i: (0, 0)),
+            pl.BlockSpec(table.shape, lambda i: (0, 0, 0)),
+        ],
+        out_specs=pl.BlockSpec((block, tokens, channels), lambda i: (i, 0, 0)),
+        out_shape=jax.ShapeDtypeStruct((count, tokens, channels), jnp.bfloat16),
+    )(grouped, mixing_weight, table)
 
 
 def body(
@@ -125,17 +168,14 @@
             concat_axis=1,
             tiled=True,
         )
-        projected = jnp.dot(moved, mixing_weight, preferred_element_type=jnp.float32).astype(
-            jnp.bfloat16
-        )
         inner_rows = span // G
-        inner_cols = projected.shape[2]
+        inner_cols = moved.shape[2]
         grouped = (
-            projected.reshape(G, inner_rows, G, inner_cols, 3 * channels)
+            moved.reshape(G, inner_rows, G, inner_cols, channels)
             .transpose(1, 3, 0, 2, 4)
-            .reshape(inner_rows, inner_cols, G * G, 3 * channels)
-        )
-        heads_out = lax.map(lambda block: attend(block, table, HEADS), grouped)
+            .reshape(inner_rows * inner_cols, G * G, channels)
+        )
+        heads_out = grid_attention(grouped, mixing_weight, table)
         returned = (
             heads_out.reshape(inner_rows, inner_cols, G, G, channels)
             .transpose(2, 0, 3, 1, 4)

time: 365 us -> 356 us (0.975)
  local copies, waits for them, and re-layouts: 103 us -> 58.3 us
  waiting for transfers between devices: 84.9 us -> 129 us
  Pallas kernels: 0 us -> 32 us
  matrix products: 80.4 us -> 52.2 us
  other arithmetic: 35.3 us -> 26.1 us
  starting transfers between devices: 33.3 us -> 29.6 us
    pallas_call x0 -> x2, Pallas kernels: none -> 32 us  [grid_attention(): pl.pallas_call(attention_kernel, grid=(count // block,), in_specs=[pl.Blo...]
    dot_general x10 -> x0, matrix products: 29.1 us -> none  [the longest x4 14.2 us: attend(): jnp.einsum('nqhd,nkhd->nhqk', query_part, key_part, preferred_element_typ...]
    dynamic_slice x8 -> x0, local copies, waits for them, and re-layouts: 28.4 us -> none  [body(): heads_out = lax.map(lambda block: attend(block, table, HEADS), grouped)]
    all_to_all x2, waiting for transfers between devices: 45.3 us -> 68.3 us  [body(): lax.all_to_all(returned, 'row', split_axis=0, concat_axis=0, tiled=True)]
    all_to_all x2, waiting for transfers between devices: 28.2 us -> 49 us  [body(): lax.all_to_all(normed.reshape(span, across, stride, channels), 'row', spl...]
    sub x4 -> x0, other arithmetic: 10.8 us -> none  [attend(): probs = jax.nn.softmax(scores, axis=-1).astype(jnp.bfloat16)]
    dynamic_update_slice x8 -> x0, local copies, waits for them, and re-layouts: 8.01 us -> none  [body(): heads_out = lax.map(lambda block: attend(block, table, HEADS), grouped)]
    reshape x2, local copies, waits for them, and re-layouts: 12.9 us -> 8.54 us  [body(): heads_out.reshape(inner_rows, inner_cols, G, G, channels)]
  transfers between devices with their start and end apart: 8 -> 8, of which waited for: 4 -> 7; matrix products, arithmetic and copies ran while one was open for 36% -> 13% of each run, Pallas kernels for 0% -> 9%
where the time goes in v5:
time: 356 us; the launch traced here: 352 us
  waiting for transfers between devices  129 us (36%)
  local copies, waits for them, and re-layouts  58.3 us (16%)
  matrix products  52.2 us (15%)
  Pallas kernels  32 us (9%)
  starting transfers between devices  29.6 us (8%)
  other arithmetic  26.1 us (7%)
  blocking collectives  24.4 us (7%)
    all_to_all x2, waiting for transfers between devices, body(): lax.all_to_all(returned, 'row', split_axis=0, concat_axis=0, tiled=True)  68.3 us
    all_to_all x2, waiting for transfers between devices, body(): lax.all_to_all(normed.reshape(span, across, stride, channels), 'row', spl...  49 us
    dot_general x2, matrix products, body(): jnp.dot(hidden, project_weight, preferred_element_type=jnp.float32)  42.2 us
    pallas_call x2, Pallas kernels, grid_attention(): pl.pallas_call(attention_kernel, grid=(count // block,), in_specs=[pl.Blo...  32 us
    gather x2, local copies, waits for them, and re-layouts, grid_bias(): return jnp.take(position_bias, offset_index, axis=1)  16.5 us
    all_to_all x2, blocking collectives, body(): lax.all_to_all(lax.all_to_all(normed.reshape(span, across, stride, channe...  12.6 us
    concatenate x1, other arithmetic, with_halo(): array = jnp.concatenate([before, array, after], axis=dim)  12.1 us
    all_to_all x2, blocking collectives, body(): lax.all_to_all(lax.all_to_all(returned, 'row', split_axis=0, concat_axis=...  11.8 us
  transfers between devices with their start and end apart: 8, of which 7 were waited for; matrix products, arithmetic and copies ran while one was open for 13% of the time, Pallas kernels for 9%

profile of v5, /device:TPU:0, one launch (start us, length us, event | category | flops | bytes accessed | tf_op | source)
XLA Modules:
  0.0 352.1 jit_solution(14158615488885898570)
XLA Ops:
  0.8 8.5 %fusion.7 = bf16[32,512,256]{2,1,0:T(8,128)(2,1)S(1)} fusion(bf16[32,512,128]{2,1,0:T(8,128)(2,1)} %param.12, f32[256]{0:T(256)} %param.14, bf16[128,256]{1,0:T(8,128)(2,1)S(1)} %copy-done), kind=kOutput, calls=%fused_computation.9 | convolution fusion | flops 1115684864 | bytes 12649472 | tf_op jit(solution)/shard_map/dot_general | solution.py:30
  10.8 5.5 %collective-permute-start = (bf16[1,512,256]{2,1,0:T(8,128)(2,1)S(1)}, bf16[1,512,256]{2,1,0:T(8,128)(2,1)S(1)}, u32[]{:S(2)}, u32[]{:S(2)}) collective-permute-start(bf16[1,512,256]{2,1,0:T(8,128)(2,1)S(1)} %get-tuple-element.9), channel_id=1, source_target_pairs={{0,2},{2,4},{4,6},{6,8},{8,10},{10,12},{12,14},{1,3},{3,5},{5,7},{... | collective-permute-start | bytes 786440 | tf_op jit(solution)/shard_map/ppermute | solution.py:18
  16.3 4.3 %collective-permute-done.1 = bf16[1,512,256]{2,1,0:T(8,128)(2,1)S(1)} collective-permute-done((bf16[1,512,256]{2,1,0:T(8,128)(2,1)S(1)}, bf16[1,512,256]{2,1,0:T(8,128)(2,1)S(1)}, u32[]{:S(2)}, u32[]{:S(2)}) %collective-permute-start.1) | collective-permute-done | bytes 262176 | tf_op jit(solution)/shard_map/ppermute | solution.py:19
  20.6 5.8 %collective-permute-done = bf16[1,512,256]{2,1,0:T(8,128)(2,1)S(1)} collective-permute-done((bf16[1,512,256]{2,1,0:T(8,128)(2,1)S(1)}, bf16[1,512,256]{2,1,0:T(8,128)(2,1)S(1)}, u32[]{:S(2)}, u32[]{:S(2)}) %collective-permute-start) | collective-permute-done | bytes 262176 | tf_op jit(solution)/shard_map/ppermute | solution.py:18
  31.5 12.1 %maximum_maximum_fusion = (bf16[34,513,256]{2,1,0:T(8,128)(2,1)}, bf16[34,513,256]{2,1,0:T(8,128)(2,1)}) fusion(bf16[1,512,256]{2,1,0:T(8,128)(2,1)S(1)} %collective-permute-done.1, bf16[32,512,256]{2,1,0:T(8,128)(2,1)S(1)} %fusion.7, bf16[1,512,256]{2,1,0:T(8,128)(2,1)S(1)} %collective-permute-done, bf16[34,1,256]{2,1,0:T(2,128)(2,1)S(1)} %collective-permute-done.2, ...), kind=kLoop, calls=%fused_computation.12 | loop fusion | flops 71442432 | bytes 26808320 | tf_op jit(solution)/shard_map/concatenate | solution.py:20
  43.6 20.6 %convert_reduce_fusion = (f32[16,512]{1,0:T(8,128)S(1)}, bf16[16,512,128]{2,1,0:T(8,128)(2,1)S(1)}) fusion(f32[128]{0:T(128)S(1)} %copy-done.13, bf16[256,128]{1,0:T(8,128)(2,1)S(1)} %copy-done.11, bf16[34,513,256]{2,1,0:T(8,128)(2,1)} %get-tuple-element.6, bf16[1,512,256]{2,1,0:T(8,128)(2,1)S(1)} %collective-permute-done.1, ...), kind=kOutput, calls=%fused_computation.32 | convolution fusion | flops 620748800 | bytes 46508544 | tf_op jit(solution)/shard_map/dot_general | solution.py:154
  64.3 21.7 %convert_reduce_fusion.1 = (f32[16,512]{1,0:T(8,128)S(1)}, bf16[16,512,128]{2,1,0:T(8,128)(2,1)S(1)}) fusion(f32[128]{0:T(128)S(1)} %copy-done.13, bf16[256,128]{1,0:T(8,128)(2,1)S(1)} %copy-done.11, bf16[34,513,256]{2,1,0:T(8,128)(2,1)} %get-tuple-element.6, bf16[32,512,256]{2,1,0:T(8,128)(2,1)} %copy-done.2, bf16[34,513,256]{2,1,0:T(8,128)(2,1)} %get-tuple-element.5, ...), kind=kOutput, calls=%fused_computation.35 | convolution fusion | flops 620748800 | bytes 46508544 | tf_op jit(solution)/shard_map/dot_general | solution.py:154
  90.8 5.9 %fusion.35 = (bf16[16,512,128]{2,1,0:T(8,128)(2,1)}, bf16[16,512,128]{2,1,0:T(8,128)(2,1)S(1)}) fusion(bf16[16,512,128]{2,1,0:T(8,128)(2,1)S(1)} %get-tuple-element.23, f32[128]{0:T(128)S(1)} %copy-done.9, f32[128]{0:T(128)S(1)} %copy-done.10, f32[16,512]{1,0:T(8,128)S(1)} %get-tuple-element.27, f32[16,512]{1,0:T(8,128)S(1)} %broadcast_multiply_fusion.1, ...), kind=kLoop, calls=%fused_computation.47 | loop fusion | flops 12582912 | bytes 8520704 | tf_op jit(solution)/shard_map/convert_element_type | solution.py:50
  96.7 3.1 copy.62
  99.8 6.0 %all-to-all-start.4 = ((bf16[16,4,128,128]{3,1,2,0:T(4,128)(2,1)}), bf16[16,4,128,128]{3,1,2,0:T(4,128)(2,1)}, u32[]{:S(2)}, u32[]{:S(2)}) async-start(bf16[16,4,128,128]{3,1,2,0:T(4,128)(2,1)} %copy.62), calls=%async_computation.4 | async-start | bytes 4194304 | tf_op jit(solution)/shard_map/all_to_all | solution.py:159
  105.8 4.7 %copy.51 = bf16[16,4,128,128]{3,1,2,0:T(4,128)(2,1)} copy(bf16[16,4,128,128]{3,2,1,0:T(8,128)(2,1)} %bitcast.67) | data formatting | bytes 4194304 | tf_op jit(solution)/shard_map/reshape | solution.py:160
  110.5 43.9 %all-to-all-done.4 = bf16[16,4,128,128]{3,1,2,0:T(4,128)(2,1)} async-done(((bf16[16,4,128,128]{3,1,2,0:T(4,128)(2,1)}), bf16[16,4,128,128]{3,1,2,0:T(4,128)(2,1)}, u32[]{:S(2)}, u32[]{:S(2)}) %all-to-all-start.4) | async-done | bytes 2097184 | tf_op jit(solution)/shard_map/all_to_all | solution.py:159
  154.4 2.8 copy.63
  157.2 6.3 %all_to_all.80 = bf16[16,4,128,128]{3,1,0,2:T(4,128)(2,1)} all-to-all(bf16[16,4,128,128]{3,1,0,2:T(4,128)(2,1)S(1)} %copy.63), channel_id=1, replica_groups=mesh['groups'=2,'row'=8,'col'=2] {'col'}, dimensions={2} | all-to-all | bytes 4194304 | tf_op jit(solution)/shard_map/all_to_all | solution.py:158
  163.5 4.4 %all-to-all-start = ((bf16[16,4,128,128]{3,1,2,0:T(4,128)(2,1)}), bf16[16,4,128,128]{3,1,2,0:T(4,128)(2,1)}, u32[]{:S(2)}, u32[]{:S(2)}) async-start(bf16[16,4,128,128]{3,1,2,0:T(4,128)(2,1)} %copy.51), calls=%async_computation | async-start | bytes 4194304 | tf_op jit(solution)/shard_map/all_to_all | solution.py:159
  168.2 14.2 %gather_fusion = f32[4096,4]{1,0:T(8,128)} fusion(f32[4,225]{0,1:T(8,128)S(1)} %copy.56, s32[4096]{0:T(1024)S(1)} %broadcast_clamp_fusion), kind=kCustom, calls=%fused_computation | custom fusion | bytes 147456 | tf_op jit(solution)/shard_map/jit(_take)/gather | solution.py:62
  185.4 2.9 copy.64
  191.3 16.0 %shard_map.119 = bf16[128,64,128]{2,1,0:T(8,128)(2,1)} custom-call(bf16[128,64,128]{2,1,0:T(8,128)(2,1)} %bitcast.77, bf16[128,384]{1,0:T(8,128)(2,1)} %w_ref.3, f32[4,64,64]{2,1,0:T(8,128)} %select_bitcast_fusion.bias_ref), custom_call_target="tpu_custom_call" | custom-call | tf_op jit(solution)/shard_map/pallas_call | solution.py:112
  207.3 4.3 %copy.67 = bf16[2,64,8,8,128]{4,1,3,0,2:T(8,128)(2,1)} copy(bf16[2,64,8,8,128]{4,3,2,1,0:T(8,128)(2,1)} %bitcast.78) | data formatting | bytes 4194304 | tf_op jit(solution)/shard_map/reshape | solution.py:180
  211.5 5.1 %all-to-all-done = bf16[16,4,128,128]{3,1,2,0:T(4,128)(2,1)} async-done(((bf16[16,4,128,128]{3,1,2,0:T(4,128)(2,1)}), bf16[16,4,128,128]{3,1,2,0:T(4,128)(2,1)}, u32[]{:S(2)}, u32[]{:S(2)}) %all-to-all-start) | async-done | bytes 2097184 | tf_op jit(solution)/shard_map/all_to_all | solution.py:159
  216.6 2.8 copy.52
  219.4 6.3 %all_to_all.81 = bf16[16,4,128,128]{3,1,0,2:T(4,128)(2,1)} all-to-all(bf16[16,4,128,128]{3,1,0,2:T(4,128)(2,1)S(1)} %copy.52), channel_id=1, replica_groups=mesh['groups'=2,'row'=8,'col'=2] {'col'}, dimensions={2} | all-to-all | bytes 4194304 | tf_op jit(solution)/shard_map/all_to_all | solution.py:158
  225.7 4.6 %all-to-all-start.6 = ((bf16[16,8,64,128]{3,2,1,0:T(8,128)(2,1)}), bf16[16,8,64,128]{3,2,1,0:T(8,128)(2,1)}, u32[]{:S(2)}, u32[]{:S(2)}) async-start(bf16[16,8,64,128]{3,2,1,0:T(8,128)(2,1)} %bitcast.70), calls=%async_computation.6 | async-start | bytes 4194304 | tf_op jit(solution)/shard_map/all_to_all | solution.py:185
  230.3 2.9 copy.53
  236.2 16.0 %shard_map.118 = bf16[128,64,128]{2,1,0:T(8,128)(2,1)} custom-call(bf16[128,64,128]{2,1,0:T(8,128)(2,1)} %bitcast.73, bf16[128,384]{1,0:T(8,128)(2,1)} %w_ref.3, f32[4,64,64]{2,1,0:T(8,128)} %select_bitcast_fusion.bias_ref), custom_call_target="tpu_custom_call" | custom-call | tf_op jit(solution)/shard_map/pallas_call | solution.py:112
  252.2 4.3 %copy.58 = bf16[2,64,8,8,128]{4,1,3,0,2:T(8,128)(2,1)} copy(bf16[2,64,8,8,128]{4,3,2,1,0:T(8,128)(2,1)} %bitcast.74) | data formatting | bytes 4194304 | tf_op jit(solution)/shard_map/reshape | solution.py:180
  256.5 22.6 %all-to-all-done.6 = bf16[16,8,64,128]{3,2,1,0:T(8,128)(2,1)} async-done(((bf16[16,8,64,128]{3,2,1,0:T(8,128)(2,1)}), bf16[16,8,64,128]{3,2,1,0:T(8,128)(2,1)}, u32[]{:S(2)}, u32[]{:S(2)}) %all-to-all-start.6) | async-done | bytes 2097184 | tf_op jit(solution)/shard_map/all_to_all | solution.py:185
  280.9 6.3 %all_to_all.82 = bf16[16,8,64,128]{3,2,0,1:T(8,128)(2,1)} all-to-all(bf16[16,8,64,128]{3,2,0,1:T(8,128)(2,1)S(1)} %copy.68), channel_id=1, replica_groups=mesh['groups'=2,'row'=8,'col'=2] {'col'}, dimensions={1} | all-to-all | bytes 4194304 | tf_op jit(solution)/shard_map/all_to_all | solution.py:184
  287.2 4.4 %all-to-all-start.2 = ((bf16[16,8,64,128]{3,2,1,0:T(8,128)(2,1)}), bf16[16,8,64,128]{3,2,1,0:T(8,128)(2,1)}, u32[]{:S(2)}, u32[]{:S(2)}) async-start(bf16[16,8,64,128]{3,2,1,0:T(8,128)(2,1)} %bitcast.71), calls=%async_computation.2 | async-start | bytes 4194304 | tf_op jit(solution)/shard_map/all_to_all | solution.py:185
  291.5 3.2 copy.70
  294.7 45.6 %all-to-all-done.2 = bf16[16,8,64,128]{3,2,1,0:T(8,128)(2,1)} async-done(((bf16[16,8,64,128]{3,2,1,0:T(8,128)(2,1)}), bf16[16,8,64,128]{3,2,1,0:T(8,128)(2,1)}, u32[]{:S(2)}, u32[]{:S(2)}) %all-to-all-start.2) | async-done | bytes 2097184 | tf_op jit(solution)/shard_map/all_to_all | solution.py:185
  342.3 5.5 %all_to_all.83 = bf16[16,8,64,128]{3,2,0,1:T(8,128)(2,1)S(1)} all-to-all(bf16[16,8,64,128]{3,2,0,1:T(8,128)(2,1)S(1)} %copy.59), channel_id=1, replica_groups=mesh['groups'=2,'row'=8,'col'=2] {'col'}, dimensions={1} | all-to-all | bytes 4194304 | tf_op jit(solution)/shard_map/all_to_all | solution.py:184
  (59 shorter events, 28.9 us)
Async XLA Ops:
  0.0 0.8 copy-start
  9.4 34.2 %copy-start.2 = (bf16[32,512,256]{2,1,0:T(8,128)(2,1)}, bf16[32,512,256]{2,1,0:T(8,128)(2,1)S(1)}, u32[]{:S(2)}) copy-start(bf16[32,512,256]{2,1,0:T(8,128)(2,1)S(1)} %fusion.7) | copy-start | bytes 25165828
  9.4 20.6 %copy-start.7 = (f32[3,3,256]{2,1,0:T(4,128)S(1)}, f32[3,3,256]{2,1,0:T(4,128)}, u32[]{:S(2)}) copy-start(f32[3,3,256]{2,1,0:T(4,128)} %param.15) | copy-start | bytes 27652
  9.5 11.2 %collective-permute-start.1 = (bf16[1,512,256]{2,1,0:T(8,128)(2,1)S(1)}, bf16[1,512,256]{2,1,0:T(8,128)(2,1)S(1)}, u32[]{:S(2)}, u32[]{:S(2)}) collective-permute-start(bf16[1,512,256]{2,1,0:T(8,128)(2,1)S(1)} %get-tuple-element.10), channel_id=1, source_target_pairs={{2,0},{4,2},{6,4},{8,6},{10,8},{12,10},{14,12},{3,1},{5,3},{7,5},{... | collective-permute-start | bytes 786440 | tf_op jit(solution)/shard_map/ppermute | solution.py:19
  10.8 15.6 %collective-permute-start = (bf16[1,512,256]{2,1,0:T(8,128)(2,1)S(1)}, bf16[1,512,256]{2,1,0:T(8,128)(2,1)S(1)}, u32[]{:S(2)}, u32[]{:S(2)}) collective-permute-start(bf16[1,512,256]{2,1,0:T(8,128)(2,1)S(1)} %get-tuple-element.9), channel_id=1, source_target_pairs={{0,2},{2,4},{4,6},{6,8},{8,10},{10,12},{12,14},{1,3},{3,5},{5,7},{... | collective-permute-start | bytes 786440 | tf_op jit(solution)/shard_map/ppermute | solution.py:18
  26.5 3.6 %collective-permute-start.2 = (bf16[34,1,256]{2,1,0:T(2,128)(2,1)S(1)}, bf16[34,1,256]{2,1,0:T(2,128)(2,1)S(1)}, u32[]{:S(2)}, u32[]{:S(2)}) collective-permute-start(bf16[34,1,256]{2,1,0:T(2,128)(2,1)S(1)} %get-tuple-element.7), channel_id=1, source_target_pairs={{0,1},{2,3},{4,5},{6,7},{8,9},{10,11},{12,13},{14,15},{16,17},{18,... | collective-permute-start | bytes 52232 | tf_op jit(solution)/shard_map/ppermute | solution.py:18
  28.4 3.1 collective-permute-start.3
  30.0 13.6 %copy-start.11 = (bf16[256,128]{1,0:T(8,128)(2,1)S(1)}, bf16[256,128]{1,0:T(8,128)(2,1)}, u32[]{:S(2)}) copy-start(bf16[256,128]{1,0:T(8,128)(2,1)} %param.17) | copy-start | bytes 196612
  30.0 13.6 %copy-start.12 = (f32[256]{0:T(256)S(1)}, f32[256]{0:T(256)}, u32[]{:S(2)}) copy-start(f32[256]{0:T(256)} %param.16) | copy-start | bytes 3076
  30.0 13.6 %copy-start.13 = (f32[128]{0:T(128)S(1)}, f32[128]{0:T(128)}, u32[]{:S(2)}) copy-start(f32[128]{0:T(128)} %param.18) | copy-start | bytes 1540
  64.2 26.5 %copy-start.9 = (f32[128]{0:T(128)S(1)}, f32[128]{0:T(128)}, u32[]{:S(2)}) copy-start(f32[128]{0:T(128)} %param.20) | copy-start | bytes 1540
  64.2 26.5 %copy-start.10 = (f32[128]{0:T(128)S(1)}, f32[128]{0:T(128)}, u32[]{:S(2)}) copy-start(f32[128]{0:T(128)} %param.19) | copy-start | bytes 1540
  85.9 4.8 %copy-start.3 = (bf16[16,512,128]{2,1,0:T(8,128)(2,1)}, bf16[16,512,128]{2,1,0:T(8,128)(2,1)S(1)}, u32[]{:S(2)}) copy-start(bf16[16,512,128]{2,1,0:T(8,128)(2,1)S(1)} %get-tuple-element.23) | copy-start | bytes 6291460
  99.8 54.6 %all-to-all-start.4 = ((bf16[16,4,128,128]{3,1,2,0:T(4,128)(2,1)}), bf16[16,4,128,128]{3,1,2,0:T(4,128)(2,1)}, u32[]{:S(2)}, u32[]{:S(2)}) async-start(bf16[16,4,128,128]{3,1,2,0:T(4,128)(2,1)} %copy.62), calls=%async_computation.4 | async-start | bytes 4194304 | tf_op jit(solution)/shard_map/all_to_all | solution.py:159
  105.8 62.0 %copy-start.8 = (f32[4,225]{1,0:T(4,128)S(1)}, f32[4,225]{1,0:T(4,128)}, u32[]{:S(2)}) copy-start(f32[4,225]{1,0:T(4,128)} %param.22) | copy-start | bytes 10804
  163.5 53.2 %all-to-all-start = ((bf16[16,4,128,128]{3,1,2,0:T(4,128)(2,1)}), bf16[16,4,128,128]{3,1,2,0:T(4,128)(2,1)}, u32[]{:S(2)}, u32[]{:S(2)}) async-start(bf16[16,4,128,128]{3,1,2,0:T(4,128)(2,1)} %copy.51), calls=%async_computation | async-start | bytes 4194304 | tf_op jit(solution)/shard_map/all_to_all | solution.py:159
  225.7 53.4 %all-to-all-start.6 = ((bf16[16,8,64,128]{3,2,1,0:T(8,128)(2,1)}), bf16[16,8,64,128]{3,2,1,0:T(8,128)(2,1)}, u32[]{:S(2)}, u32[]{:S(2)}) async-start(bf16[16,8,64,128]{3,2,1,0:T(8,128)(2,1)} %bitcast.70), calls=%async_computation.6 | async-start | bytes 4194304 | tf_op jit(solution)/shard_map/all_to_all | solution.py:185
  287.2 53.2 %all-to-all-start.2 = ((bf16[16,8,64,128]{3,2,1,0:T(8,128)(2,1)}), bf16[16,8,64,128]{3,2,1,0:T(8,128)(2,1)}, u32[]{:S(2)}, u32[]{:S(2)}) async-start(bf16[16,8,64,128]{3,2,1,0:T(8,128)(2,1)} %bitcast.71), calls=%async_computation.2 | async-start | bytes 4194304 | tf_op jit(solution)/shard_map/all_to_all | solution.py:185
  291.5 56.5 %copy-start.6 = (bf16[128,128]{1,0:T(8,128)(2,1)S(1)}, bf16[128,128]{1,0:T(8,128)(2,1)}, u32[]{:S(2)}) copy-start(bf16[128,128]{1,0:T(8,128)(2,1)} %param.23) | copy-start | bytes 98308
  340.3 7.7 %copy-start.5 = (bf16[16,4,2,64,128]{4,3,2,1,0:T(8,128)(2,1)S(1)}, bf16[16,4,2,64,128]{4,3,2,1,0:T(8,128)(2,1)}, u32[]{:S(2)}) copy-start(bf16[16,4,2,64,128]{4,3,2,1,0:T(8,128)(2,1)} %copy.70) | copy-start | bytes 6291460
  342.2 6.6 %copy-start.4 = (bf16[16,512,128]{2,1,0:T(8,128)(2,1)S(1)}, bf16[16,512,128]{2,1,0:T(8,128)(2,1)}, u32[]{:S(2)}) copy-start(bf16[16,512,128]{2,1,0:T(8,128)(2,1)} %copy-done.3) | copy-start | bytes 6291460
  348.1 3.8 %copy-start.1 = (bf16[128,256]{1,0:T(8,128)(2,1)S(1)}, bf16[128,256]{1,0:T(8,128)(2,1)}, u32[]{:S(2)}) copy-start(bf16[128,256]{1,0:T(8,128)(2,1)} %param.13) | copy-start | bytes 196612

commit v6 on v5

--- a/solution.py
+++ b/solution.py
@@ -120,6 +120,16 @@
         out_specs=pl.BlockSpec((block, tokens, channels), lambda i: (i, 0, 0)),
         out_shape=jax.ShapeDtypeStruct((count, tokens, channels), jnp.bfloat16),
     )(grouped, mixing_weight, table)
+
+
+def pieces_of(normed, row_size, col_size, pp, span, col_count, channels):
+    across = G // col_size
+    inner_cols = col_count // across // col_size
+    return (
+        normed.reshape(row_size, pp, across, col_size, inner_cols, channels)
+        .transpose(0, 3, 1, 2, 4, 5)
+        .reshape(row_size * col_size, pp, across, inner_cols, channels)
+    )
 
 
 def body(
@@ -145,6 +155,10 @@
     table = grid_bias(position_bias, G)
     pieces = 2 if row_count % (2 * row_size) == 0 and (row_count // 2) % G == 0 else 1
     span = row_count // pieces
+    col_size = lax.axis_size("col")
+    sub = row_size // G
+    pp = span // row_size
+    inner_cols = stride // col_size
     outs = []
     for piece in range(pieces):
         first = piece * span
@@ -155,40 +169,25 @@
             + project_bias
         ).astype(jnp.bfloat16)
         normed = layer_norm(after_conv, norm_gain, norm_bias)
-        moved = lax.all_to_all(
-            lax.all_to_all(
-                normed.reshape(span, across, stride, channels),
-                "row",
-                split_axis=0,
-                concat_axis=0,
-                tiled=True,
-            ),
-            "col",
-            split_axis=2,
-            concat_axis=1,
-            tiled=True,
-        )
-        inner_rows = span // G
-        inner_cols = moved.shape[2]
+        pair = pieces_of(normed, row_size, col_size, pp, span, col_count, channels)
+        moved = lax.all_to_all(pair, ("row", "col"), 0, 0, tiled=True)
         grouped = (
-            moved.reshape(G, inner_rows, G, inner_cols, channels)
-            .transpose(1, 3, 0, 2, 4)
-            .reshape(inner_rows * inner_cols, G * G, channels)
+            moved.reshape(G, sub, col_size, pp, across, inner_cols, channels)
+            .transpose(1, 3, 5, 0, 2, 4, 6)
+            .reshape(sub * pp * inner_cols, G * G, channels)
         )
         heads_out = grid_attention(grouped, mixing_weight, table)
         returned = (
-            heads_out.reshape(inner_rows, inner_cols, G, G, channels)
-            .transpose(2, 0, 3, 1, 4)
-            .reshape(span, G, inner_cols, channels)
-        )
-        returned = lax.all_to_all(
-            lax.all_to_all(returned, "row", split_axis=0, concat_axis=0, tiled=True),
-            "col",
-            split_axis=1,
-            concat_axis=2,
-            tiled=True,
-        )
-        returned = returned.reshape(span, col_count, channels)
+            heads_out.reshape(sub, pp, inner_cols, G, col_size, across, channels)
+            .transpose(3, 0, 4, 1, 5, 2, 6)
+            .reshape(row_size * col_size, pp, across, inner_cols, channels)
+        )
+        returned = lax.all_to_all(returned, ("row", "col"), 0, 0, tiled=True)
+        returned = (
+            returned.reshape(row_size, col_size, pp, across, inner_cols, channels)
+            .transpose(0, 2, 3, 1, 4, 5)
+            .reshape(span, col_count, channels)
+        )
         outs.append(
             (
                 after_conv.astype(jnp.float32)

time: 356 us -> 320 us (0.90)
  the two profiles are of different devices: /device:TPU:0 before, /device:TPU:13 now
where the time goes in v6:
time: 320 us; the launch traced here: 316 us
  waiting for transfers between devices  125 us (39%)
  matrix products  53.5 us (17%)
  local copies, waits for them, and re-layouts  47.2 us (15%)
  Pallas kernels  32 us (10%)
  starting transfers between devices  31.7 us (10%)
  other arithmetic  26.1 us (8%)
    all_to_all x2, waiting for transfers between devices, body(): returned = lax.all_to_all(returned, ('row', 'col'), 0, 0, tiled=True)  65.8 us
    all_to_all x2, waiting for transfers between devices, body(): moved = lax.all_to_all(pair, ('row', 'col'), 0, 0, tiled=True)  48.3 us
    dot_general x2, matrix products, body(): jnp.dot(hidden, project_weight, preferred_element_type=jnp.float32)  41.9 us
    pallas_call x2, Pallas kernels, grid_attention(): pl.pallas_call(attention_kernel, grid=(count // block,), in_specs=[pl.Blo...  32 us
    gather x2, local copies, waits for them, and re-layouts, grid_bias(): return jnp.take(position_bias, offset_index, axis=1)  16.5 us
    concatenate x1, other arithmetic, with_halo(): array = jnp.concatenate([before, array, after], axis=dim)  12.1 us
    transpose x2, local copies, waits for them, and re-layouts, body(): returned = heads_out.reshape(sub, pp, inner_cols, G, col_size, across, ch...  10.7 us
    all_to_all x2, starting transfers between devices, body(): moved = lax.all_to_all(pair, ('row', 'col'), 0, 0, tiled=True)  10.5 us
  transfers between devices with their start and end apart: 8, of which 7 were waited for; matrix products, arithmetic and copies ran while one was open for 14% of the time, Pallas kernels for 10%

profile of v6, /device:TPU:13, one launch (start us, length us, event | category | flops | bytes accessed | tf_op | source)
XLA Modules:
  0.0 315.8 jit_solution(8817939884425128949)
XLA Ops:
  0.8 8.5 %fusion.7 = bf16[32,512,256]{2,1,0:T(8,128)(2,1)S(1)} fusion(bf16[32,512,128]{2,1,0:T(8,128)(2,1)} %param.12, f32[256]{0:T(256)} %param.14, bf16[128,256]{1,0:T(8,128)(2,1)S(1)} %copy-done), kind=kOutput, calls=%fused_computation.9 | convolution fusion | flops 1115684864 | bytes 12649472 | tf_op jit(solution)/shard_map/dot_general | solution.py:30
  9.5 2.1 collective-permute-start.1
  11.6 4.0 %collective-permute-start = (bf16[1,512,256]{2,1,0:T(8,128)(2,1)S(1)}, bf16[1,512,256]{2,1,0:T(8,128)(2,1)S(1)}, u32[]{:S(2)}, u32[]{:S(2)}) collective-permute-start(bf16[1,512,256]{2,1,0:T(8,128)(2,1)S(1)} %get-tuple-element.9), channel_id=1, source_target_pairs={{0,2},{2,4},{4,6},{6,8},{8,10},{10,12},{12,14},{1,3},{3,5},{5,7},{... | collective-permute-start | bytes 786440 | tf_op jit(solution)/shard_map/ppermute | solution.py:18
  15.6 6.4 %collective-permute-done.1 = bf16[1,512,256]{2,1,0:T(8,128)(2,1)S(1)} collective-permute-done((bf16[1,512,256]{2,1,0:T(8,128)(2,1)S(1)}, bf16[1,512,256]{2,1,0:T(8,128)(2,1)S(1)}, u32[]{:S(2)}, u32[]{:S(2)}) %collective-permute-start.1) | collective-permute-done | bytes 262176 | tf_op jit(solution)/shard_map/ppermute | solution.py:19
  22.0 4.1 %collective-permute-done = bf16[1,512,256]{2,1,0:T(8,128)(2,1)S(1)} collective-permute-done((bf16[1,512,256]{2,1,0:T(8,128)(2,1)S(1)}, bf16[1,512,256]{2,1,0:T(8,128)(2,1)S(1)}, u32[]{:S(2)}, u32[]{:S(2)}) %collective-permute-start) | collective-permute-done | bytes 262176 | tf_op jit(solution)/shard_map/ppermute | solution.py:18
  27.4 3.6 %collective-permute-start.3 = (bf16[34,1,256]{2,1,0:T(2,128)(2,1)S(1)}, bf16[34,1,256]{2,1,0:T(2,128)(2,1)S(1)}, u32[]{:S(2)}, u32[]{:S(2)}) collective-permute-start(bf16[34,1,256]{2,1,0:T(2,128)(2,1)S(1)} %get-tuple-element.8), channel_id=1, source_target_pairs={{1,0},{3,2},{5,4},{7,6},{9,8},{11,10},{13,12},{15,14},{17,16},{19,... | collective-permute-start | bytes 52232 | tf_op jit(solution)/shard_map/ppermute | solution.py:19
  31.3 12.1 %maximum_maximum_fusion = (bf16[34,513,256]{2,1,0:T(8,128)(2,1)}, bf16[34,513,256]{2,1,0:T(8,128)(2,1)}) fusion(bf16[1,512,256]{2,1,0:T(8,128)(2,1)S(1)} %collective-permute-done.1, bf16[32,512,256]{2,1,0:T(8,128)(2,1)S(1)} %fusion.7, bf16[1,512,256]{2,1,0:T(8,128)(2,1)S(1)} %collective-permute-done, bf16[34,1,256]{2,1,0:T(2,128)(2,1)S(1)} %collective-permute-done.2, ...), kind=kLoop, calls=%fused_computation.12 | loop fusion | flops 71442432 | bytes 26808320 | tf_op jit(solution)/shard_map/concatenate | solution.py:20
  43.5 20.6 %convert_reduce_fusion = (f32[16,512]{1,0:T(8,128)S(1)}, bf16[16,512,128]{2,1,0:T(8,128)(2,1)S(1)}) fusion(f32[128]{0:T(128)S(1)} %copy-done.12, bf16[256,128]{1,0:T(8,128)(2,1)S(1)} %copy-done.10, bf16[34,513,256]{2,1,0:T(8,128)(2,1)} %get-tuple-element.6, bf16[1,512,256]{2,1,0:T(8,128)(2,1)S(1)} %collective-permute-done.1, ...), kind=kOutput, calls=%fused_computation.32 | convolution fusion | flops 620748800 | bytes 46508544 | tf_op jit(solution)/shard_map/dot_general | solution.py:168
  64.2 21.3 %convert_reduce_fusion.1 = (f32[16,512]{1,0:T(8,128)S(1)}, bf16[16,512,128]{2,1,0:T(8,128)(2,1)S(1)}) fusion(f32[128]{0:T(128)S(1)} %copy-done.12, bf16[256,128]{1,0:T(8,128)(2,1)S(1)} %copy-done.10, bf16[34,513,256]{2,1,0:T(8,128)(2,1)} %get-tuple-element.6, bf16[32,512,256]{2,1,0:T(8,128)(2,1)} %copy-done.2, bf16[34,513,256]{2,1,0:T(8,128)(2,1)} %get-tuple-element.5, ...), kind=kOutput, calls=%fused_computation.35 | convolution fusion | flops 620748800 | bytes 46508544 | tf_op jit(solution)/shard_map/dot_general | solution.py:168
  85.5 2.4 fusion.28
  87.8 2.4 fusion.32
  90.3 5.9 %fusion.35 = (bf16[16,512,128]{2,1,0:T(8,128)(2,1)}, bf16[16,512,128]{2,1,0:T(8,128)(2,1)S(1)}) fusion(bf16[16,512,128]{2,1,0:T(8,128)(2,1)S(1)} %get-tuple-element.23, f32[128]{0:T(128)S(1)} %copy-done.8, f32[128]{0:T(128)S(1)} %copy-done.9, f32[16,512]{1,0:T(8,128)S(1)} %get-tuple-element.27, f32[16,512]{1,0:T(8,128)S(1)} %broadcast_multiply_fusion.1, ...), kind=kLoop, calls=%fused_computation.47 | loop fusion | flops 12582912 | bytes 8520704 | tf_op jit(solution)/shard_map/convert_element_type | solution.py:50
  97.7 5.2 %all-to-all-start.2 = ((bf16[16,2,4,64,128]{4,3,2,1,0:T(8,128)(2,1)}), bf16[16,2,4,64,128]{4,3,2,1,0:T(8,128)(2,1)}, u32[]{:S(2)}, u32[]{:S(2)}) async-start(bf16[16,2,4,64,128]{4,3,2,1,0:T(8,128)(2,1)} %bitcast.73), calls=%async_computation.2 | async-start | bytes 4194304 | tf_op jit(solution)/shard_map/all_to_all | solution.py:173
  102.9 3.1 copy.15
  106.1 44.4 %all-to-all-done.2 = bf16[16,2,4,64,128]{4,3,2,1,0:T(8,128)(2,1)} async-done(((bf16[16,2,4,64,128]{4,3,2,1,0:T(8,128)(2,1)}), bf16[16,2,4,64,128]{4,3,2,1,0:T(8,128)(2,1)}, u32[]{:S(2)}, u32[]{:S(2)}) %all-to-all-start.2) | async-done | bytes 2097184 | tf_op jit(solution)/shard_map/all_to_all | solution.py:173
  150.5 5.3 %all-to-all-start = ((bf16[16,2,4,64,128]{4,3,2,1,0:T(8,128)(2,1)}), bf16[16,2,4,64,128]{4,3,2,1,0:T(8,128)(2,1)}, u32[]{:S(2)}, u32[]{:S(2)}) async-start(bf16[16,2,4,64,128]{4,3,2,1,0:T(8,128)(2,1)} %bitcast.70), calls=%async_computation | async-start | bytes 4194304 | tf_op jit(solution)/shard_map/all_to_all | solution.py:173
  156.1 14.2 %gather_fusion = f32[4096,4]{1,0:T(8,128)} fusion(f32[4,225]{0,1:T(8,128)S(1)} %copy.17, s32[4096]{0:T(1024)S(1)} %broadcast_clamp_fusion), kind=kCustom, calls=%fused_computation | custom fusion | bytes 147456 | tf_op jit(solution)/shard_map/jit(_take)/gather | solution.py:62
  170.3 2.3 copy.25
  173.3 4.5 %copy.22 = bf16[8,1,2,2,4,64,128]{6,4,2,0,5,3,1:T(4,128)(2,1)} copy(bf16[8,1,2,2,4,64,128]{6,5,4,3,2,0,1:T(8,128)(2,1)} %bitcast.29) | data formatting | bytes 4194304 | tf_op jit(solution)/shard_map/reshape | solution.py:175
  177.9 16.0 %shard_map.119 = bf16[128,64,128]{2,1,0:T(8,128)(2,1)} custom-call(bf16[128,64,128]{2,1,0:T(8,128)(2,1)} %bitcast.76, bf16[128,384]{1,0:T(8,128)(2,1)} %w_ref.3, f32[4,64,64]{2,1,0:T(8,128)} %select_bitcast_fusion.bias_ref), custom_call_target="tpu_custom_call" | custom-call | tf_op jit(solution)/shard_map/pallas_call | solution.py:112
  193.8 5.3 %copy.23 = bf16[8,1,2,2,4,64,128]{6,5,4,3,2,0,1:T(8,128)(2,1)} copy(bf16[8,1,2,2,4,64,128]{6,4,2,0,5,3,1:T(4,128)(2,1)} %bitcast.77) | data formatting | bytes 4194304 | tf_op jit(solution)/shard_map/transpose | solution.py:182
  199.2 3.9 %all-to-all-done = bf16[16,2,4,64,128]{4,3,2,1,0:T(8,128)(2,1)} async-done(((bf16[16,2,4,64,128]{4,3,2,1,0:T(8,128)(2,1)}), bf16[16,2,4,64,128]{4,3,2,1,0:T(8,128)(2,1)}, u32[]{:S(2)}, u32[]{:S(2)}) %all-to-all-start) | async-done | bytes 2097184 | tf_op jit(solution)/shard_map/all_to_all | solution.py:173
  203.1 5.3 %all-to-all-start.3 = ((bf16[16,2,4,64,128]{4,3,2,1,0:T(8,128)(2,1)}), bf16[16,2,4,64,128]{4,3,2,1,0:T(8,128)(2,1)}, u32[]{:S(2)}, u32[]{:S(2)}) async-start(bf16[16,2,4,64,128]{4,3,2,1,0:T(8,128)(2,1)} %bitcast.71), calls=%async_computation.3 | async-start | bytes 4194304 | tf_op jit(solution)/shard_map/all_to_all | solution.py:185
  208.4 4.6 %copy.16 = bf16[8,1,2,2,4,64,128]{6,4,2,0,5,3,1:T(4,128)(2,1)} copy(bf16[8,1,2,2,4,64,128]{6,5,4,3,2,0,1:T(8,128)(2,1)} %bitcast.14) | data formatting | bytes 4194304 | tf_op jit(solution)/shard_map/reshape | solution.py:175
  213.0 16.0 %shard_map.118 = bf16[128,64,128]{2,1,0:T(8,128)(2,1)} custom-call(bf16[128,64,128]{2,1,0:T(8,128)(2,1)} %bitcast.74, bf16[128,384]{1,0:T(8,128)(2,1)} %w_ref.3, f32[4,64,64]{2,1,0:T(8,128)} %select_bitcast_fusion.bias_ref), custom_call_target="tpu_custom_call" | custom-call | tf_op jit(solution)/shard_map/pallas_call | solution.py:112
  229.0 5.4 %copy.19 = bf16[8,1,2,2,4,64,128]{6,5,4,3,2,0,1:T(8,128)(2,1)} copy(bf16[8,1,2,2,4,64,128]{6,4,2,0,5,3,1:T(4,128)(2,1)} %bitcast.75) | data formatting | bytes 4194304 | tf_op jit(solution)/shard_map/transpose | solution.py:182
  234.4 21.4 %all-to-all-done.3 = bf16[16,2,4,64,128]{4,3,2,1,0:T(8,128)(2,1)} async-done(((bf16[16,2,4,64,128]{4,3,2,1,0:T(8,128)(2,1)}), bf16[16,2,4,64,128]{4,3,2,1,0:T(8,128)(2,1)}, u32[]{:S(2)}, u32[]{:S(2)}) %all-to-all-start.3) | async-done | bytes 2097184 | tf_op jit(solution)/shard_map/all_to_all | solution.py:185
  255.8 4.9 %all-to-all-start.1 = ((bf16[16,2,4,64,128]{4,3,2,1,0:T(8,128)(2,1)}), bf16[16,2,4,64,128]{4,3,2,1,0:T(8,128)(2,1)}, u32[]{:S(2)}, u32[]{:S(2)}) async-start(bf16[16,2,4,64,128]{4,3,2,1,0:T(8,128)(2,1)} %bitcast.72), calls=%async_computation.1 | async-start | bytes 4194304 | tf_op jit(solution)/shard_map/all_to_all | solution.py:185
  260.7 3.2 %copy.24 = bf16[8,2,4,2,64,128]{5,4,3,2,1,0:T(8,128)(2,1)} copy(bf16[8,2,4,2,64,128]{5,4,2,1,3,0:T(8,128)(2,1)} %bitcast.36) | data formatting | bytes 4194304 | tf_op jit(solution)/shard_map/transpose | solution.py:188
  263.8 44.4 %all-to-all-done.1 = bf16[16,2,4,64,128]{4,3,2,1,0:T(8,128)(2,1)} async-done(((bf16[16,2,4,64,128]{4,3,2,1,0:T(8,128)(2,1)}), bf16[16,2,4,64,128]{4,3,2,1,0:T(8,128)(2,1)}, u32[]{:S(2)}, u32[]{:S(2)}) %all-to-all-start.1) | async-done | bytes 2097184 | tf_op jit(solution)/shard_map/all_to_all | solution.py:185
  310.1 2.3 fusion.37
  313.2 2.4 pad_maximum_fusion.3
  (45 shorter events, 7.8 us)
Async XLA Ops:
  0.0 0.8 copy-start
  9.4 34.1 %copy-start.2 = (bf16[32,512,256]{2,1,0:T(8,128)(2,1)}, bf16[32,512,256]{2,1,0:T(8,128)(2,1)S(1)}, u32[]{:S(2)}) copy-start(bf16[32,512,256]{2,1,0:T(8,128)(2,1)S(1)} %fusion.7) | copy-start | bytes 25165828
  9.4 21.6 %copy-start.6 = (f32[3,3,256]{2,1,0:T(4,128)S(1)}, f32[3,3,256]{2,1,0:T(4,128)}, u32[]{:S(2)}) copy-start(f32[3,3,256]{2,1,0:T(4,128)} %param.15) | copy-start | bytes 27652
  9.5 12.6 %collective-permute-start.1 = (bf16[1,512,256]{2,1,0:T(8,128)(2,1)S(1)}, bf16[1,512,256]{2,1,0:T(8,128)(2,1)S(1)}, u32[]{:S(2)}, u32[]{:S(2)}) collective-permute-start(bf16[1,512,256]{2,1,0:T(8,128)(2,1)S(1)} %get-tuple-element.10), channel_id=1, source_target_pairs={{2,0},{4,2},{6,4},{8,6},{10,8},{12,10},{14,12},{3,1},{5,3},{7,5},{... | collective-permute-start | bytes 786440 | tf_op jit(solution)/shard_map/ppermute | solution.py:19
  11.6 14.5 %collective-permute-start = (bf16[1,512,256]{2,1,0:T(8,128)(2,1)S(1)}, bf16[1,512,256]{2,1,0:T(8,128)(2,1)S(1)}, u32[]{:S(2)}, u32[]{:S(2)}) collective-permute-start(bf16[1,512,256]{2,1,0:T(8,128)(2,1)S(1)} %get-tuple-element.9), channel_id=1, source_target_pairs={{0,2},{2,4},{4,6},{6,8},{8,10},{10,12},{12,14},{1,3},{3,5},{5,7},{... | collective-permute-start | bytes 786440 | tf_op jit(solution)/shard_map/ppermute | solution.py:18
  26.1 4.9 %collective-permute-start.2 = (bf16[34,1,256]{2,1,0:T(2,128)(2,1)S(1)}, bf16[34,1,256]{2,1,0:T(2,128)(2,1)S(1)}, u32[]{:S(2)}, u32[]{:S(2)}) collective-permute-start(bf16[34,1,256]{2,1,0:T(2,128)(2,1)S(1)} %get-tuple-element.7), channel_id=1, source_target_pairs={{0,1},{2,3},{4,5},{6,7},{8,9},{10,11},{12,13},{14,15},{16,17},{18,... | collective-permute-start | bytes 52232 | tf_op jit(solution)/shard_map/ppermute | solution.py:18
  27.4 3.9 %collective-permute-start.3 = (bf16[34,1,256]{2,1,0:T(2,128)(2,1)S(1)}, bf16[34,1,256]{2,1,0:T(2,128)(2,1)S(1)}, u32[]{:S(2)}, u32[]{:S(2)}) collective-permute-start(bf16[34,1,256]{2,1,0:T(2,128)(2,1)S(1)} %get-tuple-element.8), channel_id=1, source_target_pairs={{1,0},{3,2},{5,4},{7,6},{9,8},{11,10},{13,12},{15,14},{17,16},{19,... | collective-permute-start | bytes 52232 | tf_op jit(solution)/shard_map/ppermute | solution.py:19
  31.0 12.4 %copy-start.10 = (bf16[256,128]{1,0:T(8,128)(2,1)S(1)}, bf16[256,128]{1,0:T(8,128)(2,1)}, u32[]{:S(2)}) copy-start(bf16[256,128]{1,0:T(8,128)(2,1)} %param.17) | copy-start | bytes 196612
  31.1 12.4 %copy-start.11 = (f32[256]{0:T(256)S(1)}, f32[256]{0:T(256)}, u32[]{:S(2)}) copy-start(f32[256]{0:T(256)} %param.16) | copy-start | bytes 3076
  31.1 12.4 %copy-start.12 = (f32[128]{0:T(128)S(1)}, f32[128]{0:T(128)}, u32[]{:S(2)}) copy-start(f32[128]{0:T(128)} %param.18) | copy-start | bytes 1540
  64.1 26.1 %copy-start.8 = (f32[128]{0:T(128)S(1)}, f32[128]{0:T(128)}, u32[]{:S(2)}) copy-start(f32[128]{0:T(128)} %param.20) | copy-start | bytes 1540
  64.2 26.1 %copy-start.9 = (f32[128]{0:T(128)S(1)}, f32[128]{0:T(128)}, u32[]{:S(2)}) copy-start(f32[128]{0:T(128)} %param.19) | copy-start | bytes 1540
  85.4 12.3 %copy-start.3 = (bf16[16,512,128]{2,1,0:T(8,128)(2,1)}, bf16[16,512,128]{2,1,0:T(8,128)(2,1)S(1)}, u32[]{:S(2)}) copy-start(bf16[16,512,128]{2,1,0:T(8,128)(2,1)S(1)} %get-tuple-element.23) | copy-start | bytes 6291460
  96.2 59.5 %copy-start.7 = (f32[4,225]{1,0:T(4,128)S(1)}, f32[4,225]{1,0:T(4,128)}, u32[]{:S(2)}) copy-start(f32[4,225]{1,0:T(4,128)} %param.22) | copy-start | bytes 10804
  97.7 52.7 %all-to-all-start.2 = ((bf16[16,2,4,64,128]{4,3,2,1,0:T(8,128)(2,1)}), bf16[16,2,4,64,128]{4,3,2,1,0:T(8,128)(2,1)}, u32[]{:S(2)}, u32[]{:S(2)}) async-start(bf16[16,2,4,64,128]{4,3,2,1,0:T(8,128)(2,1)} %bitcast.73), calls=%async_computation.2 | async-start | bytes 4194304 | tf_op jit(solution)/shard_map/all_to_all | solution.py:173
  150.5 52.6 %all-to-all-start = ((bf16[16,2,4,64,128]{4,3,2,1,0:T(8,128)(2,1)}), bf16[16,2,4,64,128]{4,3,2,1,0:T(8,128)(2,1)}, u32[]{:S(2)}, u32[]{:S(2)}) async-start(bf16[16,2,4,64,128]{4,3,2,1,0:T(8,128)(2,1)} %bitcast.70), calls=%async_computation | async-start | bytes 4194304 | tf_op jit(solution)/shard_map/all_to_all | solution.py:173
  203.1 52.7 %all-to-all-start.3 = ((bf16[16,2,4,64,128]{4,3,2,1,0:T(8,128)(2,1)}), bf16[16,2,4,64,128]{4,3,2,1,0:T(8,128)(2,1)}, u32[]{:S(2)}, u32[]{:S(2)}) async-start(bf16[16,2,4,64,128]{4,3,2,1,0:T(8,128)(2,1)} %bitcast.71), calls=%async_computation.3 | async-start | bytes 4194304 | tf_op jit(solution)/shard_map/all_to_all | solution.py:185
  229.0 81.1 %copy-start.5 = (bf16[128,128]{1,0:T(8,128)(2,1)S(1)}, bf16[128,128]{1,0:T(8,128)(2,1)}, u32[]{:S(2)}) copy-start(bf16[128,128]{1,0:T(8,128)(2,1)} %param.23) | copy-start | bytes 98308
  255.8 52.4 %all-to-all-start.1 = ((bf16[16,2,4,64,128]{4,3,2,1,0:T(8,128)(2,1)}), bf16[16,2,4,64,128]{4,3,2,1,0:T(8,128)(2,1)}, u32[]{:S(2)}, u32[]{:S(2)}) async-start(bf16[16,2,4,64,128]{4,3,2,1,0:T(8,128)(2,1)} %bitcast.72), calls=%async_computation.1 | async-start | bytes 4194304 | tf_op jit(solution)/shard_map/all_to_all | solution.py:185
  308.2 4.3 %copy-start.4 = (bf16[16,512,128]{2,1,0:T(8,128)(2,1)S(1)}, bf16[16,512,128]{2,1,0:T(8,128)(2,1)}, u32[]{:S(2)}) copy-start(bf16[16,512,128]{2,1,0:T(8,128)(2,1)} %copy-done.3) | copy-start | bytes 6291460
  310.1 5.4 %copy-start.1 = (bf16[128,256]{1,0:T(8,128)(2,1)S(1)}, bf16[128,256]{1,0:T(8,128)(2,1)}, u32[]{:S(2)}) copy-start(bf16[128,256]{1,0:T(8,128)(2,1)} %param.13) | copy-start | bytes 196612

commit v7 on v6

--- a/solution.py
+++ b/solution.py
@@ -170,6 +170,8 @@
         ).astype(jnp.bfloat16)
         normed = layer_norm(after_conv, norm_gain, norm_bias)
         pair = pieces_of(normed, row_size, col_size, pp, span, col_count, channels)
+        if piece + 1 < pieces:
+            pair, padded = lax.optimization_barrier((pair, padded))
         moved = lax.all_to_all(pair, ("row", "col"), 0, 0, tiled=True)
         grouped = (
             moved.reshape(G, sub, col_size, pp, across, inner_cols, channels)

time: 320 us -> 307 us (0.959)
  waiting for transfers between devices: 125 us -> 96 us
  other arithmetic: 26.1 us -> 38.6 us
  matrix products: 53.5 us -> 56.7 us
    all_to_all x2, waiting for transfers between devices: 48.3 us -> 20.7 us  [body(): moved = lax.all_to_all(pair, ('row', 'col'), 0, 0, tiled=True)]
    concatenate x1 -> x2, other arithmetic: 12.1 us -> 25.5 us  [with_halo(): array = jnp.concatenate([before, array, after], axis=dim)]
    ppermute x2, waiting for transfers between devices: 6.63 us -> 0.25 us  [with_halo(): after = lax.ppermute(initial, axis, down)]
    ppermute x2, waiting for transfers between devices: 4.06 us -> 9.38 us  [with_halo(): before = lax.ppermute(last, axis, up)]
    dot_general x2, matrix products: 41.9 us -> 45.2 us  [body(): jnp.dot(hidden, project_weight, preferred_element_type=jnp.float32)]
  transfers between devices with their start and end apart: 8 -> 8, of which waited for: 7 -> 6; matrix products, arithmetic and copies ran while one was open for 14% -> 24% of each run, Pallas kernels for 10% -> 11%
where the time goes in v7:
time: 307 us; the launch traced here: 303 us
  waiting for transfers between devices  96 us (31%)
  matrix products  56.7 us (18%)
  local copies, waits for them, and re-layouts  45.8 us (15%)
  other arithmetic  38.6 us (13%)
  starting transfers between devices  32.8 us (11%)
  Pallas kernels  32 us (10%)
    all_to_all x2, waiting for transfers between devices, body(): returned = lax.all_to_all(returned, ('row', 'col'), 0, 0, tiled=True)  65.7 us
    dot_general x2, matrix products, body(): jnp.dot(hidden, project_weight, preferred_element_type=jnp.float32)  45.2 us
    pallas_call x2, Pallas kernels, grid_attention(): pl.pallas_call(attention_kernel, grid=(count // block,), in_specs=[pl.Blo...  32 us
    concatenate x2, other arithmetic, with_halo(): array = jnp.concatenate([before, array, after], axis=dim)  25.5 us
    all_to_all x2, waiting for transfers between devices, body(): moved = lax.all_to_all(pair, ('row', 'col'), 0, 0, tiled=True)  20.7 us
    gather x2, local copies, waits for them, and re-layouts, grid_bias(): return jnp.take(position_bias, offset_index, axis=1)  16.5 us
    all_to_all x2, starting transfers between devices, body(): moved = lax.all_to_all(pair, ('row', 'col'), 0, 0, tiled=True)  12.1 us
    transpose x2, local copies, waits for them, and re-layouts, body(): returned = heads_out.reshape(sub, pp, inner_cols, G, col_size, across, ch...  10.7 us
  transfers between devices with their start and end apart: 8, of which 6 were waited for; matrix products, arithmetic and copies ran while one was open for 24% of the time, Pallas kernels for 11%

profile of v7, /device:TPU:13, one launch (start us, length us, event | category | flops | bytes accessed | tf_op | source)
XLA Modules:
  0.0 302.6 jit_solution(13952131747086870654)
XLA Ops:
  0.8 8.5 %fusion.7 = bf16[32,512,256]{2,1,0:T(8,128)(2,1)S(1)} fusion(bf16[32,512,128]{2,1,0:T(8,128)(2,1)} %param.12, f32[256]{0:T(256)} %param.14, bf16[128,256]{1,0:T(8,128)(2,1)S(1)} %copy-done), kind=kOutput, calls=%fused_computation.9 | convolution fusion | flops 1115684864 | bytes 12649472 | tf_op jit(solution)/shard_map/dot_general | solution.py:30
  9.5 3.2 %collective-permute-start = (bf16[1,512,256]{2,1,0:T(8,128)(2,1)S(1)}, bf16[1,512,256]{2,1,0:T(8,128)(2,1)S(1)}, u32[]{:S(2)}, u32[]{:S(2)}) collective-permute-start(bf16[1,512,256]{2,1,0:T(8,128)(2,1)S(1)} %get-tuple-element.13), channel_id=1, source_target_pairs={{0,2},{2,4},{4,6},{6,8},{8,10},{10,12},{12,14},{1,3},{3,5},{5,7},{... | collective-permute-start | bytes 786440 | tf_op jit(solution)/shard_map/ppermute | solution.py:18
  12.6 2.1 collective-permute-start.1
  14.7 9.4 %collective-permute-done = bf16[1,512,256]{2,1,0:T(8,128)(2,1)S(1)} collective-permute-done((bf16[1,512,256]{2,1,0:T(8,128)(2,1)S(1)}, bf16[1,512,256]{2,1,0:T(8,128)(2,1)S(1)}, u32[]{:S(2)}, u32[]{:S(2)}) %collective-permute-start) | collective-permute-done | bytes 262176 | tf_op jit(solution)/shard_map/ppermute | solution.py:18
  25.5 4.0 %collective-permute-start.3 = (bf16[34,1,256]{2,1,0:T(2,128)(2,1)S(1)}, bf16[34,1,256]{2,1,0:T(2,128)(2,1)S(1)}, u32[]{:S(2)}, u32[]{:S(2)}) collective-permute-start(bf16[34,1,256]{2,1,0:T(2,128)(2,1)S(1)} %get-tuple-element.12), channel_id=1, source_target_pairs={{1,0},{3,2},{5,4},{7,6},{9,8},{11,10},{13,12},{15,14},{17,16},{19,... | collective-permute-start | bytes 52232 | tf_op jit(solution)/shard_map/ppermute | solution.py:19
  29.8 12.1 %maximum_maximum_fusion = (bf16[34,513,256]{2,1,0:T(8,128)(2,1)}, bf16[34,513,256]{2,1,0:T(8,128)(2,1)}) fusion(bf16[1,512,256]{2,1,0:T(8,128)(2,1)S(1)} %collective-permute-done.1, bf16[32,512,256]{2,1,0:T(8,128)(2,1)S(1)} %fusion.7, bf16[1,512,256]{2,1,0:T(8,128)(2,1)S(1)} %collective-permute-done, bf16[34,1,256]{2,1,0:T(2,128)(2,1)S(1)} %collective-permute-done.2, ...), kind=kLoop, calls=%fused_computation.12 | loop fusion | flops 71442432 | bytes 26808320 | tf_op jit(solution)/shard_map/concatenate | solution.py:20
  41.9 21.1 %convert_reduce_fusion.1 = (f32[16,512]{1,0:T(8,128)S(1)}, bf16[16,512,128]{2,1,0:T(8,128)(2,1)S(1)}) fusion(f32[128]{0:T(128)S(1)} %copy-done.12, bf16[256,128]{1,0:T(8,128)(2,1)S(1)} %copy-done.10, bf16[34,513,256]{2,1,0:T(8,128)(2,1)} %get-tuple-element.10, bf16[32,512,256]{2,1,0:T(8,128)(2,1)} %copy-done.2, bf16[34,513,256]{2,1,0:T(8,128)(2,1)} %get-tuple-element.9, ...), kind=kOutput, calls=%fused_computation.36 | convolution fusion | flops 620748800 | bytes 46508544 | tf_op jit(solution)/shard_map/dot_general | solution.py:168
  63.0 2.4 fusion.32
  65.4 2.5 fusion.35
  69.5 13.5 %pad_maximum_fusion.1 = bf16[34,514,256]{2,1,0:T(8,128)(2,1)} fusion(bf16[34,1,256]{2,1,0:T(2,128)(2,1)S(1)} %collective-permute-done.3, bf16[1,512,256]{2,1,0:T(8,128)(2,1)S(1)} %collective-permute-done.1, bf16[32,512,256]{2,1,0:T(8,128)(2,1)} %copy-done.2, bf16[1,512,256]{2,1,0:T(8,128)(2,1)S(1)} %collective-permute-done, ...), kind=kLoop, calls=%fused_computation.14 | loop fusion | flops 44738560 | bytes 17895424 | tf_op jit(solution)/shard_map/concatenate | solution.py:20
  83.0 6.8 %all-to-all-start = ((bf16[16,2,4,64,128]{4,3,2,1,0:T(8,128)(2,1)}), bf16[16,2,4,64,128]{4,3,2,1,0:T(8,128)(2,1)}, u32[]{:S(2)}, u32[]{:S(2)}) async-start(bf16[16,2,4,64,128]{4,3,2,1,0:T(8,128)(2,1)} %bitcast.71), calls=%async_computation | async-start | bytes 4194304 | tf_op jit(solution)/shard_map/all_to_all | solution.py:175
  89.8 24.1 %convert_reduce_fusion = (f32[16,512]{1,0:T(8,128)S(1)}, bf16[16,512,128]{2,1,0:T(8,128)(2,1)S(1)}) fusion(f32[128]{0:T(128)S(1)} %copy-done.12, bf16[256,128]{1,0:T(8,128)(2,1)S(1)} %copy-done.10, bf16[34,514,256]{2,1,0:T(8,128)(2,1)} %pad_maximum_fusion.1, f32[256]{0:T(256)S(1)} %bitcast.94, f32[256]{0:T(256)S(1)} %bitcast.96, f32[256]{0:T(256)S(1)} %bitcast.82, ...), kind=kOutput, calls=%fused_computation.33 | convolution fusion | flops 618651648 | bytes 42052096 | tf_op jit(solution)/shard_map/dot_general | solution.py:168
  113.9 2.4 fusion.28
  116.4 2.5 fusion.31
  120.4 17.0 %all-to-all-done = bf16[16,2,4,64,128]{4,3,2,1,0:T(8,128)(2,1)} async-done(((bf16[16,2,4,64,128]{4,3,2,1,0:T(8,128)(2,1)}), bf16[16,2,4,64,128]{4,3,2,1,0:T(8,128)(2,1)}, u32[]{:S(2)}, u32[]{:S(2)}) %all-to-all-start) | async-done | bytes 2097184 | tf_op jit(solution)/shard_map/all_to_all | solution.py:175
  137.3 5.3 %all-to-all-start.2 = ((bf16[16,2,4,64,128]{4,3,2,1,0:T(8,128)(2,1)}), bf16[16,2,4,64,128]{4,3,2,1,0:T(8,128)(2,1)}, u32[]{:S(2)}, u32[]{:S(2)}) async-start(bf16[16,2,4,64,128]{4,3,2,1,0:T(8,128)(2,1)} %bitcast.70), calls=%async_computation.2 | async-start | bytes 4194304 | tf_op jit(solution)/shard_map/all_to_all | solution.py:175
  142.9 14.2 %gather_fusion = f32[4096,4]{1,0:T(8,128)} fusion(f32[4,225]{0,1:T(8,128)S(1)} %copy.17, s32[4096]{0:T(1024)S(1)} %broadcast_clamp_fusion), kind=kCustom, calls=%fused_computation | custom fusion | bytes 147456 | tf_op jit(solution)/shard_map/jit(_take)/gather | solution.py:62
  157.2 2.3 copy.25
  160.2 4.6 %copy.16 = bf16[8,1,2,2,4,64,128]{6,4,2,0,5,3,1:T(4,128)(2,1)} copy(bf16[8,1,2,2,4,64,128]{6,5,4,3,2,0,1:T(8,128)(2,1)} %bitcast.14) | data formatting | bytes 4194304 | tf_op jit(solution)/shard_map/reshape | solution.py:177
  164.8 16.0 %shard_map.118 = bf16[128,64,128]{2,1,0:T(8,128)(2,1)} custom-call(bf16[128,64,128]{2,1,0:T(8,128)(2,1)} %bitcast.76, bf16[128,384]{1,0:T(8,128)(2,1)} %w_ref.3, f32[4,64,64]{2,1,0:T(8,128)} %select_bitcast_fusion.bias_ref), custom_call_target="tpu_custom_call" | custom-call | tf_op jit(solution)/shard_map/pallas_call | solution.py:112
  180.8 5.4 %copy.19 = bf16[8,1,2,2,4,64,128]{6,5,4,3,2,0,1:T(8,128)(2,1)} copy(bf16[8,1,2,2,4,64,128]{6,4,2,0,5,3,1:T(4,128)(2,1)} %bitcast.77) | data formatting | bytes 4194304 | tf_op jit(solution)/shard_map/transpose | solution.py:184
  186.2 3.7 %all-to-all-done.2 = bf16[16,2,4,64,128]{4,3,2,1,0:T(8,128)(2,1)} async-done(((bf16[16,2,4,64,128]{4,3,2,1,0:T(8,128)(2,1)}), bf16[16,2,4,64,128]{4,3,2,1,0:T(8,128)(2,1)}, u32[]{:S(2)}, u32[]{:S(2)}) %all-to-all-start.2) | async-done | bytes 2097184 | tf_op jit(solution)/shard_map/all_to_all | solution.py:175
  189.9 5.3 %all-to-all-start.1 = ((bf16[16,2,4,64,128]{4,3,2,1,0:T(8,128)(2,1)}), bf16[16,2,4,64,128]{4,3,2,1,0:T(8,128)(2,1)}, u32[]{:S(2)}, u32[]{:S(2)}) async-start(bf16[16,2,4,64,128]{4,3,2,1,0:T(8,128)(2,1)} %bitcast.72), calls=%async_computation.1 | async-start | bytes 4194304 | tf_op jit(solution)/shard_map/all_to_all | solution.py:187
  195.3 4.6 %copy.22 = bf16[8,1,2,2,4,64,128]{6,4,2,0,5,3,1:T(4,128)(2,1)} copy(bf16[8,1,2,2,4,64,128]{6,5,4,3,2,0,1:T(8,128)(2,1)} %bitcast.29) | data formatting | bytes 4194304 | tf_op jit(solution)/shard_map/reshape | solution.py:177
  199.9 16.0 %shard_map.119 = bf16[128,64,128]{2,1,0:T(8,128)(2,1)} custom-call(bf16[128,64,128]{2,1,0:T(8,128)(2,1)} %bitcast.74, bf16[128,384]{1,0:T(8,128)(2,1)} %w_ref.3, f32[4,64,64]{2,1,0:T(8,128)} %select_bitcast_fusion.bias_ref), custom_call_target="tpu_custom_call" | custom-call | tf_op jit(solution)/shard_map/pallas_call | solution.py:112
  215.8 5.4 %copy.23 = bf16[8,1,2,2,4,64,128]{6,5,4,3,2,0,1:T(8,128)(2,1)} copy(bf16[8,1,2,2,4,64,128]{6,4,2,0,5,3,1:T(4,128)(2,1)} %bitcast.75) | data formatting | bytes 4194304 | tf_op jit(solution)/shard_map/transpose | solution.py:184
  221.2 21.4 %all-to-all-done.1 = bf16[16,2,4,64,128]{4,3,2,1,0:T(8,128)(2,1)} async-done(((bf16[16,2,4,64,128]{4,3,2,1,0:T(8,128)(2,1)}), bf16[16,2,4,64,128]{4,3,2,1,0:T(8,128)(2,1)}, u32[]{:S(2)}, u32[]{:S(2)}) %all-to-all-start.1) | async-done | bytes 2097184 | tf_op jit(solution)/shard_map/all_to_all | solution.py:187
  242.6 4.9 %all-to-all-start.3 = ((bf16[16,2,4,64,128]{4,3,2,1,0:T(8,128)(2,1)}), bf16[16,2,4,64,128]{4,3,2,1,0:T(8,128)(2,1)}, u32[]{:S(2)}, u32[]{:S(2)}) async-start(bf16[16,2,4,64,128]{4,3,2,1,0:T(8,128)(2,1)} %bitcast.73), calls=%async_computation.3 | async-start | bytes 4194304 | tf_op jit(solution)/shard_map/all_to_all | solution.py:187
  247.5 3.2 %copy.20 = bf16[8,2,4,2,64,128]{5,4,3,2,1,0:T(8,128)(2,1)} copy(bf16[8,2,4,2,64,128]{5,4,2,1,3,0:T(8,128)(2,1)} %bitcast.23) | data formatting | bytes 4194304 | tf_op jit(solution)/shard_map/transpose | solution.py:190
  250.7 44.3 %all-to-all-done.3 = bf16[16,2,4,64,128]{4,3,2,1,0:T(8,128)(2,1)} async-done(((bf16[16,2,4,64,128]{4,3,2,1,0:T(8,128)(2,1)}), bf16[16,2,4,64,128]{4,3,2,1,0:T(8,128)(2,1)}, u32[]{:S(2)}, u32[]{:S(2)}) %all-to-all-start.3) | async-done | bytes 2097184 | tf_op jit(solution)/shard_map/all_to_all | solution.py:187
  297.0 2.3 fusion.36
  300.0 2.4 pad_maximum_fusion.3
  (48 shorter events, 9.3 us)
Async XLA Ops:
  0.0 0.8 copy-start
  9.4 32.5 %copy-start.2 = (bf16[32,512,256]{2,1,0:T(8,128)(2,1)}, bf16[32,512,256]{2,1,0:T(8,128)(2,1)S(1)}, u32[]{:S(2)}) copy-start(bf16[32,512,256]{2,1,0:T(8,128)(2,1)S(1)} %fusion.7) | copy-start | bytes 25165828
  9.4 20.1 %copy-start.6 = (f32[3,3,256]{2,1,0:T(4,128)S(1)}, f32[3,3,256]{2,1,0:T(4,128)}, u32[]{:S(2)}) copy-start(f32[3,3,256]{2,1,0:T(4,128)} %param.15) | copy-start | bytes 27652
  9.5 14.7 %collective-permute-start = (bf16[1,512,256]{2,1,0:T(8,128)(2,1)S(1)}, bf16[1,512,256]{2,1,0:T(8,128)(2,1)S(1)}, u32[]{:S(2)}, u32[]{:S(2)}) collective-permute-start(bf16[1,512,256]{2,1,0:T(8,128)(2,1)S(1)} %get-tuple-element.13), channel_id=1, source_target_pairs={{0,2},{2,4},{4,6},{6,8},{8,10},{10,12},{12,14},{1,3},{3,5},{5,7},{... | collective-permute-start | bytes 786440 | tf_op jit(solution)/shard_map/ppermute | solution.py:18
  12.6 11.5 %collective-permute-start.1 = (bf16[1,512,256]{2,1,0:T(8,128)(2,1)S(1)}, bf16[1,512,256]{2,1,0:T(8,128)(2,1)S(1)}, u32[]{:S(2)}, u32[]{:S(2)}) collective-permute-start(bf16[1,512,256]{2,1,0:T(8,128)(2,1)S(1)} %get-tuple-element.14), channel_id=1, source_target_pairs={{2,0},{4,2},{6,4},{8,6},{10,8},{12,10},{14,12},{3,1},{5,3},{7,5},{... | collective-permute-start | bytes 786440 | tf_op jit(solution)/shard_map/ppermute | solution.py:19
  24.2 5.4 %collective-permute-start.2 = (bf16[34,1,256]{2,1,0:T(2,128)(2,1)S(1)}, bf16[34,1,256]{2,1,0:T(2,128)(2,1)S(1)}, u32[]{:S(2)}, u32[]{:S(2)}) collective-permute-start(bf16[34,1,256]{2,1,0:T(2,128)(2,1)S(1)} %get-tuple-element.11), channel_id=1, source_target_pairs={{0,1},{2,3},{4,5},{6,7},{8,9},{10,11},{12,13},{14,15},{16,17},{18,... | collective-permute-start | bytes 52232 | tf_op jit(solution)/shard_map/ppermute | solution.py:18
  25.5 4.3 %collective-permute-start.3 = (bf16[34,1,256]{2,1,0:T(2,128)(2,1)S(1)}, bf16[34,1,256]{2,1,0:T(2,128)(2,1)S(1)}, u32[]{:S(2)}, u32[]{:S(2)}) collective-permute-start(bf16[34,1,256]{2,1,0:T(2,128)(2,1)S(1)} %get-tuple-element.12), channel_id=1, source_target_pairs={{1,0},{3,2},{5,4},{7,6},{9,8},{11,10},{13,12},{15,14},{17,16},{19,... | collective-permute-start | bytes 52232 | tf_op jit(solution)/shard_map/ppermute | solution.py:19
  29.5 12.3 %copy-start.10 = (bf16[256,128]{1,0:T(8,128)(2,1)S(1)}, bf16[256,128]{1,0:T(8,128)(2,1)}, u32[]{:S(2)}) copy-start(bf16[256,128]{1,0:T(8,128)(2,1)} %param.17) | copy-start | bytes 196612
  29.5 12.3 %copy-start.11 = (f32[256]{0:T(256)S(1)}, f32[256]{0:T(256)}, u32[]{:S(2)}) copy-start(f32[256]{0:T(256)} %param.16) | copy-start | bytes 3076
  29.5 12.3 %copy-start.12 = (f32[128]{0:T(128)S(1)}, f32[128]{0:T(128)}, u32[]{:S(2)}) copy-start(f32[128]{0:T(128)} %param.18) | copy-start | bytes 1540
  41.9 23.5 %copy-start.8 = (f32[128]{0:T(128)S(1)}, f32[128]{0:T(128)}, u32[]{:S(2)}) copy-start(f32[128]{0:T(128)} %param.20) | copy-start | bytes 1540
  41.9 23.5 %copy-start.9 = (f32[128]{0:T(128)S(1)}, f32[128]{0:T(128)}, u32[]{:S(2)}) copy-start(f32[128]{0:T(128)} %param.19) | copy-start | bytes 1540
  83.0 54.3 %all-to-all-start = ((bf16[16,2,4,64,128]{4,3,2,1,0:T(8,128)(2,1)}), bf16[16,2,4,64,128]{4,3,2,1,0:T(8,128)(2,1)}, u32[]{:S(2)}, u32[]{:S(2)}) async-start(bf16[16,2,4,64,128]{4,3,2,1,0:T(8,128)(2,1)} %bitcast.71), calls=%async_computation | async-start | bytes 4194304 | tf_op jit(solution)/shard_map/all_to_all | solution.py:175
  113.9 2.5 copy-start.3
  113.9 28.9 %copy-start.7 = (f32[4,225]{1,0:T(4,128)S(1)}, f32[4,225]{1,0:T(4,128)}, u32[]{:S(2)}) copy-start(f32[4,225]{1,0:T(4,128)} %param.22) | copy-start | bytes 10804
  137.3 52.6 %all-to-all-start.2 = ((bf16[16,2,4,64,128]{4,3,2,1,0:T(8,128)(2,1)}), bf16[16,2,4,64,128]{4,3,2,1,0:T(8,128)(2,1)}, u32[]{:S(2)}, u32[]{:S(2)}) async-start(bf16[16,2,4,64,128]{4,3,2,1,0:T(8,128)(2,1)} %bitcast.70), calls=%async_computation.2 | async-start | bytes 4194304 | tf_op jit(solution)/shard_map/all_to_all | solution.py:175
  189.9 52.7 %all-to-all-start.1 = ((bf16[16,2,4,64,128]{4,3,2,1,0:T(8,128)(2,1)}), bf16[16,2,4,64,128]{4,3,2,1,0:T(8,128)(2,1)}, u32[]{:S(2)}, u32[]{:S(2)}) async-start(bf16[16,2,4,64,128]{4,3,2,1,0:T(8,128)(2,1)} %bitcast.72), calls=%async_computation.1 | async-start | bytes 4194304 | tf_op jit(solution)/shard_map/all_to_all | solution.py:187
  215.8 81.1 %copy-start.5 = (bf16[128,128]{1,0:T(8,128)(2,1)S(1)}, bf16[128,128]{1,0:T(8,128)(2,1)}, u32[]{:S(2)}) copy-start(bf16[128,128]{1,0:T(8,128)(2,1)} %param.23) | copy-start | bytes 98308
  242.6 52.4 %all-to-all-start.3 = ((bf16[16,2,4,64,128]{4,3,2,1,0:T(8,128)(2,1)}), bf16[16,2,4,64,128]{4,3,2,1,0:T(8,128)(2,1)}, u32[]{:S(2)}, u32[]{:S(2)}) async-start(bf16[16,2,4,64,128]{4,3,2,1,0:T(8,128)(2,1)} %bitcast.73), calls=%async_computation.3 | async-start | bytes 4194304 | tf_op jit(solution)/shard_map/all_to_all | solution.py:187
  295.0 4.3 %copy-start.4 = (bf16[16,512,128]{2,1,0:T(8,128)(2,1)S(1)}, bf16[16,512,128]{2,1,0:T(8,128)(2,1)}, u32[]{:S(2)}) copy-start(bf16[16,512,128]{2,1,0:T(8,128)(2,1)} %copy-done.3) | copy-start | bytes 6291460
  297.0 5.4 %copy-start.1 = (bf16[128,256]{1,0:T(8,128)(2,1)S(1)}, bf16[128,256]{1,0:T(8,128)(2,1)}, u32[]{:S(2)}) copy-start(bf16[128,256]{1,0:T(8,128)(2,1)} %param.13) | copy-start | bytes 196612

commit v8 on v7

--- a/solution.py
+++ b/solution.py
@@ -159,10 +159,11 @@
     sub = row_size // G
     pp = span // row_size
     inner_cols = stride // col_size
+    windows = [padded[piece * span : piece * span + span + 2] for piece in range(pieces)]
     outs = []
     for piece in range(pieces):
         first = piece * span
-        hidden = depthwise(padded[first : first + span + 2], depth_weight, depth_bias, span, col_count)
+        hidden = depthwise(windows[piece], depth_weight, depth_bias, span, col_count)
         after_conv = (
             sky_map[first : first + span].astype(jnp.float32)
             + jnp.dot(hidden, project_weight, preferred_element_type=jnp.float32)
@@ -171,7 +172,7 @@
         normed = layer_norm(after_conv, norm_gain, norm_bias)
         pair = pieces_of(normed, row_size, col_size, pp, span, col_count, channels)
         if piece + 1 < pieces:
-            pair, padded = lax.optimization_barrier((pair, padded))
+            pair, windows[piece + 1] = lax.optimization_barrier((pair, windows[piece + 1]))
         moved = lax.all_to_all(pair, ("row", "col"), 0, 0, tiled=True)
         grouped = (
             moved.reshape(G, sub, col_size, pp, across, inner_cols, channels)

time: 307 us -> 300 us (0.977)
  other arithmetic: 38.6 us -> 32.2 us
    concatenate x2, other arithmetic: 25.5 us -> 19.1 us  [with_halo(): array = jnp.concatenate([before, array, after], axis=dim)]
where the time goes in v8:
time: 300 us; the launch traced here: 296 us
  waiting for transfers between devices  95.9 us (32%)
  matrix products  56.8 us (19%)
  local copies, waits for them, and re-layouts  45.8 us (15%)
  starting transfers between devices  32.8 us (11%)
  other arithmetic  32.2 us (11%)
  Pallas kernels  32 us (11%)
    all_to_all x2, waiting for transfers between devices, body(): returned = lax.all_to_all(returned, ('row', 'col'), 0, 0, tiled=True)  65.7 us
    dot_general x2, matrix products, body(): jnp.dot(hidden, project_weight, preferred_element_type=jnp.float32)  45.3 us
    pallas_call x2, Pallas kernels, grid_attention(): pl.pallas_call(attention_kernel, grid=(count // block,), in_specs=[pl.Blo...  32 us
    all_to_all x2, waiting for transfers between devices, body(): moved = lax.all_to_all(pair, ('row', 'col'), 0, 0, tiled=True)  20.6 us
    concatenate x2, other arithmetic, with_halo(): array = jnp.concatenate([before, array, after], axis=dim)  19.1 us
    gather x2, local copies, waits for them, and re-layouts, grid_bias(): return jnp.take(position_bias, offset_index, axis=1)  16.5 us
    all_to_all x2, starting transfers between devices, body(): moved = lax.all_to_all(pair, ('row', 'col'), 0, 0, tiled=True)  12.1 us
    transpose x2, local copies, waits for them, and re-layouts, body(): returned = heads_out.reshape(sub, pp, inner_cols, G, col_size, across, ch...  10.7 us
  transfers between devices with their start and end apart: 8, of which 6 were waited for; matrix products, arithmetic and copies ran while one was open for 24% of the time, Pallas kernels for 11%

profile of v8, /device:TPU:13, one launch (start us, length us, event | category | flops | bytes accessed | tf_op | source)
XLA Modules:
  0.0 296.2 jit_solution(1453516083780382864)
XLA Ops:
  0.8 8.5 %fusion.7 = bf16[32,512,256]{2,1,0:T(8,128)(2,1)S(1)} fusion(bf16[32,512,128]{2,1,0:T(8,128)(2,1)} %param.12, f32[256]{0:T(256)} %param.14, bf16[128,256]{1,0:T(8,128)(2,1)S(1)} %copy-done), kind=kOutput, calls=%fused_computation.9 | convolution fusion | flops 1115684864 | bytes 12649472 | tf_op jit(solution)/shard_map/dot_general | solution.py:30
  9.5 3.2 %collective-permute-start = (bf16[1,512,256]{2,1,0:T(8,128)(2,1)S(1)}, bf16[1,512,256]{2,1,0:T(8,128)(2,1)S(1)}, u32[]{:S(2)}, u32[]{:S(2)}) collective-permute-start(bf16[1,512,256]{2,1,0:T(8,128)(2,1)S(1)} %get-tuple-element.13), channel_id=1, source_target_pairs={{0,2},{2,4},{4,6},{6,8},{8,10},{10,12},{12,14},{1,3},{3,5},{5,7},{... | collective-permute-start | bytes 786440 | tf_op jit(solution)/shard_map/ppermute | solution.py:18
  12.6 2.1 collective-permute-start.1
  14.7 9.4 %collective-permute-done = bf16[1,512,256]{2,1,0:T(8,128)(2,1)S(1)} collective-permute-done((bf16[1,512,256]{2,1,0:T(8,128)(2,1)S(1)}, bf16[1,512,256]{2,1,0:T(8,128)(2,1)S(1)}, u32[]{:S(2)}, u32[]{:S(2)}) %collective-permute-start) | collective-permute-done | bytes 262176 | tf_op jit(solution)/shard_map/ppermute | solution.py:18
  25.5 4.0 %collective-permute-start.3 = (bf16[34,1,256]{2,1,0:T(2,128)(2,1)S(1)}, bf16[34,1,256]{2,1,0:T(2,128)(2,1)S(1)}, u32[]{:S(2)}, u32[]{:S(2)}) collective-permute-start(bf16[34,1,256]{2,1,0:T(2,128)(2,1)S(1)} %get-tuple-element.12), channel_id=1, source_target_pairs={{1,0},{3,2},{5,4},{7,6},{9,8},{11,10},{13,12},{15,14},{17,16},{19,... | collective-permute-start | bytes 52232 | tf_op jit(solution)/shard_map/ppermute | solution.py:19
  29.8 12.1 %maximum_maximum_fusion = (bf16[34,513,256]{2,1,0:T(8,128)(2,1)}, bf16[34,513,256]{2,1,0:T(8,128)(2,1)}) fusion(bf16[1,512,256]{2,1,0:T(8,128)(2,1)S(1)} %collective-permute-done.1, bf16[32,512,256]{2,1,0:T(8,128)(2,1)S(1)} %fusion.7, bf16[1,512,256]{2,1,0:T(8,128)(2,1)S(1)} %collective-permute-done, bf16[34,1,256]{2,1,0:T(2,128)(2,1)S(1)} %collective-permute-done.2, ...), kind=kLoop, calls=%fused_computation.12 | loop fusion | flops 71442432 | bytes 26808320 | tf_op jit(solution)/shard_map/concatenate | solution.py:20
  41.9 21.1 %convert_reduce_fusion.1 = (f32[16,512]{1,0:T(8,128)S(1)}, bf16[16,512,128]{2,1,0:T(8,128)(2,1)S(1)}) fusion(f32[128]{0:T(128)S(1)} %copy-done.12, bf16[256,128]{1,0:T(8,128)(2,1)S(1)} %copy-done.10, bf16[34,513,256]{2,1,0:T(8,128)(2,1)} %get-tuple-element.10, bf16[32,512,256]{2,1,0:T(8,128)(2,1)} %copy-done.2, bf16[34,513,256]{2,1,0:T(8,128)(2,1)} %get-tuple-element.9, ...), kind=kOutput, calls=%fused_computation.35 | convolution fusion | flops 620748800 | bytes 46508544 | tf_op jit(solution)/shard_map/dot_general | solution.py:169
  63.0 2.4 fusion.32
  65.4 2.5 fusion.35
  69.5 7.0 %pad_maximum_fusion.1 = bf16[18,514,256]{2,1,0:T(8,128)(2,1)} fusion(bf16[34,1,256]{2,1,0:T(2,128)(2,1)S(1)} %collective-permute-done.3, bf16[34,1,256]{2,1,0:T(2,128)(2,1)S(1)} %collective-permute-done.2, bf16[1,512,256]{2,1,0:T(8,128)(2,1)S(1)} %collective-permute-done.1, bf16[32,512,256]{2,1,0:T(8,128)(2,1)} %copy-done.2, ...), kind=kLoop, calls=%fused_computation.40 | loop fusion | flops 23685120 | bytes 13684736 | tf_op jit(solution)/shard_map/concatenate | solution.py:20
  76.5 6.8 %all-to-all-start = ((bf16[16,2,4,64,128]{4,3,2,1,0:T(8,128)(2,1)}), bf16[16,2,4,64,128]{4,3,2,1,0:T(8,128)(2,1)}, u32[]{:S(2)}, u32[]{:S(2)}) async-start(bf16[16,2,4,64,128]{4,3,2,1,0:T(8,128)(2,1)} %bitcast.71), calls=%async_computation | async-start | bytes 4194304 | tf_op jit(solution)/shard_map/all_to_all | solution.py:176
  83.3 24.2 %convert_reduce_fusion = (f32[16,512]{1,0:T(8,128)S(1)}, bf16[16,512,128]{2,1,0:T(8,128)(2,1)S(1)}) fusion(f32[128]{0:T(128)S(1)} %copy-done.12, bf16[256,128]{1,0:T(8,128)(2,1)S(1)} %copy-done.10, bf16[18,514,256]{2,1,0:T(8,128)(2,1)} %pad_maximum_fusion.1, f32[256]{0:T(256)S(1)} %bitcast.94, f32[256]{0:T(256)S(1)} %bitcast.96, f32[256]{0:T(256)S(1)} %bitcast.82, ...), kind=kOutput, calls=%fused_computation.32 | convolution fusion | flops 618651648 | bytes 42052096 | tf_op jit(solution)/shard_map/dot_general | solution.py:169
  107.6 2.4 fusion.28
  110.0 2.5 fusion.31
  114.0 16.8 %all-to-all-done = bf16[16,2,4,64,128]{4,3,2,1,0:T(8,128)(2,1)} async-done(((bf16[16,2,4,64,128]{4,3,2,1,0:T(8,128)(2,1)}), bf16[16,2,4,64,128]{4,3,2,1,0:T(8,128)(2,1)}, u32[]{:S(2)}, u32[]{:S(2)}) %all-to-all-start) | async-done | bytes 2097184 | tf_op jit(solution)/shard_map/all_to_all | solution.py:176
  130.8 5.3 %all-to-all-start.2 = ((bf16[16,2,4,64,128]{4,3,2,1,0:T(8,128)(2,1)}), bf16[16,2,4,64,128]{4,3,2,1,0:T(8,128)(2,1)}, u32[]{:S(2)}, u32[]{:S(2)}) async-start(bf16[16,2,4,64,128]{4,3,2,1,0:T(8,128)(2,1)} %bitcast.70), calls=%async_computation.2 | async-start | bytes 4194304 | tf_op jit(solution)/shard_map/all_to_all | solution.py:176
  136.5 14.2 %gather_fusion = f32[4096,4]{1,0:T(8,128)} fusion(f32[4,225]{0,1:T(8,128)S(1)} %copy.17, s32[4096]{0:T(1024)S(1)} %broadcast_clamp_fusion), kind=kCustom, calls=%fused_computation | custom fusion | bytes 147456 | tf_op jit(solution)/shard_map/jit(_take)/gather | solution.py:62
  150.7 2.3 copy.25
  153.8 4.6 %copy.16 = bf16[8,1,2,2,4,64,128]{6,4,2,0,5,3,1:T(4,128)(2,1)} copy(bf16[8,1,2,2,4,64,128]{6,5,4,3,2,0,1:T(8,128)(2,1)} %bitcast.14) | data formatting | bytes 4194304 | tf_op jit(solution)/shard_map/reshape | solution.py:178
  158.4 16.0 %shard_map.118 = bf16[128,64,128]{2,1,0:T(8,128)(2,1)} custom-call(bf16[128,64,128]{2,1,0:T(8,128)(2,1)} %bitcast.76, bf16[128,384]{1,0:T(8,128)(2,1)} %w_ref.3, f32[4,64,64]{2,1,0:T(8,128)} %select_bitcast_fusion.bias_ref), custom_call_target="tpu_custom_call" | custom-call | tf_op jit(solution)/shard_map/pallas_call | solution.py:112
  174.4 5.4 %copy.19 = bf16[8,1,2,2,4,64,128]{6,5,4,3,2,0,1:T(8,128)(2,1)} copy(bf16[8,1,2,2,4,64,128]{6,4,2,0,5,3,1:T(4,128)(2,1)} %bitcast.77) | data formatting | bytes 4194304 | tf_op jit(solution)/shard_map/transpose | solution.py:185
  179.8 3.7 %all-to-all-done.2 = bf16[16,2,4,64,128]{4,3,2,1,0:T(8,128)(2,1)} async-done(((bf16[16,2,4,64,128]{4,3,2,1,0:T(8,128)(2,1)}), bf16[16,2,4,64,128]{4,3,2,1,0:T(8,128)(2,1)}, u32[]{:S(2)}, u32[]{:S(2)}) %all-to-all-start.2) | async-done | bytes 2097184 | tf_op jit(solution)/shard_map/all_to_all | solution.py:176
  183.5 5.3 %all-to-all-start.1 = ((bf16[16,2,4,64,128]{4,3,2,1,0:T(8,128)(2,1)}), bf16[16,2,4,64,128]{4,3,2,1,0:T(8,128)(2,1)}, u32[]{:S(2)}, u32[]{:S(2)}) async-start(bf16[16,2,4,64,128]{4,3,2,1,0:T(8,128)(2,1)} %bitcast.72), calls=%async_computation.1 | async-start | bytes 4194304 | tf_op jit(solution)/shard_map/all_to_all | solution.py:188
  188.8 4.6 %copy.22 = bf16[8,1,2,2,4,64,128]{6,4,2,0,5,3,1:T(4,128)(2,1)} copy(bf16[8,1,2,2,4,64,128]{6,5,4,3,2,0,1:T(8,128)(2,1)} %bitcast.29) | data formatting | bytes 4194304 | tf_op jit(solution)/shard_map/reshape | solution.py:178
  193.4 16.0 %shard_map.119 = bf16[128,64,128]{2,1,0:T(8,128)(2,1)} custom-call(bf16[128,64,128]{2,1,0:T(8,128)(2,1)} %bitcast.74, bf16[128,384]{1,0:T(8,128)(2,1)} %w_ref.3, f32[4,64,64]{2,1,0:T(8,128)} %select_bitcast_fusion.bias_ref), custom_call_target="tpu_custom_call" | custom-call | tf_op jit(solution)/shard_map/pallas_call | solution.py:112
  209.4 5.4 %copy.23 = bf16[8,1,2,2,4,64,128]{6,5,4,3,2,0,1:T(8,128)(2,1)} copy(bf16[8,1,2,2,4,64,128]{6,4,2,0,5,3,1:T(4,128)(2,1)} %bitcast.75) | data formatting | bytes 4194304 | tf_op jit(solution)/shard_map/transpose | solution.py:185
  214.8 21.4 %all-to-all-done.1 = bf16[16,2,4,64,128]{4,3,2,1,0:T(8,128)(2,1)} async-done(((bf16[16,2,4,64,128]{4,3,2,1,0:T(8,128)(2,1)}), bf16[16,2,4,64,128]{4,3,2,1,0:T(8,128)(2,1)}, u32[]{:S(2)}, u32[]{:S(2)}) %all-to-all-start.1) | async-done | bytes 2097184 | tf_op jit(solution)/shard_map/all_to_all | solution.py:188
  236.2 4.9 %all-to-all-start.3 = ((bf16[16,2,4,64,128]{4,3,2,1,0:T(8,128)(2,1)}), bf16[16,2,4,64,128]{4,3,2,1,0:T(8,128)(2,1)}, u32[]{:S(2)}, u32[]{:S(2)}) async-start(bf16[16,2,4,64,128]{4,3,2,1,0:T(8,128)(2,1)} %bitcast.73), calls=%async_computation.3 | async-start | bytes 4194304 | tf_op jit(solution)/shard_map/all_to_all | solution.py:188
  241.1 3.2 %copy.20 = bf16[8,2,4,2,64,128]{5,4,3,2,1,0:T(8,128)(2,1)} copy(bf16[8,2,4,2,64,128]{5,4,2,1,3,0:T(8,128)(2,1)} %bitcast.23) | data formatting | bytes 4194304 | tf_op jit(solution)/shard_map/transpose | solution.py:191
  244.3 44.3 %all-to-all-done.3 = bf16[16,2,4,64,128]{4,3,2,1,0:T(8,128)(2,1)} async-done(((bf16[16,2,4,64,128]{4,3,2,1,0:T(8,128)(2,1)}), bf16[16,2,4,64,128]{4,3,2,1,0:T(8,128)(2,1)}, u32[]{:S(2)}, u32[]{:S(2)}) %all-to-all-start.3) | async-done | bytes 2097184 | tf_op jit(solution)/shard_map/all_to_all | solution.py:188
  290.5 2.3 fusion.36
  293.6 2.4 pad_maximum_fusion.6
  (48 shorter events, 9.3 us)
Async XLA Ops:
  0.0 0.8 copy-start
  9.4 32.5 %copy-start.2 = (bf16[32,512,256]{2,1,0:T(8,128)(2,1)}, bf16[32,512,256]{2,1,0:T(8,128)(2,1)S(1)}, u32[]{:S(2)}) copy-start(bf16[32,512,256]{2,1,0:T(8,128)(2,1)S(1)} %fusion.7) | copy-start | bytes 25165828
  9.4 20.1 %copy-start.6 = (f32[3,3,256]{2,1,0:T(4,128)S(1)}, f32[3,3,256]{2,1,0:T(4,128)}, u32[]{:S(2)}) copy-start(f32[3,3,256]{2,1,0:T(4,128)} %param.15) | copy-start | bytes 27652
  9.5 14.7 %collective-permute-start = (bf16[1,512,256]{2,1,0:T(8,128)(2,1)S(1)}, bf16[1,512,256]{2,1,0:T(8,128)(2,1)S(1)}, u32[]{:S(2)}, u32[]{:S(2)}) collective-permute-start(bf16[1,512,256]{2,1,0:T(8,128)(2,1)S(1)} %get-tuple-element.13), channel_id=1, source_target_pairs={{0,2},{2,4},{4,6},{6,8},{8,10},{10,12},{12,14},{1,3},{3,5},{5,7},{... | collective-permute-start | bytes 786440 | tf_op jit(solution)/shard_map/ppermute | solution.py:18
  12.6 11.5 %collective-permute-start.1 = (bf16[1,512,256]{2,1,0:T(8,128)(2,1)S(1)}, bf16[1,512,256]{2,1,0:T(8,128)(2,1)S(1)}, u32[]{:S(2)}, u32[]{:S(2)}) collective-permute-start(bf16[1,512,256]{2,1,0:T(8,128)(2,1)S(1)} %get-tuple-element.14), channel_id=1, source_target_pairs={{2,0},{4,2},{6,4},{8,6},{10,8},{12,10},{14,12},{3,1},{5,3},{7,5},{... | collective-permute-start | bytes 786440 | tf_op jit(solution)/shard_map/ppermute | solution.py:19
  24.2 5.4 %collective-permute-start.2 = (bf16[34,1,256]{2,1,0:T(2,128)(2,1)S(1)}, bf16[34,1,256]{2,1,0:T(2,128)(2,1)S(1)}, u32[]{:S(2)}, u32[]{:S(2)}) collective-permute-start(bf16[34,1,256]{2,1,0:T(2,128)(2,1)S(1)} %get-tuple-element.11), channel_id=1, source_target_pairs={{0,1},{2,3},{4,5},{6,7},{8,9},{10,11},{12,13},{14,15},{16,17},{18,... | collective-permute-start | bytes 52232 | tf_op jit(solution)/shard_map/ppermute | solution.py:18
  25.5 4.3 %collective-permute-start.3 = (bf16[34,1,256]{2,1,0:T(2,128)(2,1)S(1)}, bf16[34,1,256]{2,1,0:T(2,128)(2,1)S(1)}, u32[]{:S(2)}, u32[]{:S(2)}) collective-permute-start(bf16[34,1,256]{2,1,0:T(2,128)(2,1)S(1)} %get-tuple-element.12), channel_id=1, source_target_pairs={{1,0},{3,2},{5,4},{7,6},{9,8},{11,10},{13,12},{15,14},{17,16},{19,... | collective-permute-start | bytes 52232 | tf_op jit(solution)/shard_map/ppermute | solution.py:19
  29.5 12.3 %copy-start.10 = (bf16[256,128]{1,0:T(8,128)(2,1)S(1)}, bf16[256,128]{1,0:T(8,128)(2,1)}, u32[]{:S(2)}) copy-start(bf16[256,128]{1,0:T(8,128)(2,1)} %param.17) | copy-start | bytes 196612
  29.5 12.3 %copy-start.11 = (f32[256]{0:T(256)S(1)}, f32[256]{0:T(256)}, u32[]{:S(2)}) copy-start(f32[256]{0:T(256)} %param.16) | copy-start | bytes 3076
  29.5 12.3 %copy-start.12 = (f32[128]{0:T(128)S(1)}, f32[128]{0:T(128)}, u32[]{:S(2)}) copy-start(f32[128]{0:T(128)} %param.18) | copy-start | bytes 1540
  41.9 23.5 %copy-start.8 = (f32[128]{0:T(128)S(1)}, f32[128]{0:T(128)}, u32[]{:S(2)}) copy-start(f32[128]{0:T(128)} %param.20) | copy-start | bytes 1540
  41.9 23.5 %copy-start.9 = (f32[128]{0:T(128)S(1)}, f32[128]{0:T(128)}, u32[]{:S(2)}) copy-start(f32[128]{0:T(128)} %param.19) | copy-start | bytes 1540
  76.5 54.3 %all-to-all-start = ((bf16[16,2,4,64,128]{4,3,2,1,0:T(8,128)(2,1)}), bf16[16,2,4,64,128]{4,3,2,1,0:T(8,128)(2,1)}, u32[]{:S(2)}, u32[]{:S(2)}) async-start(bf16[16,2,4,64,128]{4,3,2,1,0:T(8,128)(2,1)} %bitcast.71), calls=%async_computation | async-start | bytes 4194304 | tf_op jit(solution)/shard_map/all_to_all | solution.py:176
  107.6 2.5 copy-start.3
  107.6 28.7 %copy-start.7 = (f32[4,225]{1,0:T(4,128)S(1)}, f32[4,225]{1,0:T(4,128)}, u32[]{:S(2)}) copy-start(f32[4,225]{1,0:T(4,128)} %param.22) | copy-start | bytes 10804
  130.8 52.6 %all-to-all-start.2 = ((bf16[16,2,4,64,128]{4,3,2,1,0:T(8,128)(2,1)}), bf16[16,2,4,64,128]{4,3,2,1,0:T(8,128)(2,1)}, u32[]{:S(2)}, u32[]{:S(2)}) async-start(bf16[16,2,4,64,128]{4,3,2,1,0:T(8,128)(2,1)} %bitcast.70), calls=%async_computation.2 | async-start | bytes 4194304 | tf_op jit(solution)/shard_map/all_to_all | solution.py:176
  183.5 52.7 %all-to-all-start.1 = ((bf16[16,2,4,64,128]{4,3,2,1,0:T(8,128)(2,1)}), bf16[16,2,4,64,128]{4,3,2,1,0:T(8,128)(2,1)}, u32[]{:S(2)}, u32[]{:S(2)}) async-start(bf16[16,2,4,64,128]{4,3,2,1,0:T(8,128)(2,1)} %bitcast.72), calls=%async_computation.1 | async-start | bytes 4194304 | tf_op jit(solution)/shard_map/all_to_all | solution.py:188
  209.4 81.1 %copy-start.5 = (bf16[128,128]{1,0:T(8,128)(2,1)S(1)}, bf16[128,128]{1,0:T(8,128)(2,1)}, u32[]{:S(2)}) copy-start(bf16[128,128]{1,0:T(8,128)(2,1)} %param.23) | copy-start | bytes 98308
  236.2 52.4 %all-to-all-start.3 = ((bf16[16,2,4,64,128]{4,3,2,1,0:T(8,128)(2,1)}), bf16[16,2,4,64,128]{4,3,2,1,0:T(8,128)(2,1)}, u32[]{:S(2)}, u32[]{:S(2)}) async-start(bf16[16,2,4,64,128]{4,3,2,1,0:T(8,128)(2,1)} %bitcast.73), calls=%async_computation.3 | async-start | bytes 4194304 | tf_op jit(solution)/shard_map/all_to_all | solution.py:188
  288.6 4.3 %copy-start.4 = (bf16[16,512,128]{2,1,0:T(8,128)(2,1)S(1)}, bf16[16,512,128]{2,1,0:T(8,128)(2,1)}, u32[]{:S(2)}) copy-start(bf16[16,512,128]{2,1,0:T(8,128)(2,1)} %copy-done.3) | copy-start | bytes 6291460
  290.5 5.4 %copy-start.1 = (bf16[128,256]{1,0:T(8,128)(2,1)S(1)}, bf16[128,256]{1,0:T(8,128)(2,1)}, u32[]{:S(2)}) copy-start(bf16[128,256]{1,0:T(8,128)(2,1)} %param.13) | copy-start | bytes 196612
